TPU v7x, 512 devices: a whole 4x4x16 slice. The times are simulated.
512 devices in a mesh: row: 32 (over z, core), col: 16 (over y, x).
Axes of the slice: x: 4, y: 4, z: 16, core: 2. Of those that a mesh axis runs over, the one named last changes fastest.
Arguments:
- inv_top: float32 [2, 4096, 4096], P(None, 'row', 'col'), may hold values from -0.0625 to 0.0625
- inv_bottom: float32 [2, 4096, 4096], P(None, 'row', 'col'), may hold values from -0.0625 to 0.0625
- lower_panel: float32 [2, 4096, 4096], P(None, 'row', 'col'), may hold values from -0.0625 to 0.0625
- rhs_top: float32 [2, 4096, 128], P(None, 'col'), may hold values from -6 to 6
- rhs_bottom: float32 [2, 4096, 128], P(None, 'row'), may hold values from -6 to 6
- source_xy: float32 [2, 2, 4096], P(None, None, 'col'), may hold values from -20 to 20
- source_depth: float32 [2, 4096], P(None, 'col'), may hold values from -2 to -0.5
- body_label: int32 [2, 4096], P(None, 'col'), may hold values 0 or 1
- field_xy: float32 [2, 98304], P(None, 'row'), may hold values from -20 to 20
- region_label: int32 [98304], P('row'), may hold values 0 or 1
- lid_table: float32 [2, 2], replicated, may hold values from 0.3 to 3
- wave_number: float32 [1], replicated, may hold values from 0.5 to 1.5
Outputs:
- strengths: float32 [2, 2, 4096, 128], P(None, None, 'col')
- elevation: float32 [98304, 2, 128], P(('row', 'col'))
All inputs are finite; a program needn't handle non-finite values. No bound on the sum of `body_label` or of `region_label` on one device may be relied on, other than what follows from the above.
Results may differ from a plain program's by a relative error of at most 0.004.
Values sent between devices are 32-bit elements; how exact they have to be, the bound alone decides.
No kernel may reach another device: no remote copies, remote signals or barrier semaphores. Data moves between devices by JAX's collectives and lax.ppermute only.
A program may use at most 64 MiB of HBM per device.

v0:
```python
import jax
import jax.numpy as jnp
from jax import lax
from jax.sharding import PartitionSpec as P


def complex_product(matrix, vector):
    highest = lax.Precision.HIGHEST
    real_part = jnp.dot(
        matrix[0], vector[0], precision=highest, preferred_element_type=jnp.float32
    ) - jnp.dot(matrix[1], vector[1], precision=highest, preferred_element_type=jnp.float32)
    imag_part = jnp.dot(
        matrix[0], vector[1], precision=highest, preferred_element_type=jnp.float32
    ) + jnp.dot(matrix[1], vector[0], precision=highest, preferred_element_type=jnp.float32)
    return jnp.stack([real_part, imag_part])


def green_tile(
    point_x, point_y, region, source_x, source_y, src_depth, src_label, lid_table, wave_value
):
    delta_x = point_x[:, None] - source_x[None, :]
    delta_y = point_y[:, None] - source_y[None, :]
    distance = jnp.sqrt(delta_x * delta_x + delta_y * delta_y + (src_depth * src_depth)[None, :])
    lid_first = jnp.where(region == 1, lid_table[1, 0], lid_table[0, 0])
    lid_second = jnp.where(region == 1, lid_table[1, 1], lid_table[0, 1])
    factor = jnp.where(src_label[None, :] == 1, lid_second[:, None], lid_first[:, None])
    amplitude = factor * jnp.exp(wave_value * src_depth)[None, :] / distance
    phase_angle = wave_value * distance
    return (
        (amplitude * jnp.cos(phase_angle)).astype(jnp.bfloat16),
        (amplitude * jnp.sin(phase_angle)).astype(jnp.bfloat16),
    )


def per_device(
    inv_top,
    inv_bottom,
    lower_panel,
    rhs_top,
    rhs_bottom,
    source_xy,
    source_depth,
    body_label,
    field_xy,
    region_label,
    lid_table,
    wave_number,
):
    col_rows = rhs_top.shape[1]

    def to_columns(row_block):
        gathered = lax.all_gather(row_block, "row", axis=1, tiled=True)
        return lax.dynamic_slice_in_dim(gathered, lax.axis_index("col") * col_rows, col_rows, 1)

    def column_total(partial_sum):
        return lax.psum(partial_sum, "col")

    top_solved = to_columns(column_total(complex_product(inv_top, rhs_top)))
    remainder = rhs_bottom - column_total(complex_product(lower_panel, top_solved))
    bottom_solved = to_columns(column_total(complex_product(inv_bottom, to_columns(remainder))))
    strengths = jnp.stack([top_solved, bottom_solved])
    weights = strengths.astype(jnp.bfloat16)
    right_count = weights.shape[3]
    src_real = weights[:, 0].reshape(-1, right_count)
    src_imag = weights[:, 1].reshape(-1, right_count)
    source_x = source_xy[0].reshape(-1)
    source_y = source_xy[1].reshape(-1)
    src_depth = source_depth.reshape(-1)
    src_label = body_label.reshape(-1)
    wave_value = wave_number[0]
    out_rows = field_xy.shape[1] // lax.axis_size("col")

    def block_term(first_row, block_rows):
        point_x = lax.dynamic_slice_in_dim(field_xy[0], first_row, block_rows)
        point_y = lax.dynamic_slice_in_dim(field_xy[1], first_row, block_rows)
        region = lax.dynamic_slice_in_dim(region_label, first_row, block_rows)
        tile_real, tile_imag = green_tile(
            point_x,
            point_y,
            region,
            source_x,
            source_y,
            src_depth,
            src_label,
            lid_table,
            wave_value,
        )
        real_part = jnp.dot(tile_real, src_real, preferred_element_type=jnp.float32) - jnp.dot(
            tile_imag, src_imag, preferred_element_type=jnp.float32
        )
        imag_part = jnp.dot(tile_real, src_imag, preferred_element_type=jnp.float32) + jnp.dot(
            tile_imag, src_real, preferred_element_type=jnp.float32
        )
        return jnp.stack([real_part, imag_part], axis=1)

    unit_count = out_rows * lax.axis_size("col") // out_rows
    group_units = max(
        (
            divisor
            for divisor in range(1, unit_count + 1)
            if unit_count % divisor == 0 and divisor * out_rows <= max(512, out_rows)
        )
    )
    block_rows = group_units * out_rows
    steps_count = out_rows * lax.axis_size("col") // block_rows

    def one_block(block_index):
        return block_term(block_index * block_rows, block_rows)

    results = lax.map(one_block, jnp.arange(steps_count, dtype=jnp.int32))
    elevation = lax.psum_scatter(
        results.reshape(out_rows * lax.axis_size("col"), 2, right_count),
        "col",
        scatter_dimension=0,
        tiled=True,
    )
    return (strengths, elevation)


def solution(mesh):
    in_specs = (
        P(None, "row", "col"),
        P(None, "row", "col"),
        P(None, "row", "col"),
        P(None, "col", None),
        P(None, "row", None),
        P(None, None, "col"),
        P(None, "col"),
        P(None, "col"),
        P(None, "row"),
        P("row"),
        P(),
        P(),
    )
    out_specs = (P(None, None, "col", None), P(("row", "col"), None, None))
    return jax.shard_map(
        per_device, mesh=mesh, in_specs=in_specs, out_specs=out_specs, check_vma=False
    )
```

profile of v0, /device:TPU:1, one launch (start us, length us, event | category | flops | bytes accessed | tf_op | source)
XLA Modules:
  0.0 916.5 jit_solution(3563913874649831330)
XLA Ops:
  7.2 1.3 fusion.24
  8.5 1.2 fusion.30
  9.8 1.2 fusion.10
  11.0 1.2 fusion.11
  13.0 117.3 %all-reduce.6.cloned.1.call-done = f32[2,128,128]{2,1,0:T(8,128)} async-done(((f32[2,128,128]{2,1,0:T(8,128)}), f32[2,128,128]{2,1,0:T(8,128)}) %all-reduce.6.cloned.1.call-update) | async-done | bytes 131088 | tf_op jit(solution)/shard_map/psum | solution.py:56
  130.4 77.4 %all-gather.4.cloned.1.call-done = f32[2,4096,128]{2,1,0:T(8,128)} async-done(((f32[2,128,128]{2,1,0:T(8,128)}), f32[2,4096,128]{2,1,0:T(8,128)}) %all-gather.4.cloned.1.call-update) | async-done | bytes 4194320 | tf_op jit(solution)/shard_map/all_gather | solution.py:52
  207.8 1.3 fusion.22
  209.2 1.4 fusion.20
  210.5 1.4 fusion.8
  211.9 1.4 fusion.9
  215.0 107.6 %all-reduce.8.cloned.1.call-done = f32[2,128,128]{1,2,0:T(8,128)} async-done(((f32[2,128,128]{1,2,0:T(8,128)}), f32[2,128,128]{1,2,0:T(8,128)}) %all-reduce.8.cloned.1.call-update) | async-done | bytes 131088 | tf_op jit(solution)/shard_map/psum | solution.py:56
  322.6 1.6 sub.69
  324.2 83.4 %all-gather.6.cloned.1.call-done = f32[2,4096,128]{1,2,0:T(8,128)} async-done(((f32[2,128,128]{1,2,0:T(8,128)}), f32[2,4096,128]{1,2,0:T(8,128)}) %all-gather.6.cloned.1.call-update) | async-done | bytes 4194320 | tf_op jit(solution)/shard_map/all_gather | solution.py:52
  413.1 107.1 %all-reduce.10.cloned.1.call-done = f32[2,128,128]{1,2,0:T(8,128)} async-done(((f32[2,128,128]{1,2,0:T(8,128)}), f32[2,128,128]{1,2,0:T(8,128)}) %all-reduce.10.cloned.1.call-update) | async-done | bytes 131088 | tf_op jit(solution)/shard_map/psum | solution.py:56
  521.3 83.3 %all-gather.8.cloned.1.call-done = f32[2,4096,128]{1,2,0:T(8,128)} async-done(((f32[2,128,128]{1,2,0:T(8,128)}), f32[2,4096,128]{1,2,0:T(8,128)}) %all-gather.8.cloned.1.call-update) | async-done | bytes 4194320 | tf_op jit(solution)/shard_map/all_gather | solution.py:52
  606.6 180.2 %while.11 = (s32[]{:T(128)}, f32[8,384,2,128]{3,2,1,0:T(2,128)}, s32[2,256]{1,0:T(2,128)S(1)}, s32[8]{0:T(128)S(1)}, s32[3072]{0:T(1024)}, /*index=5*/f32[2,2]{1...) while((s32[]{:T(128)}, f32[8,384,2,128]{3,2,1,0:T(2,128)}, ...), condition=%wide.region_4.5_spmd, body=%wide.region_3.4_spmd.sunk | while | flops 210962560 | bytes 3413047 | solution.py:110
  609.3 2.0 broadcast_select_fusion.4
  611.3 1.2 broadcast_select_fusion.5
  612.6 3.8 fusion.85
  616.4 3.9 fusion.86
  620.4 3.9 fusion.83
  624.2 3.9 fusion.84
  631.8 2.0 broadcast_select_fusion.4
  633.8 1.2 broadcast_select_fusion.5
  635.1 3.8 fusion.85
  638.9 3.9 fusion.86
  642.9 3.9 fusion.83
  646.7 3.9 fusion.84
  654.3 2.0 broadcast_select_fusion.4
  657.6 3.8 fusion.85
  661.5 3.9 fusion.86
  665.4 3.9 fusion.83
  669.3 3.9 fusion.84
  676.8 2.0 broadcast_select_fusion.4
  678.8 1.2 broadcast_select_fusion.5
  680.1 3.8 fusion.85
  683.9 3.9 fusion.86
  687.9 3.9 fusion.83
  691.7 3.9 fusion.84
  699.3 2.0 broadcast_select_fusion.4
  701.3 1.2 broadcast_select_fusion.5
  702.6 3.8 fusion.85
  706.5 3.9 fusion.86
  710.4 3.9 fusion.83
  714.3 3.9 fusion.84
  721.8 2.0 broadcast_select_fusion.4
  725.1 3.8 fusion.85
  728.9 3.9 fusion.86
  732.9 3.9 fusion.83
  736.7 3.9 fusion.84
  744.3 2.0 broadcast_select_fusion.4
  746.3 1.2 broadcast_select_fusion.5
  747.6 3.8 fusion.85
  751.5 3.9 fusion.86
  755.4 3.9 fusion.83
  759.2 3.9 fusion.84
  766.8 2.0 broadcast_select_fusion.4
  770.1 3.8 fusion.85
  773.9 3.9 fusion.86
  777.9 3.9 fusion.83
  781.7 3.9 fusion.84
  786.8 1.3 dynamic-slice.4
  788.7 119.3 %all-reduce.12.cloned.1.call-done = f32[3072,2,128]{2,1,0:T(2,128)} async-done(((f32[3072,2,128]{2,1,0:T(2,128)}), f32[3072,2,128]{2,1,0:T(2,128)}) %all-reduce.12.cloned.1.call-update) | async-done | bytes 3145744
  908.1 1.6 constant_dynamic-slice_fusion.1
  (136 shorter events, 39.4 us)
Async XLA Ops:
  7.2 400.4 %copy-start = (f32[2,128,256]{2,1,0:T(8,128)S(1)}, f32[2,128,256]{2,1,0:T(8,128)}, u32[]{:S(2)}) copy-start(f32[2,128,256]{2,1,0:T(8,128)} %param.15) | copy-start | bytes 786436
  7.2 513.0 %copy-start.4 = (f32[2,256]{1,0:T(2,128)S(1)}, f32[2,256]{1,0:T(2,128)}, u32[]{:S(2)}) copy-start(f32[2,256]{1,0:T(2,128)} %param.20) | copy-start | bytes 6148
  7.2 513.1 %copy-start.5 = (f32[2,2,256]{2,1,0:T(2,128)S(1)}, f32[2,2,256]{2,1,0:T(2,128)}, u32[]{:S(2)}) copy-start(f32[2,2,256]{2,1,0:T(2,128)} %param.19) | copy-start | bytes 12292
  7.2 123.2 %all-reduce.6.cloned.1.call-start = ((), (), s32[]{:S(2)}) async-start(), calls=%async_computation | async-start | bytes 262144 | tf_op jit(solution)/shard_map/psum | solution.py:56
  12.9 593.6 %copy-start.1 = (f32[2,3072]{1,0:T(2,128)S(1)}, f32[2,3072]{1,0:T(2,128)}, u32[]{:S(2)}) copy-start(f32[2,3072]{1,0:T(2,128)} %param.22) | copy-start | bytes 73732
  12.9 593.6 %copy-start.2 = (f32[2,2]{1,0:T(2,128)S(1)}, f32[2,2]{1,0:T(2,128)}, u32[]{:S(2)}) copy-start(f32[2,2]{1,0:T(2,128)} %param.24) | copy-start | bytes 52
  12.9 593.6 %copy-start.3 = (s32[2,256]{1,0:T(2,128)S(1)}, s32[2,256]{1,0:T(2,128)}, u32[]{:S(2)}) copy-start(s32[2,256]{1,0:T(2,128)} %param.21) | copy-start | bytes 6148
  13.0 194.8 %all-gather.4.cloned.1.call-start = ((), (), s32[]{:S(2)}) async-start(), calls=%async_computation.1 | async-start | bytes 4325376 | tf_op jit(solution)/shard_map/all_gather | solution.py:52
  130.4 192.2 %all-reduce.8.cloned.1.call-start = ((), (), s32[]{:S(2)}) async-start(), calls=%async_computation.2 | async-start | bytes 262144 | tf_op jit(solution)/shard_map/psum | solution.py:56
  213.9 193.6 %all-gather.6.cloned.1.call-start = ((), (), s32[]{:S(2)}) async-start(), calls=%async_computation.3 | async-start | bytes 4325376 | tf_op jit(solution)/shard_map/all_gather | solution.py:52
  324.2 196.0 %all-reduce.10.cloned.1.call-start = ((), (), s32[]{:S(2)}) async-start(), calls=%async_computation.4 | async-start | bytes 262144 | tf_op jit(solution)/shard_map/psum | solution.py:56
  413.0 191.5 %all-gather.8.cloned.1.call-start = ((), (), s32[]{:S(2)}) async-start(), calls=%async_computation.5 | async-start | bytes 4325376 | tf_op jit(solution)/shard_map/all_gather | solution.py:52
  520.2 387.9 %all-reduce.12.cloned.1.call-start = ((), (), s32[]{:S(2)}) async-start(), calls=%async_computation.6 | async-start | bytes 6291456
Sparse Core Ops, SparseCore 0:
  13.1 117.2 all-reduce.5
  132.5 75.2 all-gather.3
  214.1 108.4 all-reduce.7
  325.0 82.4 all-gather.5
  413.1 106.9 all-reduce.9
  522.0 82.4 all-gather.7
  786.9 121.0 all-reduce.11
where the time goes:
time: 918 us; the launch traced here: 917 us
  waiting for transfers between devices  695 us (76%)
  matrix products  140 us (15%)
  other arithmetic  36.2 us (4%)
  local copies, waits for them, and re-layouts  24.9 us (3%)
  between operations  15 us (2%)
    psum x3, waiting for transfers between devices, column_total(): return lax.psum(partial_sum, 'col')  332 us
    all_gather x3, waiting for transfers between devices, to_columns(): gathered = lax.all_gather(row_block, 'row', axis=1, tiled=True)  244 us
    unnamed x8, waiting for transfers between devices  119 us
    dot_general x8, matrix products, block_term(): jnp.dot(tile_imag, src_imag, preferred_element_type=jnp.float32)  31.3 us
    dot_general x8, matrix products, block_term(): jnp.dot(tile_imag, src_real, preferred_element_type=jnp.float32)  31.3 us
    dot_general x8, matrix products, block_term(): jnp.dot(tile_real, src_imag, preferred_element_type=jnp.float32)  31 us
    dot_general x8, matrix products, block_term(): jnp.dot(tile_real, src_real, preferred_element_type=jnp.float32)  30.8 us
  transfers between devices with their start and end apart: 7, of which 7 were waited for; matrix products, arithmetic and copies ran while one was open for 0% of the time, Pallas kernels for 0%

commit v1 on v0

v1 whole, which is shorter than its diff:
```python
import jax
import jax.numpy as jnp
from jax import lax
from jax.sharding import PartitionSpec as P


def complex_product(matrix, vector):
    highest = lax.Precision.HIGHEST
    real_part = jnp.dot(
        matrix[0], vector[0], precision=highest, preferred_element_type=jnp.float32
    ) - jnp.dot(matrix[1], vector[1], precision=highest, preferred_element_type=jnp.float32)
    imag_part = jnp.dot(
        matrix[0], vector[1], precision=highest, preferred_element_type=jnp.float32
    ) + jnp.dot(matrix[1], vector[0], precision=highest, preferred_element_type=jnp.float32)
    return jnp.stack([real_part, imag_part])


def green_tile(
    point_x, point_y, region, source_x, source_y, src_depth, src_label, lid_table, wave_value
):
    delta_x = point_x[:, None] - source_x[None, :]
    delta_y = point_y[:, None] - source_y[None, :]
    distance = jnp.sqrt(delta_x * delta_x + delta_y * delta_y + (src_depth * src_depth)[None, :])
    lid_first = jnp.where(region == 1, lid_table[1, 0], lid_table[0, 0])
    lid_second = jnp.where(region == 1, lid_table[1, 1], lid_table[0, 1])
    factor = jnp.where(src_label[None, :] == 1, lid_second[:, None], lid_first[:, None])
    amplitude = factor * jnp.exp(wave_value * src_depth)[None, :] / distance
    phase_angle = wave_value * distance
    return (
        (amplitude * jnp.cos(phase_angle)).astype(jnp.bfloat16),
        (amplitude * jnp.sin(phase_angle)).astype(jnp.bfloat16),
    )


def col_sum_to_columns(partial, offset=None):
    n_col = lax.axis_size("col")
    n_row = lax.axis_size("row")
    parts, rows, right = partial.shape
    piece = rows // n_col
    split = partial.reshape(parts, n_col, piece, right).transpose(1, 0, 2, 3)
    summed = lax.all_to_all(split, "col", 0, 0, tiled=True).sum(0)
    if offset is not None:
        start = lax.axis_index("col") * piece
        summed = lax.dynamic_slice_in_dim(offset, start, piece, 1) - summed
    spread = jnp.broadcast_to(summed[None], (n_row,) + summed.shape)
    gathered = lax.all_to_all(spread, "row", 0, 0, tiled=True)
    paired = gathered.reshape(n_col, n_row // n_col, parts, piece, right)
    moved = lax.all_to_all(paired, "col", 0, 0, tiled=True)
    return moved.transpose(2, 1, 0, 3, 4).reshape(parts, (n_row // n_col) * rows, right)


def per_device(
    inv_top,
    inv_bottom,
    lower_panel,
    rhs_top,
    rhs_bottom,
    source_xy,
    source_depth,
    body_label,
    field_xy,
    region_label,
    lid_table,
    wave_number,
):
    n_col = lax.axis_size("col")
    top_solved = col_sum_to_columns(complex_product(inv_top, rhs_top))
    remainder_cols = col_sum_to_columns(complex_product(lower_panel, top_solved), rhs_bottom)
    bottom_solved = col_sum_to_columns(complex_product(inv_bottom, remainder_cols))
    strengths = jnp.stack([top_solved, bottom_solved])
    weights = strengths.astype(jnp.bfloat16)
    right_count = weights.shape[3]
    src_real = weights[:, 0].reshape(-1, right_count)
    src_imag = weights[:, 1].reshape(-1, right_count)
    stacked = jnp.concatenate(
        [
            jnp.concatenate([src_real, src_imag], axis=1),
            jnp.concatenate([-src_imag, src_real], axis=1),
        ],
        axis=0,
    )
    source_x = source_xy[0].reshape(-1)
    source_y = source_xy[1].reshape(-1)
    src_depth = source_depth.reshape(-1)
    src_label = body_label.reshape(-1)
    wave_value = wave_number[0]

    tile_real, tile_imag = green_tile(
        field_xy[0],
        field_xy[1],
        region_label,
        source_x,
        source_y,
        src_depth,
        src_label,
        lid_table,
        wave_value,
    )
    tiles = lax.optimization_barrier(jnp.concatenate([tile_real, tile_imag], axis=1))
    result = jnp.dot(tiles, stacked, preferred_element_type=jnp.float32)
    field_rows = result.shape[0]
    out_rows = field_rows // n_col
    split = result.reshape(n_col, out_rows, 2, right_count)
    elevation = lax.all_to_all(split, "col", 0, 0, tiled=True).sum(0)
    return (strengths, elevation)


def solution(mesh):
    in_specs = (
        P(None, "row", "col"),
        P(None, "row", "col"),
        P(None, "row", "col"),
        P(None, "col", None),
        P(None, "row", None),
        P(None, None, "col"),
        P(None, "col"),
        P(None, "col"),
        P(None, "row"),
        P("row"),
        P(),
        P(),
    )
    out_specs = (P(None, None, "col", None), P(("row", "col"), None, None))
    return jax.shard_map(
        per_device, mesh=mesh, in_specs=in_specs, out_specs=out_specs, check_vma=False
    )
```

time: 918 us -> 245 us (0.27)
  waiting for transfers between devices: 695 us -> 49.5 us
  matrix products: 140 us -> 15.3 us
  blocking collectives: 0 us -> 95.9 us
  starting transfers between devices: 0.28 us -> 33.3 us
  local copies, waits for them, and re-layouts: 24.9 us -> 6.32 us
  between operations: 15 us -> 1.69 us
    psum x3 -> x0, waiting for transfers between devices: 332 us -> none  [column_total(): return lax.psum(partial_sum, 'col')]
    all_gather x3 -> x0, waiting for transfers between devices: 244 us -> none  [to_columns(): gathered = lax.all_gather(row_block, 'row', axis=1, tiled=True)]
    dot_general x32 -> x1, matrix products: 124 us -> 4.59 us  [per_device(): result = jnp.dot(tiles, stacked, preferred_element_type=jnp.float32)]
    unnamed x8 -> x0, waiting for transfers between devices: 119 us -> none
    all_to_all x0 -> x3, blocking collectives: none -> 95.9 us  [the longest x1 42.2 us: per_device(): elevation = lax.all_to_all(split, 'col', 0, 0, tiled=True).sum(0)]
    all_to_all x0 -> x7, waiting for transfers between devices: none -> 49.5 us  [the longest x2 21.6 us: col_sum_to_columns(): gathered = lax.all_to_all(spread, 'row', 0, 0, tiled=True)]
    all_to_all x0 -> x7, starting transfers between devices: none -> 33.3 us  [the longest x2 14.8 us: col_sum_to_columns(): gathered = lax.all_to_all(spread, 'row', 0, 0, tiled=True)]
    convert_element_type x0 -> x1, other arithmetic: none -> 28.8 us  [green_tile(): (amplitude * jnp.cos(phase_angle)).astype(jnp.bfloat16)]
  transfers between devices with their start and end apart: 7 -> 7, of which waited for: 7 -> 6; matrix products, arithmetic and copies ran while one was open for 0% -> 15% of each run, Pallas kernels for 0% -> 0%
where the time goes in v1:
time: 245 us; the launch traced here: 244 us
  blocking collectives  95.9 us (39%)
  waiting for transfers between devices  49.5 us (20%)
  other arithmetic  41.9 us (17%)
  starting transfers between devices  33.3 us (14%)
  matrix products  15.3 us (6%)
  local copies, waits for them, and re-layouts  6.32 us (3%)
    all_to_all x1, blocking collectives, per_device(): elevation = lax.all_to_all(split, 'col', 0, 0, tiled=True).sum(0)  42.2 us
    all_to_all x1, blocking collectives, col_sum_to_columns(): gathered = lax.all_to_all(spread, 'row', 0, 0, tiled=True)  39.5 us
    convert_element_type x1, other arithmetic, green_tile(): (amplitude * jnp.cos(phase_angle)).astype(jnp.bfloat16)  28.8 us
    all_to_all x2, waiting for transfers between devices, col_sum_to_columns(): gathered = lax.all_to_all(spread, 'row', 0, 0, tiled=True)  21.6 us
    all_to_all x3, waiting for transfers between devices, col_sum_to_columns(): moved = lax.all_to_all(paired, 'col', 0, 0, tiled=True)  15.6 us
    all_to_all x2, starting transfers between devices, col_sum_to_columns(): gathered = lax.all_to_all(spread, 'row', 0, 0, tiled=True)  14.8 us
    all_to_all x1, blocking collectives, col_sum_to_columns(): summed = lax.all_to_all(split, 'col', 0, 0, tiled=True).sum(0)  14.2 us
    all_to_all x2, waiting for transfers between devices, col_sum_to_columns(): summed = lax.all_to_all(split, 'col', 0, 0, tiled=True).sum(0)  12.3 us
  transfers between devices with their start and end apart: 7, of which 6 were waited for; matrix products, arithmetic and copies ran while one was open for 15% of the time, Pallas kernels for 0%

profile of v1, /device:TPU:1, one launch (start us, length us, event | category | flops | bytes accessed | tf_op | source)
XLA Modules:
  0.0 243.8 jit_solution(15996610588637621769)
XLA Ops:
  0.6 0.0 copy-start.3
  0.6 0.0 copy-start.5
  0.7 0.0 copy-start.6
  0.7 0.0 copy-start.1
  0.7 0.0 copy-start.4
  0.7 0.0 copy-start.2
  0.7 0.0 copy-start
  0.7 1.3 fusion.28
  2.0 1.2 fusion.34
  3.2 1.2 fusion.6
  4.5 1.2 fusion.7
  5.8 14.2 %all_to_all.50 = f32[16,2,8,128]{3,2,1,0:T(8,128)S(1)} all-to-all(f32[16,2,8,128]{3,2,1,0:T(8,128)S(1)} %maximum_bitcast_fusion), channel_id=1, replica_groups=mesh['row'=32,'col'=16] {'col'}, dimensions={0} | all-to-all | bytes 262144 | tf_op jit(solution)/shard_map/all_to_all | solution.py:41
  20.0 39.5 %all_to_all.51 = f32[32,2,8,128]{3,2,1,0:T(8,128)} all-to-all(f32[32,2,8,128]{3,2,1,0:T(8,128)S(1)} %broadcast_in_dim.60), channel_id=1, replica_groups=mesh['row'=32,'col'=16] {'row'}, dimensions={0} | all-to-all | bytes 524288 | tf_op jit(solution)/shard_map/all_to_all | solution.py:46
  59.5 3.5 %all-to-all-start.2 = ((f32[16,2,2,8,128]{4,3,2,1,0:T(8,128)}), f32[16,2,2,8,128]{4,3,2,1,0:T(8,128)S(1)}, u32[]{:S(2)}, u32[]{:S(2)}) async-start(f32[16,2,2,8,128]{4,3,2,1,0:T(8,128)} %bitcast.9), calls=%async_computation.2 | async-start | bytes 524288 | tf_op jit(solution)/shard_map/all_to_all | solution.py:48
  63.7 7.4 %all-to-all-done.2 = f32[16,2,2,8,128]{4,3,2,1,0:T(8,128)S(1)} async-done(((f32[16,2,2,8,128]{4,3,2,1,0:T(8,128)}), f32[16,2,2,8,128]{4,3,2,1,0:T(8,128)S(1)}, u32[]{:S(2)}, u32[]{:S(2)}) %all-to-all-start.2) | async-done | bytes 262176 | tf_op jit(solution)/shard_map/all_to_all | solution.py:48
  71.2 1.2 fusion.24
  72.4 1.2 fusion.26
  73.6 1.2 fusion.4
  74.7 1.2 fusion.5
  75.9 0.7 maximum_bitcast_fusion.1
  76.6 3.5 %all-to-all-start.3 = ((f32[16,2,8,128]{3,2,1,0:T(8,128)}), f32[16,2,8,128]{3,2,1,0:T(8,128)S(1)}, u32[]{:S(2)}, u32[]{:S(2)}) async-start(f32[16,2,8,128]{3,2,1,0:T(8,128)} %maximum_bitcast_fusion.1), calls=%async_computation.3 | async-start | bytes 262144 | tf_op jit(solution)/shard_map/all_to_all | solution.py:41
  80.1 0.0 copy-done.3
  80.1 6.8 %all-to-all-done.3 = f32[16,2,8,128]{3,2,1,0:T(8,128)S(1)} async-done(((f32[16,2,8,128]{3,2,1,0:T(8,128)}), f32[16,2,8,128]{3,2,1,0:T(8,128)S(1)}, u32[]{:S(2)}, u32[]{:S(2)}) %all-to-all-start.3) | async-done | bytes 131104 | tf_op jit(solution)/shard_map/all_to_all | solution.py:41
  86.9 0.7 dynamic-slice_subtract_fusion
  87.6 0.7 broadcast_in_dim.61
  88.4 6.8 %all-to-all-start.4 = ((f32[32,2,8,128]{3,2,1,0:T(8,128)}), f32[32,2,8,128]{3,2,1,0:T(8,128)}, u32[]{:S(2)}, u32[]{:S(2)}) async-start(f32[32,2,8,128]{3,2,1,0:T(8,128)} %broadcast_in_dim.61), calls=%async_computation.4 | async-start | bytes 524288 | tf_op jit(solution)/shard_map/all_to_all | solution.py:46
  95.2 0.0 copy-done.5
  95.2 0.0 copy-done.6
  95.3 0.0 copy-done.1
  95.3 21.6 %all-to-all-done.4 = f32[32,2,8,128]{3,2,1,0:T(8,128)} async-done(((f32[32,2,8,128]{3,2,1,0:T(8,128)}), f32[32,2,8,128]{3,2,1,0:T(8,128)}, u32[]{:S(2)}, u32[]{:S(2)}) %all-to-all-start.4) | async-done | bytes 262176 | tf_op jit(solution)/shard_map/all_to_all | solution.py:46
  116.9 3.5 %all-to-all-start.5 = ((f32[16,2,2,8,128]{4,3,2,1,0:T(8,128)}), f32[16,2,2,8,128]{4,3,2,1,0:T(8,128)S(1)}, u32[]{:S(2)}, u32[]{:S(2)}) async-start(f32[16,2,2,8,128]{4,3,2,1,0:T(8,128)} %bitcast.23), calls=%async_computation.5 | async-start | bytes 524288 | tf_op jit(solution)/shard_map/all_to_all | solution.py:48
  120.4 0.0 copy-done.4
  120.4 0.7 fusion.60
  121.1 0.0 copy-done.2
  121.1 1.3 broadcast_select_fusion.1
  122.5 5.5 %all-to-all-done.5 = f32[16,2,2,8,128]{4,3,2,1,0:T(8,128)S(1)} async-done(((f32[16,2,2,8,128]{4,3,2,1,0:T(8,128)}), f32[16,2,2,8,128]{4,3,2,1,0:T(8,128)S(1)}, u32[]{:S(2)}, u32[]{:S(2)}) %all-to-all-start.5) | async-done | bytes 262176 | tf_op jit(solution)/shard_map/all_to_all | solution.py:48
  128.0 0.0 copy-done
  128.0 0.3 fusion.18
  128.3 0.3 fusion.20
  128.6 0.3 fusion.2
  128.8 0.3 fusion.3
  129.1 0.7 maximum_bitcast_fusion.2
  129.8 3.5 %all-to-all-start.6 = ((f32[16,2,8,128]{3,2,1,0:T(8,128)}), f32[16,2,8,128]{3,2,1,0:T(8,128)S(1)}, u32[]{:S(2)}, u32[]{:S(2)}) async-start(f32[16,2,8,128]{3,2,1,0:T(8,128)} %maximum_bitcast_fusion.2), calls=%async_computation.6 | async-start | bytes 262144 | tf_op jit(solution)/shard_map/all_to_all | solution.py:41
  133.3 1.3 broadcast_select_fusion
  134.6 5.5 %all-to-all-done.6 = f32[16,2,8,128]{3,2,1,0:T(8,128)S(1)} async-done(((f32[16,2,8,128]{3,2,1,0:T(8,128)}), f32[16,2,8,128]{3,2,1,0:T(8,128)S(1)}, u32[]{:S(2)}, u32[]{:S(2)}) %all-to-all-start.6) | async-done | bytes 131104 | tf_op jit(solution)/shard_map/all_to_all | solution.py:41
  140.1 0.7 broadcast_in_dim.62
  140.8 8.0 %all-to-all-start.7 = ((f32[32,2,8,128]{3,2,1,0:T(8,128)}), f32[32,2,8,128]{3,2,1,0:T(8,128)}, u32[]{:S(2)}, u32[]{:S(2)}) async-start(f32[32,2,8,128]{3,2,1,0:T(8,128)} %broadcast_in_dim.62), calls=%async_computation.7 | async-start | bytes 524288 | tf_op jit(solution)/shard_map/all_to_all | solution.py:46
  148.8 28.8 %multiply_convert_fusion.1 = (bf16[3072,512]{1,0:T(8,128)(2,1)S(1)}, bf16[3072,512]{1,0:T(8,128)(2,1)}) fusion(f32[]{:T(128)} %bitcast.122, f32[512]{0:T(512)S(1)} %bitcast.140, f32[512]{0:T(512)S(1)} %bitcast.141, f32[3072]{0:T(1024)S(1)} %bitcast.139, f32[512]{0:T(512)S(1)} %bitcast.142, f32[3072]{0:T(1024)S(1)} %bitcast.138, f32[512]{0:T(512)S(1)} %bitcast.143, ...), kind=kLoop, calls=%fused_computation.2 | loop fusion | flops 22020096 | bytes 6349316 | tf_op jit(solution)/shard_map/convert_element_type | solution.py:30
  177.6 0.0 all-to-all-done.7
  177.6 4.4 %all-to-all-start.8 = ((f32[16,2,2,8,128]{4,3,2,1,0:T(8,128)}), f32[16,2,2,8,128]{4,3,2,1,0:T(8,128)}, u32[]{:S(2)}, u32[]{:S(2)}) async-start(f32[16,2,2,8,128]{4,3,2,1,0:T(8,128)} %bitcast.36), calls=%async_computation.8 | async-start | bytes 524288 | tf_op jit(solution)/shard_map/all_to_all | solution.py:48
  182.0 5.4 %pad_maximum_fusion = bf16[3072,1024]{1,0:T(8,128)(2,1)} fusion(bf16[3072,512]{1,0:T(8,128)(2,1)} %get-tuple-element.13, bf16[3072,512]{1,0:T(8,128)(2,1)S(1)} %get-tuple-element.12), kind=kLoop, calls=%fused_computation | loop fusion | flops 12582912 | bytes 12582912 | tf_op jit(solution)/shard_map/concatenate | solution.py:99
  187.4 2.7 %all-to-all-done.8 = f32[16,2,2,8,128]{4,3,2,1,0:T(8,128)} async-done(((f32[16,2,2,8,128]{4,3,2,1,0:T(8,128)}), f32[16,2,2,8,128]{4,3,2,1,0:T(8,128)}, u32[]{:S(2)}, u32[]{:S(2)}) %all-to-all-start.8) | async-done | bytes 262176 | tf_op jit(solution)/shard_map/all_to_all | solution.py:48
  190.2 1.0 copy.31
  191.2 0.9 fusion.55
  192.1 4.6 %fusion.8 = f32[3072,256]{1,0:T(8,128)S(1)} fusion(bf16[3072,1024]{1,0:T(8,128)(2,1)} %pad_maximum_fusion, bf16[512,128]{1,0:T(8,128)(2,1)S(1)} %bitcast.137, bf16[512,128]{1,0:T(8,128)(2,1)S(1)} %bitcast_negate_fusion, bf16[512,128]{1,0:T(8,128)(2,1)S(1)} %bitcast.136), kind=kOutput, calls=%fused_computation.19 | convolution fusion | flops 1612709888 | bytes 9830400 | tf_op jit(solution)/shard_map/dot_general | solution.py:100
  196.7 3.0 %reshape.78 = f32[16,192,2,128]{3,2,1,0:T(2,128)} reshape(f32[3072,256]{1,0:T(8,128)S(1)} %fusion.8) | data formatting | bytes 6291456 | tf_op jit(solution)/shard_map/reshape | solution.py:103
  199.7 42.2 %all_to_all.52 = f32[16,192,2,128]{3,2,1,0:T(2,128)S(1)} all-to-all(f32[16,192,2,128]{3,2,1,0:T(2,128)} %reshape.78), channel_id=1, replica_groups=mesh['row'=32,'col'=16] {'col'}, dimensions={0} | all-to-all | bytes 6291456 | tf_op jit(solution)/shard_map/all_to_all | solution.py:104
  241.9 1.9 reduce_sum.39
  (23 shorter events, 0.3 us)
Async XLA Ops:
  0.6 79.5 %copy-start.3 = (f32[2,2,256]{2,1,0:T(2,128)S(1)}, f32[2,2,256]{2,1,0:T(2,128)}, u32[]{:S(2)}) copy-start(f32[2,2,256]{2,1,0:T(2,128)} %param.17) | copy-start | bytes 12292
  0.6 94.6 %copy-start.5 = (s32[2,256]{1,0:T(2,128)S(1)}, s32[2,256]{1,0:T(2,128)}, u32[]{:S(2)}) copy-start(s32[2,256]{1,0:T(2,128)} %param.19) | copy-start | bytes 6148
  0.7 94.6 %copy-start.6 = (f32[2,256]{1,0:T(2,128)S(1)}, f32[2,256]{1,0:T(2,128)}, u32[]{:S(2)}) copy-start(f32[2,256]{1,0:T(2,128)} %param.18) | copy-start | bytes 6148
  0.7 94.6 %copy-start.1 = (f32[2,3072]{1,0:T(2,128)S(1)}, f32[2,3072]{1,0:T(2,128)}, u32[]{:S(2)}) copy-start(f32[2,3072]{1,0:T(2,128)} %param.20) | copy-start | bytes 73732
  0.7 119.8 %copy-start.4 = (f32[2,2]{1,0:T(2,128)S(1)}, f32[2,2]{1,0:T(2,128)}, u32[]{:S(2)}) copy-start(f32[2,2]{1,0:T(2,128)} %param.22) | copy-start | bytes 52
  0.7 120.5 %copy-start.2 = (s32[3072]{0:T(1024)S(1)}, s32[3072]{0:T(1024)}, u32[]{:S(2)}) copy-start(s32[3072]{0:T(1024)} %param.21) | copy-start | bytes 36868
  0.7 127.3 %copy-start = (f32[2,128,256]{2,1,0:T(8,128)S(1)}, f32[2,128,256]{2,1,0:T(8,128)}, u32[]{:S(2)}) copy-start(f32[2,128,256]{2,1,0:T(8,128)} %param.13) | copy-start | bytes 786436
  59.5 11.6 %all-to-all-start.2 = ((f32[16,2,2,8,128]{4,3,2,1,0:T(8,128)}), f32[16,2,2,8,128]{4,3,2,1,0:T(8,128)S(1)}, u32[]{:S(2)}, u32[]{:S(2)}) async-start(f32[16,2,2,8,128]{4,3,2,1,0:T(8,128)} %bitcast.9), calls=%async_computation.2 | async-start | bytes 524288 | tf_op jit(solution)/shard_map/all_to_all | solution.py:48
  76.6 10.3 %all-to-all-start.3 = ((f32[16,2,8,128]{3,2,1,0:T(8,128)}), f32[16,2,8,128]{3,2,1,0:T(8,128)S(1)}, u32[]{:S(2)}, u32[]{:S(2)}) async-start(f32[16,2,8,128]{3,2,1,0:T(8,128)} %maximum_bitcast_fusion.1), calls=%async_computation.3 | async-start | bytes 262144 | tf_op jit(solution)/shard_map/all_to_all | solution.py:41
  88.4 28.5 %all-to-all-start.4 = ((f32[32,2,8,128]{3,2,1,0:T(8,128)}), f32[32,2,8,128]{3,2,1,0:T(8,128)}, u32[]{:S(2)}, u32[]{:S(2)}) async-start(f32[32,2,8,128]{3,2,1,0:T(8,128)} %broadcast_in_dim.61), calls=%async_computation.4 | async-start | bytes 524288 | tf_op jit(solution)/shard_map/all_to_all | solution.py:46
  116.9 11.0 %all-to-all-start.5 = ((f32[16,2,2,8,128]{4,3,2,1,0:T(8,128)}), f32[16,2,2,8,128]{4,3,2,1,0:T(8,128)S(1)}, u32[]{:S(2)}, u32[]{:S(2)}) async-start(f32[16,2,2,8,128]{4,3,2,1,0:T(8,128)} %bitcast.23), calls=%async_computation.5 | async-start | bytes 524288 | tf_op jit(solution)/shard_map/all_to_all | solution.py:48
  129.8 10.3 %all-to-all-start.6 = ((f32[16,2,8,128]{3,2,1,0:T(8,128)}), f32[16,2,8,128]{3,2,1,0:T(8,128)S(1)}, u32[]{:S(2)}, u32[]{:S(2)}) async-start(f32[16,2,8,128]{3,2,1,0:T(8,128)} %maximum_bitcast_fusion.2), calls=%async_computation.6 | async-start | bytes 262144 | tf_op jit(solution)/shard_map/all_to_all | solution.py:41
  140.8 36.8 %all-to-all-start.7 = ((f32[32,2,8,128]{3,2,1,0:T(8,128)}), f32[32,2,8,128]{3,2,1,0:T(8,128)}, u32[]{:S(2)}, u32[]{:S(2)}) async-start(f32[32,2,8,128]{3,2,1,0:T(8,128)} %broadcast_in_dim.62), calls=%async_computation.7 | async-start | bytes 524288 | tf_op jit(solution)/shard_map/all_to_all | solution.py:46
  177.6 12.6 %all-to-all-start.8 = ((f32[16,2,2,8,128]{4,3,2,1,0:T(8,128)}), f32[16,2,2,8,128]{4,3,2,1,0:T(8,128)}, u32[]{:S(2)}, u32[]{:S(2)}) async-start(f32[16,2,2,8,128]{4,3,2,1,0:T(8,128)} %bitcast.36), calls=%async_computation.8 | async-start | bytes 524288 | tf_op jit(solution)/shard_map/all_to_all | solution.py:48

commit v2 on v1

--- a/solution.py
+++ b/solution.py
@@ -1,7 +1,7 @@
 import jax
 import jax.numpy as jnp
 from jax import lax
-from jax.sharding import PartitionSpec as P
+from jax.sharding import Mesh, PartitionSpec as P
 
 
 def complex_product(matrix, vector):
@@ -34,7 +34,7 @@
 
 def col_sum_to_columns(partial, offset=None):
     n_col = lax.axis_size("col")
-    n_row = lax.axis_size("row")
+    n_z = lax.axis_size("z")
     parts, rows, right = partial.shape
     piece = rows // n_col
     split = partial.reshape(parts, n_col, piece, right).transpose(1, 0, 2, 3)
@@ -42,11 +42,15 @@
     if offset is not None:
         start = lax.axis_index("col") * piece
         summed = lax.dynamic_slice_in_dim(offset, start, piece, 1) - summed
-    spread = jnp.broadcast_to(summed[None], (n_row,) + summed.shape)
-    gathered = lax.all_to_all(spread, "row", 0, 0, tiled=True)
-    paired = gathered.reshape(n_col, n_row // n_col, parts, piece, right)
-    moved = lax.all_to_all(paired, "col", 0, 0, tiled=True)
-    return moved.transpose(2, 1, 0, 3, 4).reshape(parts, (n_row // n_col) * rows, right)
+    spread = jnp.broadcast_to(summed[None], (n_z,) + summed.shape)
+    gathered = lax.all_to_all(spread, "z", 0, 0, tiled=True)
+    moved = lax.all_to_all(gathered, "col", 0, 0, tiled=True)
+    block = moved.transpose(1, 0, 2, 3).reshape(parts, rows, right)
+    other = lax.ppermute(block, "core", [(0, 1), (1, 0)])
+    first_core = lax.axis_index("core") == 0
+    return jnp.concatenate(
+        [jnp.where(first_core, block, other), jnp.where(first_core, other, block)], axis=1
+    )
 
 
 def per_device(
@@ -100,27 +104,33 @@
     result = jnp.dot(tiles, stacked, preferred_element_type=jnp.float32)
     field_rows = result.shape[0]
     out_rows = field_rows // n_col
-    split = result.reshape(n_col, out_rows, 2, right_count)
-    elevation = lax.all_to_all(split, "col", 0, 0, tiled=True).sum(0)
+    split = result.reshape(n_col, out_rows, 2 * right_count)
+    summed = lax.all_to_all(split, "col", 0, 0, tiled=True).sum(0)
+    elevation = summed.reshape(out_rows, 2, right_count)
     return (strengths, elevation)
 
 
 def solution(mesh):
+    n_row = mesh.shape["row"]
+    split_mesh = Mesh(
+        mesh.devices.reshape(n_row // 2, 2, mesh.shape["col"]), ("z", "core", "col")
+    )
+    row = ("z", "core")
     in_specs = (
-        P(None, "row", "col"),
-        P(None, "row", "col"),
-        P(None, "row", "col"),
+        P(None, row, "col"),
+        P(None, row, "col"),
+        P(None, row, "col"),
         P(None, "col", None),
-        P(None, "row", None),
+        P(None, row, None),
         P(None, None, "col"),
         P(None, "col"),
         P(None, "col"),
-        P(None, "row"),
-        P("row"),
+        P(None, row),
+        P(row),
         P(),
         P(),
     )
-    out_specs = (P(None, None, "col", None), P(("row", "col"), None, None))
+    out_specs = (P(None, None, "col", None), P(("z", "core", "col"), None, None))
     return jax.shard_map(
-        per_device, mesh=mesh, in_specs=in_specs, out_specs=out_specs, check_vma=False
+        per_device, mesh=split_mesh, in_specs=in_specs, out_specs=out_specs, check_vma=False
     )

time: 245 us -> 239 us (0.976)
  waiting for transfers between devices: 49.5 us -> 39.5 us
  starting transfers between devices: 33.3 us -> 41.9 us
  matrix products: 15.3 us -> 12.7 us
    ppermute x0 -> x3, starting transfers between devices: none -> 19.5 us  [col_sum_to_columns(): other = lax.ppermute(block, 'core', [(0, 1), (1, 0)])]
    all_to_all x5 -> x4, starting transfers between devices: 26.2 us -> 15.4 us  [the longest x2 8.33 us: col_sum_to_columns(): gathered = lax.all_to_all(spread, 'z', 0, 0, tiled=True)]
    all_to_all x5 -> x4, waiting for transfers between devices: 37.2 us -> 26.4 us  [the longest x2 22.6 us: col_sum_to_columns(): gathered = lax.all_to_all(spread, 'z', 0, 0, tiled=True)]
    concatenate x1, other arithmetic: 5.43 us -> 2.76 us  [per_device(): jnp.concatenate([tile_real, tile_imag], axis=1)]
    dot_general x1, matrix products: 4.59 us -> 1.92 us  [per_device(): result = jnp.dot(tiles, stacked, preferred_element_type=jnp.float32)]
    all_to_all x2 -> x3, blocking collectives: 81.7 us -> 82.6 us  [the longest x1 46 us: per_device(): summed = lax.all_to_all(split, 'col', 0, 0, tiled=True).sum(0)]
  transfers between devices with their start and end apart: 7 -> 9, of which waited for: 6 -> 6; matrix products, arithmetic and copies ran while one was open for 15% -> 17% of each run, Pallas kernels for 0% -> 0%
where the time goes in v2:
time: 239 us; the launch traced here: 238 us
  blocking collectives  96.8 us (41%)
  starting transfers between devices  41.9 us (18%)
  other arithmetic  39.6 us (17%)
  waiting for transfers between devices  39.5 us (17%)
  matrix products  12.7 us (5%)
  local copies, waits for them, and re-layouts  5.78 us (2%)
    all_to_all x1, blocking collectives, per_device(): summed = lax.all_to_all(split, 'col', 0, 0, tiled=True).sum(0)  46 us
    convert_element_type x1, other arithmetic, green_tile(): (amplitude * jnp.cos(phase_angle)).astype(jnp.bfloat16)  30.3 us
    all_to_all x1, blocking collectives, col_sum_to_columns(): gathered = lax.all_to_all(spread, 'z', 0, 0, tiled=True)  26.7 us
    all_to_all x2, waiting for transfers between devices, col_sum_to_columns(): gathered = lax.all_to_all(spread, 'z', 0, 0, tiled=True)  22.6 us
    ppermute x3, starting transfers between devices, col_sum_to_columns(): other = lax.ppermute(block, 'core', [(0, 1), (1, 0)])  19.5 us
    all_to_all x1, blocking collectives, col_sum_to_columns(): summed = lax.all_to_all(split, 'col', 0, 0, tiled=True).sum(0)  14.2 us
    all_to_all x2, waiting for transfers between devices, col_sum_to_columns(): summed = lax.all_to_all(split, 'col', 0, 0, tiled=True).sum(0)  12.2 us
    all_to_all x1, blocking collectives, col_sum_to_columns(): moved = lax.all_to_all(gathered, 'col', 0, 0, tiled=True)  9.89 us
  transfers between devices with their start and end apart: 9, of which 6 were waited for; matrix products, arithmetic and copies ran while one was open for 17% of the time, Pallas kernels for 0%

profile of v2, /device:TPU:1, one launch (start us, length us, event | category | flops | bytes accessed | tf_op | source)
XLA Modules:
  0.0 238.0 jit_solution(14384611570024121553)
XLA Ops:
  0.6 0.0 copy-start.3
  0.6 0.0 copy-start.6
  0.7 0.0 copy-start.5
  0.7 0.0 copy-start.4
  0.7 0.0 copy-start.2
  0.7 0.0 copy-start
  0.7 0.0 copy-start.1
  0.7 1.3 fusion.36
  2.0 1.2 fusion.42
  3.2 1.2 fusion.6
  4.5 1.2 fusion.7
  5.8 14.2 %all_to_all.50 = f32[16,2,8,128]{3,2,1,0:T(8,128)S(1)} all-to-all(f32[16,2,8,128]{3,2,1,0:T(8,128)S(1)} %maximum_bitcast_fusion.1), channel_id=1, replica_groups=mesh['z'=16,'core'=2,'col'=16] {'col'}, dimensions={0} | all-to-all | bytes 262144 | tf_op jit(solution)/shard_map/all_to_all | solution.py:41
  20.0 26.7 %all_to_all.51 = f32[16,2,8,128]{3,2,1,0:T(8,128)S(1)} all-to-all(f32[16,2,8,128]{3,2,1,0:T(8,128)S(1)} %broadcast_in_dim.60), channel_id=1, replica_groups=mesh['z'=16,'core'=2,'col'=16] {'z'}, dimensions={0} | all-to-all | bytes 262144 | tf_op jit(solution)/shard_map/all_to_all | solution.py:46
  46.7 9.9 %all_to_all.52 = f32[16,2,8,128]{3,2,1,0:T(8,128)S(1)} all-to-all(f32[16,2,8,128]{3,2,1,0:T(8,128)S(1)} %all_to_all.51), channel_id=1, replica_groups=mesh['z'=16,'core'=2,'col'=16] {'col'}, dimensions={0} | all-to-all | bytes 262144 | tf_op jit(solution)/shard_map/all_to_all | solution.py:47
  56.6 7.4 %collective-permute-start = (f32[2,128,128]{2,1,0:T(8,128)S(1)}, f32[2,128,128]{2,1,0:T(8,128)S(1)}, u32[]{:S(2)}, u32[]{:S(2)}) collective-permute-start(f32[2,128,128]{2,1,0:T(8,128)S(1)} %bitcast.153), channel_id=1, source_target_pairs={{0,16},{16,0},{1,17},{17,1},{2,18},{18,2},{3,19},{19,3},{4,20},{20... | collective-permute-start | bytes 393224 | tf_op jit(solution)/shard_map/ppermute | solution.py:49
  64.0 1.0 collective-permute-done
  65.0 1.2 fusion.32
  66.2 1.2 fusion.34
  67.4 1.2 fusion.4
  68.5 1.2 fusion.5
  69.7 0.7 maximum_bitcast_fusion.2
  70.4 3.5 %all-to-all-start.3 = ((f32[16,2,8,128]{3,2,1,0:T(8,128)}), f32[16,2,8,128]{3,2,1,0:T(8,128)S(1)}, u32[]{:S(2)}, u32[]{:S(2)}) async-start(f32[16,2,8,128]{3,2,1,0:T(8,128)} %maximum_bitcast_fusion.2), calls=%async_computation.3 | async-start | bytes 262144 | tf_op jit(solution)/shard_map/all_to_all | solution.py:41
  73.9 6.8 %all-to-all-done.3 = f32[16,2,8,128]{3,2,1,0:T(8,128)S(1)} async-done(((f32[16,2,8,128]{3,2,1,0:T(8,128)}), f32[16,2,8,128]{3,2,1,0:T(8,128)S(1)}, u32[]{:S(2)}, u32[]{:S(2)}) %all-to-all-start.3) | async-done | bytes 131104 | tf_op jit(solution)/shard_map/all_to_all | solution.py:41
  80.7 0.7 dynamic-slice_subtract_fusion
  81.5 0.7 broadcast_in_dim.61
  82.1 4.2 %all-to-all-start.4 = ((f32[16,2,8,128]{3,2,1,0:T(8,128)}), f32[16,2,8,128]{3,2,1,0:T(8,128)}, u32[]{:S(2)}, u32[]{:S(2)}) async-start(f32[16,2,8,128]{3,2,1,0:T(8,128)} %broadcast_in_dim.61), calls=%async_computation.4 | async-start | bytes 262144 | tf_op jit(solution)/shard_map/all_to_all | solution.py:46
  87.0 0.0 copy-done.6
  87.0 11.3 %all-to-all-done.4 = f32[16,2,8,128]{3,2,1,0:T(8,128)} async-done(((f32[16,2,8,128]{3,2,1,0:T(8,128)}), f32[16,2,8,128]{3,2,1,0:T(8,128)}, u32[]{:S(2)}, u32[]{:S(2)}) %all-to-all-start.4) | async-done | bytes 131104 | tf_op jit(solution)/shard_map/all_to_all | solution.py:46
  98.2 3.5 %all-to-all-start.5 = ((f32[16,2,8,128]{3,2,1,0:T(8,128)}), f32[16,2,8,128]{3,2,1,0:T(8,128)S(1)}, u32[]{:S(2)}, u32[]{:S(2)}) async-start(f32[16,2,8,128]{3,2,1,0:T(8,128)} %all-to-all-done.4), calls=%async_computation.5 | async-start | bytes 262144 | tf_op jit(solution)/shard_map/all_to_all | solution.py:47
  101.8 0.0 copy-done.5
  101.8 0.6 copy.31
  102.4 0.6 copy.30
  103.0 0.6 copy.29
  103.6 0.6 eq.26
  104.1 0.6 fusion.82
  104.8 3.8 %all-to-all-done.5 = f32[16,2,8,128]{3,2,1,0:T(8,128)S(1)} async-done(((f32[16,2,8,128]{3,2,1,0:T(8,128)}), f32[16,2,8,128]{3,2,1,0:T(8,128)S(1)}, u32[]{:S(2)}, u32[]{:S(2)}) %all-to-all-start.5) | async-done | bytes 131104 | tf_op jit(solution)/shard_map/all_to_all | solution.py:47
  108.6 6.7 %collective-permute-start.1 = (f32[2,128,128]{2,1,0:T(8,128)S(1)}, f32[2,128,128]{2,1,0:T(8,128)S(1)}, u32[]{:S(2)}, u32[]{:S(2)}) collective-permute-start(f32[2,128,128]{2,1,0:T(8,128)S(1)} %bitcast.155), channel_id=1, source_target_pairs={{0,16},{16,0},{1,17},{17,1},{2,18},{18,2},{3,19},{19,3},{4,20},{20... | collective-permute-start | bytes 393224 | tf_op jit(solution)/shard_map/ppermute | solution.py:49
  115.3 0.0 copy-done.2
  115.3 1.3 broadcast_select_fusion.7
  116.6 0.0 collective-permute-done.1
  116.7 0.0 copy-done
  116.7 0.3 fusion.24
  117.0 0.3 fusion.28
  117.2 0.3 fusion.2
  117.5 0.3 fusion.3
  117.8 0.7 maximum_bitcast_fusion.3
  118.4 3.5 %all-to-all-start.6 = ((f32[16,2,8,128]{3,2,1,0:T(8,128)}), f32[16,2,8,128]{3,2,1,0:T(8,128)S(1)}, u32[]{:S(2)}, u32[]{:S(2)}) async-start(f32[16,2,8,128]{3,2,1,0:T(8,128)} %maximum_bitcast_fusion.3), calls=%async_computation.6 | async-start | bytes 262144 | tf_op jit(solution)/shard_map/all_to_all | solution.py:41
  122.0 1.9 broadcast_select_fusion.6
  123.9 5.4 %all-to-all-done.6 = f32[16,2,8,128]{3,2,1,0:T(8,128)S(1)} async-done(((f32[16,2,8,128]{3,2,1,0:T(8,128)}), f32[16,2,8,128]{3,2,1,0:T(8,128)S(1)}, u32[]{:S(2)}, u32[]{:S(2)}) %all-to-all-start.6) | async-done | bytes 131104 | tf_op jit(solution)/shard_map/all_to_all | solution.py:41
  129.3 0.7 broadcast_in_dim.62
  130.0 4.2 %all-to-all-start.7 = ((f32[16,2,8,128]{3,2,1,0:T(8,128)}), f32[16,2,8,128]{3,2,1,0:T(8,128)}, u32[]{:S(2)}, u32[]{:S(2)}) async-start(f32[16,2,8,128]{3,2,1,0:T(8,128)} %broadcast_in_dim.62), calls=%async_computation.7 | async-start | bytes 262144 | tf_op jit(solution)/shard_map/all_to_all | solution.py:46
  134.2 0.6 fusion.81
  134.8 11.3 %all-to-all-done.7 = f32[16,2,8,128]{3,2,1,0:T(8,128)} async-done(((f32[16,2,8,128]{3,2,1,0:T(8,128)}), f32[16,2,8,128]{3,2,1,0:T(8,128)}, u32[]{:S(2)}, u32[]{:S(2)}) %all-to-all-start.7) | async-done | bytes 131104 | tf_op jit(solution)/shard_map/all_to_all | solution.py:46
  146.1 3.5 %all-to-all-start.8 = ((f32[16,2,8,128]{3,2,1,0:T(8,128)}), f32[16,2,8,128]{3,2,1,0:T(8,128)S(1)}, u32[]{:S(2)}, u32[]{:S(2)}) async-start(f32[16,2,8,128]{3,2,1,0:T(8,128)} %all-to-all-done.7), calls=%async_computation.8 | async-start | bytes 262144 | tf_op jit(solution)/shard_map/all_to_all | solution.py:47
  149.6 30.3 %multiply_convert_fusion.1 = (bf16[3072,512]{1,0:T(8,128)(2,1)S(1)}, bf16[3072,512]{1,0:T(8,128)(2,1)}) fusion(f32[]{:T(128)} %bitcast.150, f32[512]{0:T(512)S(1)} %bitcast.159, f32[512]{0:T(512)} %bitcast.160, f32[3072]{0:T(1024)} %bitcast.158, f32[512]{0:T(512)} %bitcast.161, f32[3072]{0:T(1024)} %bitcast.157, f32[512]{0:T(512)} %bitcast.162, ...), kind=kLoop, calls=%fused_computation.2 | loop fusion | flops 22020096 | bytes 6349316 | tf_op jit(solution)/shard_map/convert_element_type | solution.py:30
  179.9 0.0 all-to-all-done.8
  179.9 5.4 %collective-permute-start.2 = (f32[2,128,128]{2,1,0:T(8,128)S(1)}, f32[2,128,128]{2,1,0:T(8,128)S(1)}, u32[]{:S(2)}, u32[]{:S(2)}) collective-permute-start(f32[2,128,128]{2,1,0:T(8,128)S(1)} %bitcast.154), channel_id=1, source_target_pairs={{0,16},{16,0},{1,17},{17,1},{2,18},{18,2},{3,19},{19,3},{4,20},{20... | collective-permute-start | bytes 393224 | tf_op jit(solution)/shard_map/ppermute | solution.py:49
  185.3 2.8 %pad_maximum_fusion = bf16[3072,1024]{1,0:T(8,128)(2,1)S(1)} fusion(bf16[3072,512]{1,0:T(8,128)(2,1)} %get-tuple-element.15, bf16[3072,512]{1,0:T(8,128)(2,1)S(1)} %get-tuple-element.14), kind=kLoop, calls=%fused_computation | loop fusion | flops 12582912 | bytes 12582912 | tf_op jit(solution)/shard_map/concatenate | solution.py:103
  188.1 0.0 collective-permute-done.2
  188.2 0.9 fusion.79
  189.1 1.9 fusion.8
  191.0 46.0 %all_to_all.53 = f32[16,192,256]{2,1,0:T(8,128)S(1)} all-to-all(f32[16,192,256]{2,1,0:T(8,128)S(1)} %bitcast.151), channel_id=1, replica_groups=mesh['z'=16,'core'=2,'col'=16] {'col'}, dimensions={0} | all-to-all | bytes 6291456 | tf_op jit(solution)/shard_map/all_to_all | solution.py:108
  237.1 0.2 reduce_sum.39
  237.3 0.8 reshape.72
  (22 shorter events, 0.3 us)
Async XLA Ops:
  0.6 86.3 %copy-start.3 = (f32[2,2,256]{2,1,0:T(2,128)S(1)}, f32[2,2,256]{2,1,0:T(2,128)}, u32[]{:S(2)}) copy-start(f32[2,2,256]{2,1,0:T(2,128)} %param.17) | copy-start | bytes 12292
  0.6 86.3 %copy-start.6 = (f32[2,256]{1,0:T(2,128)S(1)}, f32[2,256]{1,0:T(2,128)}, u32[]{:S(2)}) copy-start(f32[2,256]{1,0:T(2,128)} %param.18) | copy-start | bytes 6148
  0.7 101.1 %copy-start.5 = (s32[2,256]{1,0:T(2,128)S(1)}, s32[2,256]{1,0:T(2,128)}, u32[]{:S(2)}) copy-start(s32[2,256]{1,0:T(2,128)} %param.19) | copy-start | bytes 6148
  0.7 103.5 %copy-start.4 = (f32[2,2]{1,0:T(2,128)S(1)}, f32[2,2]{1,0:T(2,128)}, u32[]{:S(2)}) copy-start(f32[2,2]{1,0:T(2,128)} %param.22) | copy-start | bytes 52
  0.7 114.7 %copy-start.2 = (s32[3072]{0:T(1024)S(1)}, s32[3072]{0:T(1024)}, u32[]{:S(2)}) copy-start(s32[3072]{0:T(1024)} %param.21) | copy-start | bytes 36868
  0.7 116.0 %copy-start = (f32[2,128,256]{2,1,0:T(8,128)S(1)}, f32[2,128,256]{2,1,0:T(8,128)}, u32[]{:S(2)}) copy-start(f32[2,128,256]{2,1,0:T(8,128)} %param.13) | copy-start | bytes 786436
  0.7 133.5 %copy-start.1 = (f32[2,3072]{1,0:T(2,128)S(1)}, f32[2,3072]{1,0:T(2,128)}, u32[]{:S(2)}) copy-start(f32[2,3072]{1,0:T(2,128)} %param.20) | copy-start | bytes 73732
  56.6 8.4 %collective-permute-start = (f32[2,128,128]{2,1,0:T(8,128)S(1)}, f32[2,128,128]{2,1,0:T(8,128)S(1)}, u32[]{:S(2)}, u32[]{:S(2)}) collective-permute-start(f32[2,128,128]{2,1,0:T(8,128)S(1)} %bitcast.153), channel_id=1, source_target_pairs={{0,16},{16,0},{1,17},{17,1},{2,18},{18,2},{3,19},{19,3},{4,20},{20... | collective-permute-start | bytes 393224 | tf_op jit(solution)/shard_map/ppermute | solution.py:49
  70.4 10.3 %all-to-all-start.3 = ((f32[16,2,8,128]{3,2,1,0:T(8,128)}), f32[16,2,8,128]{3,2,1,0:T(8,128)S(1)}, u32[]{:S(2)}, u32[]{:S(2)}) async-start(f32[16,2,8,128]{3,2,1,0:T(8,128)} %maximum_bitcast_fusion.2), calls=%async_computation.3 | async-start | bytes 262144 | tf_op jit(solution)/shard_map/all_to_all | solution.py:41
  82.1 16.1 %all-to-all-start.4 = ((f32[16,2,8,128]{3,2,1,0:T(8,128)}), f32[16,2,8,128]{3,2,1,0:T(8,128)}, u32[]{:S(2)}, u32[]{:S(2)}) async-start(f32[16,2,8,128]{3,2,1,0:T(8,128)} %broadcast_in_dim.61), calls=%async_computation.4 | async-start | bytes 262144 | tf_op jit(solution)/shard_map/all_to_all | solution.py:46
  98.2 10.3 %all-to-all-start.5 = ((f32[16,2,8,128]{3,2,1,0:T(8,128)}), f32[16,2,8,128]{3,2,1,0:T(8,128)S(1)}, u32[]{:S(2)}, u32[]{:S(2)}) async-start(f32[16,2,8,128]{3,2,1,0:T(8,128)} %all-to-all-done.4), calls=%async_computation.5 | async-start | bytes 262144 | tf_op jit(solution)/shard_map/all_to_all | solution.py:47
  108.6 8.1 %collective-permute-start.1 = (f32[2,128,128]{2,1,0:T(8,128)S(1)}, f32[2,128,128]{2,1,0:T(8,128)S(1)}, u32[]{:S(2)}, u32[]{:S(2)}) collective-permute-start(f32[2,128,128]{2,1,0:T(8,128)S(1)} %bitcast.155), channel_id=1, source_target_pairs={{0,16},{16,0},{1,17},{17,1},{2,18},{18,2},{3,19},{19,3},{4,20},{20... | collective-permute-start | bytes 393224 | tf_op jit(solution)/shard_map/ppermute | solution.py:49
  118.4 10.8 %all-to-all-start.6 = ((f32[16,2,8,128]{3,2,1,0:T(8,128)}), f32[16,2,8,128]{3,2,1,0:T(8,128)S(1)}, u32[]{:S(2)}, u32[]{:S(2)}) async-start(f32[16,2,8,128]{3,2,1,0:T(8,128)} %maximum_bitcast_fusion.3), calls=%async_computation.6 | async-start | bytes 262144 | tf_op jit(solution)/shard_map/all_to_all | solution.py:41
  130.0 16.1 %all-to-all-start.7 = ((f32[16,2,8,128]{3,2,1,0:T(8,128)}), f32[16,2,8,128]{3,2,1,0:T(8,128)}, u32[]{:S(2)}, u32[]{:S(2)}) async-start(f32[16,2,8,128]{3,2,1,0:T(8,128)} %broadcast_in_dim.62), calls=%async_computation.7 | async-start | bytes 262144 | tf_op jit(solution)/shard_map/all_to_all | solution.py:46
  146.1 33.8 %all-to-all-start.8 = ((f32[16,2,8,128]{3,2,1,0:T(8,128)}), f32[16,2,8,128]{3,2,1,0:T(8,128)S(1)}, u32[]{:S(2)}, u32[]{:S(2)}) async-start(f32[16,2,8,128]{3,2,1,0:T(8,128)} %all-to-all-done.7), calls=%async_computation.8 | async-start | bytes 262144 | tf_op jit(solution)/shard_map/all_to_all | solution.py:47
  179.9 8.2 %collective-permute-start.2 = (f32[2,128,128]{2,1,0:T(8,128)S(1)}, f32[2,128,128]{2,1,0:T(8,128)S(1)}, u32[]{:S(2)}, u32[]{:S(2)}) collective-permute-start(f32[2,128,128]{2,1,0:T(8,128)S(1)} %bitcast.154), channel_id=1, source_target_pairs={{0,16},{16,0},{1,17},{17,1},{2,18},{18,2},{3,19},{19,3},{4,20},{20... | collective-permute-start | bytes 393224 | tf_op jit(solution)/shard_map/ppermute | solution.py:49

commit v3 on v2

--- a/solution.py
+++ b/solution.py
@@ -32,25 +32,48 @@
     )
 
 
-def col_sum_to_columns(partial, offset=None):
+def beside(step, value, work):
+    if work is None:
+        return step(value), None
+    inputs, fn = work
+    value, inputs = lax.optimization_barrier((value, inputs))
+    result = step(value)
+    done = fn(*inputs)
+    return lax.optimization_barrier((result, done))
+
+
+def col_sum_to_columns(partial, offset=None, works=(None, None, None)):
     n_col = lax.axis_size("col")
     n_z = lax.axis_size("z")
     parts, rows, right = partial.shape
     piece = rows // n_col
+    outputs = []
+
+    def col_step(value):
+        return lax.all_to_all(value, "col", 0, 0, tiled=True)
+
+    def z_step(value):
+        return lax.all_to_all(value, "z", 0, 0, tiled=True)
+
     split = partial.reshape(parts, n_col, piece, right).transpose(1, 0, 2, 3)
-    summed = lax.all_to_all(split, "col", 0, 0, tiled=True).sum(0)
+    scattered, out = beside(col_step, split, works[0])
+    outputs.append(out)
+    summed = scattered.sum(0)
     if offset is not None:
         start = lax.axis_index("col") * piece
         summed = lax.dynamic_slice_in_dim(offset, start, piece, 1) - summed
     spread = jnp.broadcast_to(summed[None], (n_z,) + summed.shape)
-    gathered = lax.all_to_all(spread, "z", 0, 0, tiled=True)
-    moved = lax.all_to_all(gathered, "col", 0, 0, tiled=True)
+    gathered, out = beside(z_step, spread, works[1])
+    outputs.append(out)
+    moved, out = beside(col_step, gathered, works[2])
+    outputs.append(out)
     block = moved.transpose(1, 0, 2, 3).reshape(parts, rows, right)
     other = lax.ppermute(block, "core", [(0, 1), (1, 0)])
     first_core = lax.axis_index("core") == 0
-    return jnp.concatenate(
+    vector = jnp.concatenate(
         [jnp.where(first_core, block, other), jnp.where(first_core, other, block)], axis=1
     )
+    return vector, [o for o in outputs if o is not None]
 
 
 def per_device(
@@ -68,9 +91,49 @@
     wave_number,
 ):
     n_col = lax.axis_size("col")
-    top_solved = col_sum_to_columns(complex_product(inv_top, rhs_top))
-    remainder_cols = col_sum_to_columns(complex_product(lower_panel, top_solved), rhs_bottom)
-    bottom_solved = col_sum_to_columns(complex_product(inv_bottom, remainder_cols))
+    source_x = source_xy[0].reshape(-1)
+    source_y = source_xy[1].reshape(-1)
+    src_depth = source_depth.reshape(-1)
+    src_label = body_label.reshape(-1)
+    wave_value = wave_number[0]
+
+    def tile_chunk(point_xy, region):
+        tile_real, tile_imag = green_tile(
+            point_xy[0],
+            point_xy[1],
+            region,
+            source_x,
+            source_y,
+            src_depth,
+            src_label,
+            lid_table,
+            wave_value,
+        )
+        return jnp.concatenate([tile_real, tile_imag], axis=1)
+
+    field_rows = field_xy.shape[1]
+    n_chunks = 6
+    chunk_rows = field_rows // n_chunks
+    works = [
+        (
+            (
+                field_xy[:, i * chunk_rows : (i + 1) * chunk_rows],
+                region_label[i * chunk_rows : (i + 1) * chunk_rows],
+            ),
+            tile_chunk,
+        )
+        for i in range(n_chunks)
+    ]
+    top_solved, tiles_a = col_sum_to_columns(
+        complex_product(inv_top, rhs_top), works=(None, works[0], works[1])
+    )
+    remainder_cols, tiles_b = col_sum_to_columns(
+        complex_product(lower_panel, top_solved), rhs_bottom, works=(works[2], works[3], None)
+    )
+    bottom_solved, tiles_c = col_sum_to_columns(
+        complex_product(inv_bottom, remainder_cols), works=(works[4], works[5], None)
+    )
+    tile_chunks = tiles_a + tiles_b + tiles_c
     strengths = jnp.stack([top_solved, bottom_solved])
     weights = strengths.astype(jnp.bfloat16)
     right_count = weights.shape[3]
@@ -83,26 +146,10 @@
         ],
         axis=0,
     )
-    source_x = source_xy[0].reshape(-1)
-    source_y = source_xy[1].reshape(-1)
-    src_depth = source_depth.reshape(-1)
-    src_label = body_label.reshape(-1)
-    wave_value = wave_number[0]
-
-    tile_real, tile_imag = green_tile(
-        field_xy[0],
-        field_xy[1],
-        region_label,
-        source_x,
-        source_y,
-        src_depth,
-        src_label,
-        lid_table,
-        wave_value,
+    result = jnp.concatenate(
+        [jnp.dot(tiles, stacked, preferred_element_type=jnp.float32) for tiles in tile_chunks],
+        axis=0,
     )
-    tiles = lax.optimization_barrier(jnp.concatenate([tile_real, tile_imag], axis=1))
-    result = jnp.dot(tiles, stacked, preferred_element_type=jnp.float32)
-    field_rows = result.shape[0]
     out_rows = field_rows // n_col
     split = result.reshape(n_col, out_rows, 2 * right_count)
     summed = lax.all_to_all(split, "col", 0, 0, tiled=True).sum(0)

time: 239 us -> 241 us (level)
  blocking collectives: 96.8 us -> 66.2 us
  starting transfers between devices: 41.9 us -> 68.5 us
  waiting for transfers between devices: 39.5 us -> 18 us
  other arithmetic: 39.6 us -> 59.1 us
  local copies, waits for them, and re-layouts: 5.78 us -> 12.1 us
    all_to_all x3 -> x2, blocking collectives: 50.8 us -> 24.6 us  [col_step(): return lax.all_to_all(value, 'col', 0, 0, tiled=True)]
    all_to_all x6 -> x7, starting transfers between devices: 22.4 us -> 47.3 us  [the longest x3 25.4 us: z_step(): return lax.all_to_all(value, 'z', 0, 0, tiled=True)]
    all_to_all x6 -> x7, waiting for transfers between devices: 38.6 us -> 15.2 us  [the longest x3 11.6 us: z_step(): return lax.all_to_all(value, 'z', 0, 0, tiled=True)]
    select_n x1 -> x6, other arithmetic: 1.28 us -> 10 us  [green_tile(): lid_second = jnp.where(region == 1, lid_table[1, 1], lid_table[0, 1])]
    select_n x1 -> x6, other arithmetic: 1.93 us -> 8.2 us  [green_tile(): lid_first = jnp.where(region == 1, lid_table[1, 0], lid_table[0, 0])]
    all_to_all x1, blocking collectives: 46 us -> 41.6 us  [per_device(): summed = lax.all_to_all(split, 'col', 0, 0, tiled=True).sum(0)]
    slice x1 -> x8, local copies, waits for them, and re-layouts: 0.62 us -> 4.72 us  [the longest x6 1.98 us: tile_chunk(): point_xy[0]]
    convert_element_type x1 -> x6, other arithmetic: 30.3 us -> 31.8 us  [green_tile(): (amplitude * jnp.cos(phase_angle)).astype(jnp.bfloat16)]
  transfers between devices with their start and end apart: 9 -> 10, of which waited for: 6 -> 8; matrix products, arithmetic and copies ran while one was open for 17% -> 20% of each run, Pallas kernels for 0% -> 0%
where the time goes in v3:
time: 241 us; the launch traced here: 239 us
  starting transfers between devices  68.5 us (28%)
  blocking collectives  66.2 us (27%)
  other arithmetic  59.1 us (25%)
  waiting for transfers between devices  18 us (7%)
  matrix products  13.3 us (6%)
  local copies, waits for them, and re-layouts  12.1 us (5%)
    all_to_all x1, blocking collectives, per_device(): summed = lax.all_to_all(split, 'col', 0, 0, tiled=True).sum(0)  41.6 us
    convert_element_type x6, other arithmetic, green_tile(): (amplitude * jnp.cos(phase_angle)).astype(jnp.bfloat16)  31.8 us
    all_to_all x3, starting transfers between devices, z_step(): return lax.all_to_all(value, 'z', 0, 0, tiled=True)  25.4 us
    all_to_all x2, blocking collectives, col_step(): return lax.all_to_all(value, 'col', 0, 0, tiled=True)  24.6 us
    all_to_all x4, starting transfers between devices, col_step(): return lax.all_to_all(value, 'col', 0, 0, tiled=True)  22 us
    ppermute x3, starting transfers between devices, col_sum_to_columns(): other = lax.ppermute(block, 'core', [(0, 1), (1, 0)])  21.2 us
    all_to_all x3, waiting for transfers between devices, z_step(): return lax.all_to_all(value, 'z', 0, 0, tiled=True)  11.6 us
    select_n x6, other arithmetic, green_tile(): lid_second = jnp.where(region == 1, lid_table[1, 1], lid_table[0, 1])  10 us
  transfers between devices with their start and end apart: 10, of which 8 were waited for; matrix products, arithmetic and copies ran while one was open for 20% of the time, Pallas kernels for 0%

profile of v3, /device:TPU:1, one launch (start us, length us, event | category | flops | bytes accessed | tf_op | source)
XLA Modules:
  0.0 239.2 jit_solution(13019436606483509618)
XLA Ops:
  0.6 1.2 fusion.38
  1.9 1.2 fusion.44
  3.1 1.2 fusion.4
  4.4 1.2 fusion.5
  6.3 7.6 %all-to-all-start = ((f32[16,2,8,128]{3,2,1,0:T(8,128)}), f32[16,2,8,128]{3,2,1,0:T(8,128)S(1)}, u32[]{:S(2)}, u32[]{:S(2)}) async-start(f32[16,2,8,128]{3,2,1,0:T(8,128)} %maximum_bitcast_fusion.1), calls=%async_computation | async-start | bytes 262144 | tf_op jit(solution)/shard_map/all_to_all | solution.py:53
  14.5 0.7 slice_bitcast_fusion.1
  15.2 1.4 fusion.83
  16.6 1.4 fusion.82
  18.0 0.7 exponential_bitcast_fusion
  18.6 0.7 broadcast_compare_fusion.6
  19.4 1.4 fusion.90
  21.6 15.0 %all-to-all-start.1 = ((f32[16,2,8,128]{3,2,1,0:T(8,128)}), f32[16,2,8,128]{3,2,1,0:T(8,128)}, u32[]{:S(2)}, u32[]{:S(2)}) async-start(f32[16,2,8,128]{3,2,1,0:T(8,128)} %broadcast_in_dim.165), calls=%async_computation.1 | async-start | bytes 262144 | tf_op jit(solution)/shard_map/all_to_all | solution.py:56
  36.5 1.2 broadcast_select_fusion.17
  37.7 1.3 broadcast_select_fusion.11
  39.0 4.9 %multiply_convert_fusion.11 = (bf16[512,512]{1,0:T(8,128)(2,1)S(1)}, bf16[512,512]{1,0:T(8,128)(2,1)S(1)}) fusion(f32[]{:T(128)} %bitcast.165, f32[512]{0:T(512)S(1)} %bitcast.205, f32[512]{0:T(512)S(1)} %bitcast.193, f32[512]{0:T(512)S(1)} %bitcast.214, f32[512]{0:T(512)S(1)} %bitcast.187, f32[512]{0:T(512)S(1)} %bitcast.213, f32[512]{0:T(512)S(1)} %bitcast.199, ...), kind=kLoop, calls=%fused_computation.50 | loop fusion | flops 3670016 | bytes 1065476 | tf_op jit(solution)/shard_map/convert_element_type | solution.py:30
  44.1 4.5 %all-to-all-done.1 = f32[16,2,8,128]{3,2,1,0:T(8,128)} async-done(((f32[16,2,8,128]{3,2,1,0:T(8,128)}), f32[16,2,8,128]{3,2,1,0:T(8,128)}, u32[]{:S(2)}, u32[]{:S(2)}) %all-to-all-start.1) | async-done | bytes 131104 | tf_op jit(solution)/shard_map/all_to_all | solution.py:56
  48.5 1.2 broadcast_select_fusion.16
  49.7 1.3 broadcast_select_fusion.10
  51.0 6.7 %all-to-all-start.2 = ((f32[16,2,8,128]{3,2,1,0:T(8,128)}), f32[16,2,8,128]{3,2,1,0:T(8,128)S(1)}, u32[]{:S(2)}, u32[]{:S(2)}) async-start(f32[16,2,8,128]{3,2,1,0:T(8,128)} %all-to-all-done.1), calls=%async_computation.2 | async-start | bytes 262144 | tf_op jit(solution)/shard_map/all_to_all | solution.py:53
  57.7 4.9 %multiply_convert_fusion.9 = (bf16[512,512]{1,0:T(8,128)(2,1)S(1)}, bf16[512,512]{1,0:T(8,128)(2,1)S(1)}) fusion(f32[512]{0:T(512)S(1)} %bitcast.218, f32[512]{0:T(512)S(1)} %bitcast.217, f32[]{:T(128)} %bitcast.166, f32[512]{0:T(512)S(1)} %bitcast.206, f32[512]{0:T(512)S(1)} %bitcast.194, f32[512]{0:T(512)S(1)} %bitcast.188, f32[512]{0:T(512)S(1)} %bitcast.200, ...), kind=kLoop, calls=%fused_computation.45 | loop fusion | flops 3670016 | bytes 1065476 | tf_op jit(solution)/shard_map/convert_element_type | solution.py:30
  62.7 1.8 all-to-all-done.2
  64.5 7.1 %collective-permute-start = (f32[2,128,128]{2,1,0:T(8,128)S(1)}, f32[2,128,128]{2,1,0:T(8,128)S(1)}, u32[]{:S(2)}, u32[]{:S(2)}) collective-permute-start(f32[2,128,128]{2,1,0:T(8,128)S(1)} %bitcast.178), channel_id=1, source_target_pairs={{0,16},{16,0},{1,17},{17,1},{2,18},{18,2},{3,19},{19,3},{4,20},{20... | collective-permute-start | bytes 393224 | tf_op jit(solution)/shard_map/ppermute | solution.py:71
  71.7 1.0 collective-permute-done
  73.8 0.7 maximum_bitcast_fusion.2
  74.4 1.2 broadcast_select_fusion.15
  75.6 1.3 broadcast_select_fusion.9
  76.9 4.0 %all-to-all-start.3 = ((f32[16,2,8,128]{3,2,1,0:T(8,128)}), f32[16,2,8,128]{3,2,1,0:T(8,128)S(1)}, u32[]{:S(2)}, u32[]{:S(2)}) async-start(f32[16,2,8,128]{3,2,1,0:T(8,128)} %maximum_bitcast_fusion.2), calls=%async_computation.3 | async-start | bytes 262144 | tf_op jit(solution)/shard_map/all_to_all | solution.py:53
  81.0 4.9 %multiply_convert_fusion.7 = (bf16[512,512]{1,0:T(8,128)(2,1)S(1)}, bf16[512,512]{1,0:T(8,128)(2,1)S(1)}) fusion(f32[512]{0:T(512)S(1)} %bitcast.220, f32[512]{0:T(512)S(1)} %bitcast.219, f32[]{:T(128)} %bitcast.170, f32[512]{0:T(512)S(1)} %bitcast.207, f32[512]{0:T(512)S(1)} %bitcast.195, f32[512]{0:T(512)S(1)} %bitcast.189, f32[512]{0:T(512)S(1)} %bitcast.201, ...), kind=kLoop, calls=%fused_computation.40 | loop fusion | flops 3670016 | bytes 1065476 | tf_op jit(solution)/shard_map/convert_element_type | solution.py:30
  86.0 1.7 all-to-all-done.3
  87.8 0.7 dynamic-slice_subtract_fusion
  89.2 2.4 %broadcast_select_fusion.14 = (f32[512]{0:T(512)}, pred[512]{0:T(512)(128)(4,1)S(1)}) fusion(f32[]{:T(128)} %bitcast.10, f32[]{:T(128)} %bitcast.9, s32[512]{0:T(512)} %get-tuple-element.45), kind=kLoop, calls=%fused_computation.136 | loop fusion | flops 1024 | bytes 4616 | tf_op jit(solution)/shard_map/jit(_where)/select_n | solution.py:25
  91.6 1.4 fusion.86
  92.9 5.0 %all-to-all-start.4 = ((f32[16,2,8,128]{3,2,1,0:T(8,128)}), f32[16,2,8,128]{3,2,1,0:T(8,128)S(1)}, u32[]{:S(2)}, u32[]{:S(2)}) async-start(f32[16,2,8,128]{3,2,1,0:T(8,128)} %broadcast_in_dim.177), calls=%async_computation.4 | async-start | bytes 262144 | tf_op jit(solution)/shard_map/all_to_all | solution.py:56
  97.9 1.3 broadcast_select_fusion.8
  99.2 5.7 %multiply_convert_fusion.5 = (bf16[512,512]{1,0:T(8,128)(2,1)S(1)}, bf16[512,512]{1,0:T(8,128)(2,1)S(1)}) fusion(f32[512]{0:T(512)} %bitcast.216, f32[512]{0:T(512)} %bitcast.215, f32[]{:T(128)} %bitcast.169, f32[512]{0:T(512)} %bitcast.208, f32[512]{0:T(512)} %bitcast.196, f32[512]{0:T(512)} %bitcast.190, f32[512]{0:T(512)} %bitcast.202, ...), kind=kLoop, calls=%fused_computation.35 | loop fusion | flops 3670016 | bytes 1065476 | tf_op jit(solution)/shard_map/convert_element_type | solution.py:30
  104.9 1.1 pad_maximum_fusion.3
  106.0 3.8 %all-to-all-done.4 = f32[16,2,8,128]{3,2,1,0:T(8,128)S(1)} async-done(((f32[16,2,8,128]{3,2,1,0:T(8,128)}), f32[16,2,8,128]{3,2,1,0:T(8,128)S(1)}, u32[]{:S(2)}, u32[]{:S(2)}) %all-to-all-start.4) | async-done | bytes 131104 | tf_op jit(solution)/shard_map/all_to_all | solution.py:56
  109.9 11.6 %all_to_all.50 = f32[16,2,8,128]{3,2,1,0:T(8,128)S(1)} all-to-all(f32[16,2,8,128]{3,2,1,0:T(8,128)S(1)} %all-to-all-done.4), channel_id=1, replica_groups=mesh['z'=16,'core'=2,'col'=16] {'col'}, dimensions={0} | all-to-all | bytes 262144 | tf_op jit(solution)/shard_map/all_to_all | solution.py:53
  121.5 7.0 %collective-permute-start.1 = (f32[2,128,128]{2,1,0:T(8,128)S(1)}, f32[2,128,128]{2,1,0:T(8,128)S(1)}, u32[]{:S(2)}, u32[]{:S(2)}) collective-permute-start(f32[2,128,128]{2,1,0:T(8,128)S(1)} %bitcast.179), channel_id=1, source_target_pairs={{0,16},{16,0},{1,17},{17,1},{2,18},{18,2},{3,19},{19,3},{4,20},{20... | collective-permute-start | bytes 393224 | tf_op jit(solution)/shard_map/ppermute | solution.py:71
  128.5 1.0 collective-permute-done.1
  129.5 1.2 fusion.26
  130.6 1.2 fusion.30
  131.8 1.2 fusion
  133.0 1.2 fusion.1
  134.9 1.8 broadcast_select_fusion.13
  136.6 1.3 broadcast_select_fusion.7
  138.5 3.7 %all-to-all-start.6 = ((f32[16,2,8,128]{3,2,1,0:T(8,128)}), f32[16,2,8,128]{3,2,1,0:T(8,128)S(1)}, u32[]{:S(2)}, u32[]{:S(2)}) async-start(f32[16,2,8,128]{3,2,1,0:T(8,128)} %maximum_bitcast_fusion.3), calls=%async_computation.6 | async-start | bytes 262144 | tf_op jit(solution)/shard_map/all_to_all | solution.py:53
  142.2 5.7 %multiply_convert_fusion.3 = (bf16[512,512]{1,0:T(8,128)(2,1)S(1)}, bf16[512,512]{1,0:T(8,128)(2,1)S(1)}) fusion(f32[512]{0:T(512)} %bitcast.222, f32[512]{0:T(512)} %bitcast.221, f32[]{:T(128)} %bitcast.168, f32[512]{0:T(512)} %bitcast.209, f32[512]{0:T(512)} %bitcast.197, f32[512]{0:T(512)S(1)} %bitcast.192, f32[512]{0:T(512)} %bitcast.203, ...), kind=kLoop, calls=%fused_computation.30 | loop fusion | flops 3670016 | bytes 1065476 | tf_op jit(solution)/shard_map/convert_element_type | solution.py:30
  147.9 1.1 pad_maximum_fusion.4
  149.7 2.3 broadcast_select_fusion.12
  152.1 5.4 %all-to-all-start.7 = ((f32[16,2,8,128]{3,2,1,0:T(8,128)}), f32[16,2,8,128]{3,2,1,0:T(8,128)S(1)}, u32[]{:S(2)}, u32[]{:S(2)}) async-start(f32[16,2,8,128]{3,2,1,0:T(8,128)} %broadcast_in_dim.182), calls=%async_computation.7 | async-start | bytes 262144 | tf_op jit(solution)/shard_map/all_to_all | solution.py:56
  157.5 1.9 broadcast_select_fusion.6
  159.5 5.6 %multiply_convert_fusion.1 = (bf16[512,512]{1,0:T(8,128)(2,1)S(1)}, bf16[512,512]{1,0:T(8,128)(2,1)S(1)}) fusion(f32[512]{0:T(512)S(1)} %bitcast.212, f32[512]{0:T(512)S(1)} %bitcast.211, f32[]{:T(128)} %bitcast.167, f32[512]{0:T(512)} %bitcast.210, f32[512]{0:T(512)} %bitcast.198, f32[512]{0:T(512)} %bitcast.191, f32[512]{0:T(512)} %bitcast.204, ...), kind=kLoop, calls=%fused_computation.25 | loop fusion | flops 3670016 | bytes 1065476 | tf_op jit(solution)/shard_map/convert_element_type | solution.py:30
  165.1 1.1 pad_maximum_fusion.5
  166.2 3.3 %all-to-all-done.7 = f32[16,2,8,128]{3,2,1,0:T(8,128)S(1)} async-done(((f32[16,2,8,128]{3,2,1,0:T(8,128)}), f32[16,2,8,128]{3,2,1,0:T(8,128)S(1)}, u32[]{:S(2)}, u32[]{:S(2)}) %all-to-all-start.7) | async-done | bytes 131104 | tf_op jit(solution)/shard_map/all_to_all | solution.py:56
  169.5 13.1 %all_to_all.51 = f32[16,2,8,128]{3,2,1,0:T(8,128)S(1)} all-to-all(f32[16,2,8,128]{3,2,1,0:T(8,128)S(1)} %all-to-all-done.7), channel_id=1, replica_groups=mesh['z'=16,'core'=2,'col'=16] {'col'}, dimensions={0} | all-to-all | bytes 262144 | tf_op jit(solution)/shard_map/all_to_all | solution.py:53
  182.6 7.1 %collective-permute-start.2 = (f32[2,128,128]{2,1,0:T(8,128)S(1)}, f32[2,128,128]{2,1,0:T(8,128)S(1)}, u32[]{:S(2)}, u32[]{:S(2)}) collective-permute-start(f32[2,128,128]{2,1,0:T(8,128)S(1)} %bitcast.180), channel_id=1, source_target_pairs={{0,16},{16,0},{1,17},{17,1},{2,18},{18,2},{3,19},{19,3},{4,20},{20... | collective-permute-start | bytes 393224 | tf_op jit(solution)/shard_map/ppermute | solution.py:71
  189.7 1.0 collective-permute-done.2
  190.7 0.9 fusion.80
  193.0 0.8 copy-done
  194.2 0.8 copy-done.1
  195.4 0.8 copy-done.2
  196.6 41.6 %all_to_all.52 = f32[16,192,256]{2,1,0:T(8,128)S(1)} all-to-all(f32[16,192,256]{2,1,0:T(8,128)S(1)} %bitcast.171), channel_id=1, replica_groups=mesh['z'=16,'core'=2,'col'=16] {'col'}, dimensions={0} | all-to-all | bytes 6291456 | tf_op jit(solution)/shard_map/all_to_all | solution.py:155
  238.5 0.8 reshape.92
  (62 shorter events, 8.5 us)
Async XLA Ops:
  6.3 14.6 %all-to-all-start = ((f32[16,2,8,128]{3,2,1,0:T(8,128)}), f32[16,2,8,128]{3,2,1,0:T(8,128)S(1)}, u32[]{:S(2)}, u32[]{:S(2)}) async-start(f32[16,2,8,128]{3,2,1,0:T(8,128)} %maximum_bitcast_fusion.1), calls=%async_computation | async-start | bytes 262144 | tf_op jit(solution)/shard_map/all_to_all | solution.py:53
  19.4 61.6 %copy-start.10 = (pred[512]{0:T(512)(128)(4,1)}, pred[512]{0:T(512)(128)(4,1)S(1)}, u32[]{:S(2)}) copy-start(pred[512]{0:T(512)(128)(4,1)S(1)} %eq.47) | copy-start | bytes 1540
  19.4 61.6 %copy-start.5 = (f32[1,2,2,128]{3,1,2,0:T(2,128)}, f32[1,2,2,128]{3,1,2,0:T(2,128)S(1)}, u32[]{:S(2)}) copy-start(f32[1,2,2,128]{3,1,2,0:T(2,128)S(1)} %copy.30) | copy-start | bytes 6148
  19.4 61.6 %copy-start.7 = (f32[1,2,2,128]{3,1,2,0:T(2,128)}, f32[1,2,2,128]{3,1,2,0:T(2,128)S(1)}, u32[]{:S(2)}) copy-start(f32[1,2,2,128]{3,1,2,0:T(2,128)S(1)} %copy.31) | copy-start | bytes 6148
  19.4 61.5 %copy-start.8 = (f32[1,2,2,128]{3,1,2,0:T(2,128)}, f32[1,2,2,128]{3,1,2,0:T(2,128)S(1)}, u32[]{:S(2)}) copy-start(f32[1,2,2,128]{3,1,2,0:T(2,128)S(1)} %copy.29) | copy-start | bytes 6148
  19.4 61.5 %copy-start.9 = (f32[1,2,2,128]{3,1,2,0:T(2,128)}, f32[1,2,2,128]{3,1,2,0:T(2,128)S(1)}, u32[]{:S(2)}) copy-start(f32[1,2,2,128]{3,1,2,0:T(2,128)S(1)} %copy.32) | copy-start | bytes 6148
  21.6 27.0 %all-to-all-start.1 = ((f32[16,2,8,128]{3,2,1,0:T(8,128)}), f32[16,2,8,128]{3,2,1,0:T(8,128)}, u32[]{:S(2)}, u32[]{:S(2)}) async-start(f32[16,2,8,128]{3,2,1,0:T(8,128)} %broadcast_in_dim.165), calls=%async_computation.1 | async-start | bytes 262144 | tf_op jit(solution)/shard_map/all_to_all | solution.py:56
  43.9 28.8 %copy-start.3 = (f32[2,128,256]{2,1,0:T(8,128)S(1)}, f32[2,128,256]{2,1,0:T(8,128)}, u32[]{:S(2)}) copy-start(f32[2,128,256]{2,1,0:T(8,128)} %param.14) | copy-start | bytes 786436
  51.0 13.5 %all-to-all-start.2 = ((f32[16,2,8,128]{3,2,1,0:T(8,128)}), f32[16,2,8,128]{3,2,1,0:T(8,128)S(1)}, u32[]{:S(2)}, u32[]{:S(2)}) async-start(f32[16,2,8,128]{3,2,1,0:T(8,128)} %all-to-all-done.1), calls=%async_computation.2 | async-start | bytes 262144 | tf_op jit(solution)/shard_map/all_to_all | solution.py:53
  64.5 8.1 %collective-permute-start = (f32[2,128,128]{2,1,0:T(8,128)S(1)}, f32[2,128,128]{2,1,0:T(8,128)S(1)}, u32[]{:S(2)}, u32[]{:S(2)}) collective-permute-start(f32[2,128,128]{2,1,0:T(8,128)S(1)} %bitcast.178), channel_id=1, source_target_pairs={{0,16},{16,0},{1,17},{17,1},{2,18},{18,2},{3,19},{19,3},{4,20},{20... | collective-permute-start | bytes 393224 | tf_op jit(solution)/shard_map/ppermute | solution.py:71
  76.9 10.9 %all-to-all-start.3 = ((f32[16,2,8,128]{3,2,1,0:T(8,128)}), f32[16,2,8,128]{3,2,1,0:T(8,128)S(1)}, u32[]{:S(2)}, u32[]{:S(2)}) async-start(f32[16,2,8,128]{3,2,1,0:T(8,128)} %maximum_bitcast_fusion.2), calls=%async_computation.3 | async-start | bytes 262144 | tf_op jit(solution)/shard_map/all_to_all | solution.py:53
  92.9 16.9 %all-to-all-start.4 = ((f32[16,2,8,128]{3,2,1,0:T(8,128)}), f32[16,2,8,128]{3,2,1,0:T(8,128)S(1)}, u32[]{:S(2)}, u32[]{:S(2)}) async-start(f32[16,2,8,128]{3,2,1,0:T(8,128)} %broadcast_in_dim.177), calls=%async_computation.4 | async-start | bytes 262144 | tf_op jit(solution)/shard_map/all_to_all | solution.py:56
  99.2 35.7 %copy-start.4 = (s32[512]{0:T(512)S(1)}, s32[512]{0:T(512)}, u32[]{:S(2)}) copy-start(s32[512]{0:T(512)} %get-tuple-element.49) | copy-start | bytes 6148
  104.9 37.3 %copy-start.6 = (f32[1,2,2,128]{3,1,2,0:T(2,128)S(1)}, f32[1,2,2,128]{3,1,2,0:T(2,128)}, u32[]{:S(2)}) copy-start(f32[1,2,2,128]{3,1,2,0:T(2,128)} %copy-done.5) | copy-start | bytes 6148
  121.5 8.0 %collective-permute-start.1 = (f32[2,128,128]{2,1,0:T(8,128)S(1)}, f32[2,128,128]{2,1,0:T(8,128)S(1)}, u32[]{:S(2)}, u32[]{:S(2)}) collective-permute-start(f32[2,128,128]{2,1,0:T(8,128)S(1)} %bitcast.179), channel_id=1, source_target_pairs={{0,16},{16,0},{1,17},{17,1},{2,18},{18,2},{3,19},{19,3},{4,20},{20... | collective-permute-start | bytes 393224 | tf_op jit(solution)/shard_map/ppermute | solution.py:71
  138.5 10.6 %all-to-all-start.6 = ((f32[16,2,8,128]{3,2,1,0:T(8,128)}), f32[16,2,8,128]{3,2,1,0:T(8,128)S(1)}, u32[]{:S(2)}, u32[]{:S(2)}) async-start(f32[16,2,8,128]{3,2,1,0:T(8,128)} %maximum_bitcast_fusion.3), calls=%async_computation.6 | async-start | bytes 262144 | tf_op jit(solution)/shard_map/all_to_all | solution.py:53
  152.1 17.4 %all-to-all-start.7 = ((f32[16,2,8,128]{3,2,1,0:T(8,128)}), f32[16,2,8,128]{3,2,1,0:T(8,128)S(1)}, u32[]{:S(2)}, u32[]{:S(2)}) async-start(f32[16,2,8,128]{3,2,1,0:T(8,128)} %broadcast_in_dim.182), calls=%async_computation.7 | async-start | bytes 262144 | tf_op jit(solution)/shard_map/all_to_all | solution.py:56
  182.6 8.0 %collective-permute-start.2 = (f32[2,128,128]{2,1,0:T(8,128)S(1)}, f32[2,128,128]{2,1,0:T(8,128)S(1)}, u32[]{:S(2)}, u32[]{:S(2)}) collective-permute-start(f32[2,128,128]{2,1,0:T(8,128)S(1)} %bitcast.180), channel_id=1, source_target_pairs={{0,16},{16,0},{1,17},{17,1},{2,18},{18,2},{3,19},{19,3},{4,20},{20... | collective-permute-start | bytes 393224 | tf_op jit(solution)/shard_map/ppermute | solution.py:71
  192.5 1.2 copy-start
  193.7 1.2 copy-start.1
  195.0 1.2 copy-start.2

commit v4 on v3

--- a/solution.py
+++ b/solution.py
@@ -4,15 +4,25 @@
 from jax.sharding import Mesh, PartitionSpec as P
 
 
-def complex_product(matrix, vector):
-    highest = lax.Precision.HIGHEST
-    real_part = jnp.dot(
-        matrix[0], vector[0], precision=highest, preferred_element_type=jnp.float32
-    ) - jnp.dot(matrix[1], vector[1], precision=highest, preferred_element_type=jnp.float32)
-    imag_part = jnp.dot(
-        matrix[0], vector[1], precision=highest, preferred_element_type=jnp.float32
-    ) + jnp.dot(matrix[1], vector[0], precision=highest, preferred_element_type=jnp.float32)
-    return jnp.stack([real_part, imag_part])
+def stacked_matrix(matrix):
+    return jnp.concatenate(
+        [
+            jnp.concatenate([matrix[0], -matrix[1]], axis=1),
+            jnp.concatenate([matrix[1], matrix[0]], axis=1),
+        ],
+        axis=0,
+    )
+
+
+def complex_product(stacked, vector):
+    parts, rows, right = vector.shape
+    product = jnp.dot(
+        stacked,
+        vector.reshape(parts * rows, right),
+        precision=lax.Precision.HIGHEST,
+        preferred_element_type=jnp.float32,
+    )
+    return product.reshape(parts, stacked.shape[0] // parts, right)
 
 
 def green_tile(
@@ -112,28 +122,16 @@
         return jnp.concatenate([tile_real, tile_imag], axis=1)
 
     field_rows = field_xy.shape[1]
-    n_chunks = 6
-    chunk_rows = field_rows // n_chunks
-    works = [
-        (
-            (
-                field_xy[:, i * chunk_rows : (i + 1) * chunk_rows],
-                region_label[i * chunk_rows : (i + 1) * chunk_rows],
-            ),
-            tile_chunk,
-        )
-        for i in range(n_chunks)
-    ]
-    top_solved, tiles_a = col_sum_to_columns(
-        complex_product(inv_top, rhs_top), works=(None, works[0], works[1])
+    top_solved, tile_chunks = col_sum_to_columns(
+        complex_product(stacked_matrix(inv_top), rhs_top),
+        works=(None, ((field_xy, region_label), tile_chunk), None),
     )
-    remainder_cols, tiles_b = col_sum_to_columns(
-        complex_product(lower_panel, top_solved), rhs_bottom, works=(works[2], works[3], None)
+    remainder_cols, _ = col_sum_to_columns(
+        complex_product(stacked_matrix(lower_panel), top_solved), rhs_bottom
     )
-    bottom_solved, tiles_c = col_sum_to_columns(
-        complex_product(inv_bottom, remainder_cols), works=(works[4], works[5], None)
+    bottom_solved, _ = col_sum_to_columns(
+        complex_product(stacked_matrix(inv_bottom), remainder_cols)
     )
-    tile_chunks = tiles_a + tiles_b + tiles_c
     strengths = jnp.stack([top_solved, bottom_solved])
     weights = strengths.astype(jnp.bfloat16)
     right_count = weights.shape[3]

time: 241 us -> 235 us (0.975)
  blocking collectives: 66.2 us -> 100 us
  other arithmetic: 59.1 us -> 40.1 us
  starting transfers between devices: 68.5 us -> 52.5 us
  waiting for transfers between devices: 18 us -> 25.8 us
  matrix products: 13.3 us -> 6.44 us
  local copies, waits for them, and re-layouts: 12.1 us -> 7.86 us
    all_to_all x0 -> x2, blocking collectives: none -> 38.8 us  [z_step(): return lax.all_to_all(value, 'z', 0, 0, tiled=True)]
    all_to_all x4, waiting for transfers between devices: 3.52 us -> 23 us  [col_step(): return lax.all_to_all(value, 'col', 0, 0, tiled=True)]
    all_to_all x3 -> x1, waiting for transfers between devices: 11.6 us -> 0.01 us  [z_step(): return lax.all_to_all(value, 'z', 0, 0, tiled=True)]
    all_to_all x3 -> x1, starting transfers between devices: 25.4 us -> 15 us  [z_step(): return lax.all_to_all(value, 'z', 0, 0, tiled=True)]
    dot_general x12 -> x3, matrix products: 10.7 us -> 1.74 us  [complex_product(): jnp.dot(stacked, vector.reshape(parts * rows, right), precision=lax.Preci...]
    select_n x6 -> x1, other arithmetic: 10 us -> 1.89 us  [green_tile(): lid_second = jnp.where(region == 1, lid_table[1, 1], lid_table[0, 1])]
    select_n x6 -> x1, other arithmetic: 8.2 us -> 1.32 us  [green_tile(): lid_first = jnp.where(region == 1, lid_table[1, 0], lid_table[0, 0])]
    all_to_all x2, blocking collectives: 24.6 us -> 19.6 us  [col_step(): return lax.all_to_all(value, 'col', 0, 0, tiled=True)]
  transfers between devices with their start and end apart: 10 -> 8, of which waited for: 8 -> 7; matrix products, arithmetic and copies ran while one was open for 20% -> 16% of each run, Pallas kernels for 0% -> 0%
where the time goes in v4:
time: 235 us; the launch traced here: 234 us
  blocking collectives  100 us (43%)
  starting transfers between devices  52.5 us (22%)
  other arithmetic  40.1 us (17%)
  waiting for transfers between devices  25.8 us (11%)
  local copies, waits for them, and re-layouts  7.86 us (3%)
  matrix products  6.44 us (3%)
    all_to_all x1, blocking collectives, per_device(): summed = lax.all_to_all(split, 'col', 0, 0, tiled=True).sum(0)  41.6 us
    all_to_all x2, blocking collectives, z_step(): return lax.all_to_all(value, 'z', 0, 0, tiled=True)  38.8 us
    convert_element_type x1, other arithmetic, green_tile(): (amplitude * jnp.cos(phase_angle)).astype(jnp.bfloat16)  28.1 us
    all_to_all x4, waiting for transfers between devices, col_step(): return lax.all_to_all(value, 'col', 0, 0, tiled=True)  23 us
    all_to_all x2, blocking collectives, col_step(): return lax.all_to_all(value, 'col', 0, 0, tiled=True)  19.6 us
    ppermute x3, starting transfers between devices, col_sum_to_columns(): other = lax.ppermute(block, 'core', [(0, 1), (1, 0)])  18.9 us
    all_to_all x4, starting transfers between devices, col_step(): return lax.all_to_all(value, 'col', 0, 0, tiled=True)  18.6 us
    all_to_all x1, starting transfers between devices, z_step(): return lax.all_to_all(value, 'z', 0, 0, tiled=True)  15 us
  transfers between devices with their start and end apart: 8, of which 7 were waited for; matrix products, arithmetic and copies ran while one was open for 16% of the time, Pallas kernels for 0%

profile of v4, /device:TPU:1, one launch (start us, length us, event | category | flops | bytes accessed | tf_op | source)
XLA Modules:
  0.0 234.3 jit_solution(8838557348368252621)
XLA Ops:
  0.6 0.0 copy-start
  0.6 1.0 slice_bitcast_fusion.4
  1.7 0.9 fusion.11
  2.7 0.0 copy-done
  2.7 0.6 convolution_bitcast_fusion.2
  3.3 0.7 copy.17
  3.9 7.6 %all-to-all-start = ((f32[16,2,8,128]{3,2,1,0:T(8,128)}), f32[16,2,8,128]{3,2,1,0:T(8,128)S(1)}, u32[]{:S(2)}, u32[]{:S(2)}) async-start(f32[16,2,8,128]{3,2,1,0:T(8,128)} %copy.17), calls=%async_computation | async-start | bytes 262144 | tf_op jit(solution)/shard_map/all_to_all | solution.py:63
  12.1 0.7 slice_bitcast_fusion.7
  12.8 0.7 exponential_bitcast_fusion
  13.5 0.7 broadcast_compare_fusion.1
  14.3 1.4 fusion.18
  15.7 2.6 %all-to-all-done = f32[16,2,8,128]{3,2,1,0:T(8,128)S(1)} async-done(((f32[16,2,8,128]{3,2,1,0:T(8,128)}), f32[16,2,8,128]{3,2,1,0:T(8,128)S(1)}, u32[]{:S(2)}, u32[]{:S(2)}) %all-to-all-start) | async-done | bytes 131104 | tf_op jit(solution)/shard_map/all_to_all | solution.py:63
  18.4 0.7 broadcast_in_dim.60
  19.0 0.8 fusion.17
  19.9 15.0 %all-to-all-start.1 = ((f32[16,2,8,128]{3,2,1,0:T(8,128)}), f32[16,2,8,128]{3,2,1,0:T(8,128)}, u32[]{:S(2)}, u32[]{:S(2)}) async-start(f32[16,2,8,128]{3,2,1,0:T(8,128)} %broadcast_in_dim.60), calls=%async_computation.1 | async-start | bytes 262144 | tf_op jit(solution)/shard_map/all_to_all | solution.py:66
  34.9 1.9 broadcast_select_fusion.7
  36.8 1.3 broadcast_select_fusion.6
  38.1 28.1 %multiply_convert_fusion.1 = (bf16[3072,512]{1,0:T(8,128)(2,1)S(1)}, bf16[3072,512]{1,0:T(8,128)(2,1)S(1)}) fusion(f32[]{:T(128)} %bitcast.104, f32[512]{0:T(512)S(1)} %bitcast.120, f32[512]{0:T(512)S(1)} %bitcast.122, f32[3072]{0:T(1024)S(1)} %bitcast.118, f32[512]{0:T(512)S(1)} %bitcast.121, f32[3072]{0:T(1024)S(1)} %bitcast.117, f32[512]{0:T(512)S(1)} %bitcast.119, ...), kind=kLoop, calls=%fused_computation.2 | loop fusion | flops 22020096 | bytes 6349316 | tf_op jit(solution)/shard_map/convert_element_type | solution.py:40
  66.2 0.0 copy-start.1
  66.2 0.0 copy-start.2
  66.2 3.7 %pad_maximum_fusion = bf16[3072,1024]{1,0:T(8,128)(2,1)} fusion(bf16[3072,512]{1,0:T(8,128)(2,1)S(1)} %get-tuple-element.33, bf16[3072,512]{1,0:T(8,128)(2,1)S(1)} %get-tuple-element.32), kind=kLoop, calls=%fused_computation | loop fusion | flops 12582912 | bytes 12582912 | tf_op jit(solution)/shard_map/concatenate | solution.py:122
  69.9 0.0 all-to-all-done.1
  69.9 4.0 %all-to-all-start.2 = ((f32[16,2,8,128]{3,2,1,0:T(8,128)}), f32[16,2,8,128]{3,2,1,0:T(8,128)S(1)}, u32[]{:S(2)}, u32[]{:S(2)}) async-start(f32[16,2,8,128]{3,2,1,0:T(8,128)} %all-to-all-done.1), calls=%async_computation.2 | async-start | bytes 262144 | tf_op jit(solution)/shard_map/all_to_all | solution.py:63
  73.9 0.0 copy-done.1
  73.9 6.8 %all-to-all-done.2 = f32[16,2,8,128]{3,2,1,0:T(8,128)S(1)} async-done(((f32[16,2,8,128]{3,2,1,0:T(8,128)}), f32[16,2,8,128]{3,2,1,0:T(8,128)S(1)}, u32[]{:S(2)}, u32[]{:S(2)}) %all-to-all-start.2) | async-done | bytes 131104 | tf_op jit(solution)/shard_map/all_to_all | solution.py:63
  80.7 4.9 %collective-permute-start = (f32[2,128,128]{2,1,0:T(8,128)S(1)}, f32[2,128,128]{2,1,0:T(8,128)S(1)}, u32[]{:S(2)}, u32[]{:S(2)}) collective-permute-start(f32[2,128,128]{2,1,0:T(8,128)S(1)} %bitcast.113), channel_id=1, source_target_pairs={{0,16},{16,0},{1,17},{17,1},{2,18},{18,2},{3,19},{19,3},{4,20},{20... | collective-permute-start | bytes 393224 | tf_op jit(solution)/shard_map/ppermute | solution.py:81
  85.7 0.9 collective-permute-done
  86.7 0.6 convolution_bitcast_fusion.1
  87.2 0.7 copy.19
  87.9 3.5 %all-to-all-start.3 = ((f32[16,2,8,128]{3,2,1,0:T(8,128)}), f32[16,2,8,128]{3,2,1,0:T(8,128)S(1)}, u32[]{:S(2)}, u32[]{:S(2)}) async-start(f32[16,2,8,128]{3,2,1,0:T(8,128)} %copy.19), calls=%async_computation.3 | async-start | bytes 262144 | tf_op jit(solution)/shard_map/all_to_all | solution.py:63
  91.4 6.8 %all-to-all-done.3 = f32[16,2,8,128]{3,2,1,0:T(8,128)S(1)} async-done(((f32[16,2,8,128]{3,2,1,0:T(8,128)}), f32[16,2,8,128]{3,2,1,0:T(8,128)S(1)}, u32[]{:S(2)}, u32[]{:S(2)}) %all-to-all-start.3) | async-done | bytes 131104 | tf_op jit(solution)/shard_map/all_to_all | solution.py:63
  98.3 0.7 dynamic-slice_subtract_fusion
  99.0 23.6 %all_to_all.50 = f32[16,2,8,128]{3,2,1,0:T(8,128)} all-to-all(f32[16,2,8,128]{3,2,1,0:T(8,128)S(1)} %broadcast_in_dim.68), channel_id=1, replica_groups=mesh['z'=16,'core'=2,'col'=16] {'z'}, dimensions={0} | all-to-all | bytes 262144 | tf_op jit(solution)/shard_map/all_to_all | solution.py:66
  122.5 3.5 %all-to-all-start.5 = ((f32[16,2,8,128]{3,2,1,0:T(8,128)}), f32[16,2,8,128]{3,2,1,0:T(8,128)S(1)}, u32[]{:S(2)}, u32[]{:S(2)}) async-start(f32[16,2,8,128]{3,2,1,0:T(8,128)} %all_to_all.50), calls=%async_computation.5 | async-start | bytes 262144 | tf_op jit(solution)/shard_map/all_to_all | solution.py:63
  126.1 0.0 copy-done.2
  126.1 6.8 %all-to-all-done.5 = f32[16,2,8,128]{3,2,1,0:T(8,128)S(1)} async-done(((f32[16,2,8,128]{3,2,1,0:T(8,128)}), f32[16,2,8,128]{3,2,1,0:T(8,128)S(1)}, u32[]{:S(2)}, u32[]{:S(2)}) %all-to-all-start.5) | async-done | bytes 131104 | tf_op jit(solution)/shard_map/all_to_all | solution.py:63
  132.9 6.9 %collective-permute-start.1 = (f32[2,128,128]{2,1,0:T(8,128)S(1)}, f32[2,128,128]{2,1,0:T(8,128)S(1)}, u32[]{:S(2)}, u32[]{:S(2)}) collective-permute-start(f32[2,128,128]{2,1,0:T(8,128)S(1)} %bitcast.114), channel_id=1, source_target_pairs={{0,16},{16,0},{1,17},{17,1},{2,18},{18,2},{3,19},{19,3},{4,20},{20... | collective-permute-start | bytes 393224 | tf_op jit(solution)/shard_map/ppermute | solution.py:81
  139.9 0.9 collective-permute-done.1
  140.8 0.6 convolution_bitcast_fusion
  141.4 9.6 %all_to_all.51 = f32[16,2,8,128]{3,2,1,0:T(8,128)S(1)} all-to-all(f32[16,2,8,128]{3,2,1,0:T(8,128)S(1)} %copy.21), channel_id=1, replica_groups=mesh['z'=16,'core'=2,'col'=16] {'col'}, dimensions={0} | all-to-all | bytes 262144 | tf_op jit(solution)/shard_map/all_to_all | solution.py:63
  151.1 15.2 %all_to_all.52 = f32[16,2,8,128]{3,2,1,0:T(8,128)S(1)} all-to-all(f32[16,2,8,128]{3,2,1,0:T(8,128)S(1)} %broadcast_in_dim.69), channel_id=1, replica_groups=mesh['z'=16,'core'=2,'col'=16] {'z'}, dimensions={0} | all-to-all | bytes 262144 | tf_op jit(solution)/shard_map/all_to_all | solution.py:66
  166.3 10.0 %all_to_all.53 = f32[16,2,8,128]{3,2,1,0:T(8,128)S(1)} all-to-all(f32[16,2,8,128]{3,2,1,0:T(8,128)S(1)} %all_to_all.52), channel_id=1, replica_groups=mesh['z'=16,'core'=2,'col'=16] {'col'}, dimensions={0} | all-to-all | bytes 262144 | tf_op jit(solution)/shard_map/all_to_all | solution.py:63
  176.3 7.1 %collective-permute-start.2 = (f32[2,128,128]{2,1,0:T(8,128)S(1)}, f32[2,128,128]{2,1,0:T(8,128)S(1)}, u32[]{:S(2)}, u32[]{:S(2)}) collective-permute-start(f32[2,128,128]{2,1,0:T(8,128)S(1)} %bitcast.115), channel_id=1, source_target_pairs={{0,16},{16,0},{1,17},{17,1},{2,18},{18,2},{3,19},{19,3},{4,20},{20... | collective-permute-start | bytes 393224 | tf_op jit(solution)/shard_map/ppermute | solution.py:81
  183.4 1.0 collective-permute-done.2
  184.4 0.9 fusion.15
  185.4 4.7 %fusion.2 = f32[3072,256]{1,0:T(8,128)S(1)} fusion(bf16[3072,1024]{1,0:T(8,128)(2,1)} %pad_maximum_fusion, bf16[512,128]{1,0:T(8,128)(2,1)S(1)} %bitcast.116, bf16[512,128]{1,0:T(8,128)(2,1)S(1)} %bitcast_negate_fusion, bf16[512,128]{1,0:T(8,128)(2,1)S(1)} %bitcast.112), kind=kOutput, calls=%fused_computation.13 | convolution fusion | flops 1612709888 | bytes 9830400 | tf_op jit(solution)/shard_map/dot_general | solution.py:148
  190.1 41.6 %all_to_all.54 = f32[16,192,256]{2,1,0:T(8,128)S(1)} all-to-all(f32[16,192,256]{2,1,0:T(8,128)S(1)} %bitcast.106), channel_id=1, replica_groups=mesh['z'=16,'core'=2,'col'=16] {'col'}, dimensions={0} | all-to-all | bytes 6291456 | tf_op jit(solution)/shard_map/all_to_all | solution.py:153
  231.7 0.9 reduce_sum.39
  232.6 1.7 reshape.72
  (29 shorter events, 0.5 us)
Async XLA Ops:
  0.6 2.0 copy-start
  3.9 14.4 %all-to-all-start = ((f32[16,2,8,128]{3,2,1,0:T(8,128)}), f32[16,2,8,128]{3,2,1,0:T(8,128)S(1)}, u32[]{:S(2)}, u32[]{:S(2)}) async-start(f32[16,2,8,128]{3,2,1,0:T(8,128)} %copy.17), calls=%async_computation | async-start | bytes 262144 | tf_op jit(solution)/shard_map/all_to_all | solution.py:63
  19.9 50.0 %all-to-all-start.1 = ((f32[16,2,8,128]{3,2,1,0:T(8,128)}), f32[16,2,8,128]{3,2,1,0:T(8,128)}, u32[]{:S(2)}, u32[]{:S(2)}) async-start(f32[16,2,8,128]{3,2,1,0:T(8,128)} %broadcast_in_dim.60), calls=%async_computation.1 | async-start | bytes 262144 | tf_op jit(solution)/shard_map/all_to_all | solution.py:66
  66.2 7.7 %copy-start.1 = (f32[2,128,256]{2,1,0:T(8,128)S(1)}, f32[2,128,256]{2,1,0:T(8,128)}, u32[]{:S(2)}) copy-start(f32[2,128,256]{2,1,0:T(8,128)} %param.14) | copy-start | bytes 786436
  66.2 59.9 %copy-start.2 = (f32[2,128,256]{2,1,0:T(8,128)S(1)}, f32[2,128,256]{2,1,0:T(8,128)}, u32[]{:S(2)}) copy-start(f32[2,128,256]{2,1,0:T(8,128)} %param.13) | copy-start | bytes 786436
  69.9 10.8 %all-to-all-start.2 = ((f32[16,2,8,128]{3,2,1,0:T(8,128)}), f32[16,2,8,128]{3,2,1,0:T(8,128)S(1)}, u32[]{:S(2)}, u32[]{:S(2)}) async-start(f32[16,2,8,128]{3,2,1,0:T(8,128)} %all-to-all-done.1), calls=%async_computation.2 | async-start | bytes 262144 | tf_op jit(solution)/shard_map/all_to_all | solution.py:63
  80.7 5.9 %collective-permute-start = (f32[2,128,128]{2,1,0:T(8,128)S(1)}, f32[2,128,128]{2,1,0:T(8,128)S(1)}, u32[]{:S(2)}, u32[]{:S(2)}) collective-permute-start(f32[2,128,128]{2,1,0:T(8,128)S(1)} %bitcast.113), channel_id=1, source_target_pairs={{0,16},{16,0},{1,17},{17,1},{2,18},{18,2},{3,19},{19,3},{4,20},{20... | collective-permute-start | bytes 393224 | tf_op jit(solution)/shard_map/ppermute | solution.py:81
  87.9 10.3 %all-to-all-start.3 = ((f32[16,2,8,128]{3,2,1,0:T(8,128)}), f32[16,2,8,128]{3,2,1,0:T(8,128)S(1)}, u32[]{:S(2)}, u32[]{:S(2)}) async-start(f32[16,2,8,128]{3,2,1,0:T(8,128)} %copy.19), calls=%async_computation.3 | async-start | bytes 262144 | tf_op jit(solution)/shard_map/all_to_all | solution.py:63
  122.5 10.3 %all-to-all-start.5 = ((f32[16,2,8,128]{3,2,1,0:T(8,128)}), f32[16,2,8,128]{3,2,1,0:T(8,128)S(1)}, u32[]{:S(2)}, u32[]{:S(2)}) async-start(f32[16,2,8,128]{3,2,1,0:T(8,128)} %all_to_all.50), calls=%async_computation.5 | async-start | bytes 262144 | tf_op jit(solution)/shard_map/all_to_all | solution.py:63
  132.9 7.9 %collective-permute-start.1 = (f32[2,128,128]{2,1,0:T(8,128)S(1)}, f32[2,128,128]{2,1,0:T(8,128)S(1)}, u32[]{:S(2)}, u32[]{:S(2)}) collective-permute-start(f32[2,128,128]{2,1,0:T(8,128)S(1)} %bitcast.114), channel_id=1, source_target_pairs={{0,16},{16,0},{1,17},{17,1},{2,18},{18,2},{3,19},{19,3},{4,20},{20... | collective-permute-start | bytes 393224 | tf_op jit(solution)/shard_map/ppermute | solution.py:81
  176.3 8.1 %collective-permute-start.2 = (f32[2,128,128]{2,1,0:T(8,128)S(1)}, f32[2,128,128]{2,1,0:T(8,128)S(1)}, u32[]{:S(2)}, u32[]{:S(2)}) collective-permute-start(f32[2,128,128]{2,1,0:T(8,128)S(1)} %bitcast.115), channel_id=1, source_target_pairs={{0,16},{16,0},{1,17},{17,1},{2,18},{18,2},{3,19},{19,3},{4,20},{20... | collective-permute-start | bytes 393224 | tf_op jit(solution)/shard_map/ppermute | solution.py:81

commit v5 on v4

--- a/solution.py
+++ b/solution.py
@@ -119,33 +119,46 @@
             lid_table,
             wave_value,
         )
-        return jnp.concatenate([tile_real, tile_imag], axis=1)
+        return tile_real, tile_imag
 
     field_rows = field_xy.shape[1]
-    top_solved, tile_chunks = col_sum_to_columns(
-        complex_product(stacked_matrix(inv_top), rhs_top),
-        works=(None, ((field_xy, region_label), tile_chunk), None),
+    n_chunks = 3
+    chunk_rows = field_rows // n_chunks
+    works = [
+        (
+            (
+                field_xy[:, i * chunk_rows : (i + 1) * chunk_rows],
+                region_label[i * chunk_rows : (i + 1) * chunk_rows],
+            ),
+            tile_chunk,
+        )
+        for i in range(n_chunks)
+    ]
+    top_solved, tiles_a = col_sum_to_columns(
+        complex_product(stacked_matrix(inv_top), rhs_top), works=(None, works[0], None)
     )
-    remainder_cols, _ = col_sum_to_columns(
-        complex_product(stacked_matrix(lower_panel), top_solved), rhs_bottom
+    remainder_cols, tiles_b = col_sum_to_columns(
+        complex_product(stacked_matrix(lower_panel), top_solved),
+        rhs_bottom,
+        works=(None, works[1], None),
     )
-    bottom_solved, _ = col_sum_to_columns(
-        complex_product(stacked_matrix(inv_bottom), remainder_cols)
+    bottom_solved, tiles_c = col_sum_to_columns(
+        complex_product(stacked_matrix(inv_bottom), remainder_cols), works=(None, works[2], None)
     )
+    tile_chunks = tiles_a + tiles_b + tiles_c
     strengths = jnp.stack([top_solved, bottom_solved])
     weights = strengths.astype(jnp.bfloat16)
     right_count = weights.shape[3]
     src_real = weights[:, 0].reshape(-1, right_count)
     src_imag = weights[:, 1].reshape(-1, right_count)
-    stacked = jnp.concatenate(
+    for_real = jnp.concatenate([src_real, src_imag], axis=1)
+    for_imag = jnp.concatenate([-src_imag, src_real], axis=1)
+    result = jnp.concatenate(
         [
-            jnp.concatenate([src_real, src_imag], axis=1),
-            jnp.concatenate([-src_imag, src_real], axis=1),
+            jnp.dot(tile_real, for_real, preferred_element_type=jnp.float32)
+            + jnp.dot(tile_imag, for_imag, preferred_element_type=jnp.float32)
+            for tile_real, tile_imag in tile_chunks
         ],
-        axis=0,
-    )
-    result = jnp.concatenate(
-        [jnp.dot(tiles, stacked, preferred_element_type=jnp.float32) for tiles in tile_chunks],
         axis=0,
     )
     out_rows = field_rows // n_col

time: 235 us -> 223 us (0.949)
  blocking collectives: 100 us -> 61.4 us
  starting transfers between devices: 52.5 us -> 72.7 us
  waiting for transfers between devices: 25.8 us -> 31.5 us
    all_to_all x2 -> x0, blocking collectives: 38.8 us -> none  [z_step(): return lax.all_to_all(value, 'z', 0, 0, tiled=True)]
    all_to_all x1 -> x3, starting transfers between devices: 15 us -> 32.9 us  [z_step(): return lax.all_to_all(value, 'z', 0, 0, tiled=True)]
    concatenate x1, other arithmetic: 3.67 us -> 0.2 us  [per_device(): jnp.concatenate([jnp.dot(tile_real, for_real, preferred_element_type=jnp....]
    all_to_all x1 -> x3, waiting for transfers between devices: 0.01 us -> 3.21 us  [z_step(): return lax.all_to_all(value, 'z', 0, 0, tiled=True)]
    all_to_all x4, waiting for transfers between devices: 23 us -> 25.7 us  [col_step(): return lax.all_to_all(value, 'col', 0, 0, tiled=True)]
    ppermute x3, starting transfers between devices: 18.9 us -> 21.4 us  [col_sum_to_columns(): other = lax.ppermute(block, 'core', [(0, 1), (1, 0)])]
    select_n x1 -> x3, other arithmetic: 1.32 us -> 3.77 us  [green_tile(): lid_first = jnp.where(region == 1, lid_table[1, 0], lid_table[0, 0])]
    convert_element_type x1 -> x3, other arithmetic: 28.1 us -> 30.3 us  [green_tile(): (amplitude * jnp.sin(phase_angle)).astype(jnp.bfloat16)]
  transfers between devices with their start and end apart: 8 -> 10, of which waited for: 7 -> 10; matrix products, arithmetic and copies ran while one was open for 16% -> 15% of each run, Pallas kernels for 0% -> 0%
where the time goes in v5:
time: 223 us; the launch traced here: 221 us
  starting transfers between devices  72.7 us (33%)
  blocking collectives  61.4 us (28%)
  other arithmetic  41.8 us (19%)
  waiting for transfers between devices  31.5 us (14%)
  local copies, waits for them, and re-layouts  7.98 us (4%)
  matrix products  4.34 us (2%)
    all_to_all x1, blocking collectives, per_device(): summed = lax.all_to_all(split, 'col', 0, 0, tiled=True).sum(0)  41.6 us
    all_to_all x3, starting transfers between devices, z_step(): return lax.all_to_all(value, 'z', 0, 0, tiled=True)  32.9 us
    convert_element_type x3, other arithmetic, green_tile(): (amplitude * jnp.sin(phase_angle)).astype(jnp.bfloat16)  30.3 us
    all_to_all x4, waiting for transfers between devices, col_step(): return lax.all_to_all(value, 'col', 0, 0, tiled=True)  25.7 us
    ppermute x3, starting transfers between devices, col_sum_to_columns(): other = lax.ppermute(block, 'core', [(0, 1), (1, 0)])  21.4 us
    all_to_all x2, blocking collectives, col_step(): return lax.all_to_all(value, 'col', 0, 0, tiled=True)  19.7 us
    all_to_all x4, starting transfers between devices, col_step(): return lax.all_to_all(value, 'col', 0, 0, tiled=True)  18.4 us
  transfers between devices with their start and end apart: 10, of which 10 were waited for; matrix products, arithmetic and copies ran while one was open for 15% of the time, Pallas kernels for 0%

profile of v5, /device:TPU:1, one launch (start us, length us, event | category | flops | bytes accessed | tf_op | source)
XLA Modules:
  0.0 221.5 jit_solution(9893255185678502015)
XLA Ops:
  0.6 0.0 copy-start
  0.6 0.0 copy-start.9
  0.7 0.0 copy-start.8
  0.7 0.0 copy-start.7
  0.7 1.0 fusion.15
  1.7 1.0 slice_bitcast_fusion.4
  2.8 0.6 convolution_bitcast_fusion.2
  3.4 0.7 copy.17
  4.0 7.7 %all-to-all-start = ((f32[16,2,8,128]{3,2,1,0:T(8,128)}), f32[16,2,8,128]{3,2,1,0:T(8,128)S(1)}, u32[]{:S(2)}, u32[]{:S(2)}) async-start(f32[16,2,8,128]{3,2,1,0:T(8,128)} %copy.17), calls=%async_computation | async-start | bytes 262144 | tf_op jit(solution)/shard_map/all_to_all | solution.py:63
  12.4 0.0 copy-done.9
  12.6 0.0 copy-done.10
  12.6 0.6 fusion.26
  13.2 5.4 %all-to-all-done = f32[16,2,8,128]{3,2,1,0:T(8,128)S(1)} async-done(((f32[16,2,8,128]{3,2,1,0:T(8,128)}), f32[16,2,8,128]{3,2,1,0:T(8,128)S(1)}, u32[]{:S(2)}, u32[]{:S(2)}) %all-to-all-start) | async-done | bytes 131104 | tf_op jit(solution)/shard_map/all_to_all | solution.py:63
  18.6 0.7 broadcast_in_dim.102
  19.3 15.0 %all-to-all-start.1 = ((f32[16,2,8,128]{3,2,1,0:T(8,128)}), f32[16,2,8,128]{3,2,1,0:T(8,128)}, u32[]{:S(2)}, u32[]{:S(2)}) async-start(f32[16,2,8,128]{3,2,1,0:T(8,128)} %broadcast_in_dim.102), calls=%async_computation.1 | async-start | bytes 262144 | tf_op jit(solution)/shard_map/all_to_all | solution.py:66
  34.3 1.2 broadcast_select_fusion.11
  35.5 1.3 broadcast_select_fusion.8
  36.8 9.3 %multiply_convert_fusion.4 = (bf16[1024,512]{1,0:T(8,128)(2,1)S(1)}, bf16[1024,512]{1,0:T(8,128)(2,1)S(1)}) fusion(f32[]{:T(128)} %bitcast.114, f32[512]{0:T(512)S(1)} %bitcast.150, f32[512]{0:T(512)S(1)} %bitcast.144, f32[1024]{0:T(1024)S(1)} %bitcast.138, f32[512]{0:T(512)S(1)} %bitcast.141, f32[1024]{0:T(1024)S(1)} %bitcast.137, f32[512]{0:T(512)S(1)} %bitcast.147, ...), kind=kLoop, calls=%fused_computation.11 | loop fusion | flops 7340032 | bytes 2122244 | tf_op jit(solution)/shard_map/convert_element_type | solution.py:41
  46.1 0.2 all-to-all-done.1
  46.3 3.5 %all-to-all-start.2 = ((f32[16,2,8,128]{3,2,1,0:T(8,128)}), f32[16,2,8,128]{3,2,1,0:T(8,128)S(1)}, u32[]{:S(2)}, u32[]{:S(2)}) async-start(f32[16,2,8,128]{3,2,1,0:T(8,128)} %all-to-all-done.1), calls=%async_computation.2 | async-start | bytes 262144 | tf_op jit(solution)/shard_map/all_to_all | solution.py:63
  49.9 6.8 %all-to-all-done.2 = f32[16,2,8,128]{3,2,1,0:T(8,128)S(1)} async-done(((f32[16,2,8,128]{3,2,1,0:T(8,128)}), f32[16,2,8,128]{3,2,1,0:T(8,128)S(1)}, u32[]{:S(2)}, u32[]{:S(2)}) %all-to-all-start.2) | async-done | bytes 131104 | tf_op jit(solution)/shard_map/all_to_all | solution.py:63
  56.7 7.2 %collective-permute-start = (f32[2,128,128]{2,1,0:T(8,128)S(1)}, f32[2,128,128]{2,1,0:T(8,128)S(1)}, u32[]{:S(2)}, u32[]{:S(2)}) collective-permute-start(f32[2,128,128]{2,1,0:T(8,128)S(1)} %bitcast.132), channel_id=1, source_target_pairs={{0,16},{16,0},{1,17},{17,1},{2,18},{18,2},{3,19},{19,3},{4,20},{20... | collective-permute-start | bytes 393224 | tf_op jit(solution)/shard_map/ppermute | solution.py:81
  63.9 0.9 collective-permute-done
  64.9 0.6 convolution_bitcast_fusion.1
  65.5 0.7 copy.19
  66.1 3.6 %all-to-all-start.3 = ((f32[16,2,8,128]{3,2,1,0:T(8,128)}), f32[16,2,8,128]{3,2,1,0:T(8,128)S(1)}, u32[]{:S(2)}, u32[]{:S(2)}) async-start(f32[16,2,8,128]{3,2,1,0:T(8,128)} %copy.19), calls=%async_computation.3 | async-start | bytes 262144 | tf_op jit(solution)/shard_map/all_to_all | solution.py:63
  69.8 6.8 %all-to-all-done.3 = f32[16,2,8,128]{3,2,1,0:T(8,128)S(1)} async-done(((f32[16,2,8,128]{3,2,1,0:T(8,128)}), f32[16,2,8,128]{3,2,1,0:T(8,128)S(1)}, u32[]{:S(2)}, u32[]{:S(2)}) %all-to-all-start.3) | async-done | bytes 131104 | tf_op jit(solution)/shard_map/all_to_all | solution.py:63
  76.6 0.7 dynamic-slice_subtract_fusion
  77.3 0.7 broadcast_in_dim.110
  78.0 1.2 broadcast_select_fusion.10
  79.2 1.3 broadcast_select_fusion.7
  80.5 9.8 %all-to-all-start.4 = ((f32[16,2,8,128]{3,2,1,0:T(8,128)}), f32[16,2,8,128]{3,2,1,0:T(8,128)}, u32[]{:S(2)}, u32[]{:S(2)}) async-start(f32[16,2,8,128]{3,2,1,0:T(8,128)} %broadcast_in_dim.110), calls=%async_computation.4 | async-start | bytes 262144 | tf_op jit(solution)/shard_map/all_to_all | solution.py:66
  90.3 10.5 %multiply_convert_fusion.2 = (bf16[1024,512]{1,0:T(8,128)(2,1)}, bf16[1024,512]{1,0:T(8,128)(2,1)}) fusion(f32[1024]{0:T(1024)S(1)} %bitcast.140, f32[1024]{0:T(1024)S(1)} %bitcast.139, f32[]{:T(128)} %bitcast.115, f32[512]{0:T(512)S(1)} %bitcast.151, f32[512]{0:T(512)S(1)} %bitcast.145, f32[512]{0:T(512)S(1)} %bitcast.142, f32[512]{0:T(512)S(1)} %bitcast.148, ...), kind=kLoop, calls=%fused_computation.6 | loop fusion | flops 7340032 | bytes 2122244 | tf_op jit(solution)/shard_map/convert_element_type | solution.py:41
  100.8 1.5 all-to-all-done.4
  102.3 3.5 %all-to-all-start.5 = ((f32[16,2,8,128]{3,2,1,0:T(8,128)}), f32[16,2,8,128]{3,2,1,0:T(8,128)S(1)}, u32[]{:S(2)}, u32[]{:S(2)}) async-start(f32[16,2,8,128]{3,2,1,0:T(8,128)} %all-to-all-done.4), calls=%async_computation.5 | async-start | bytes 262144 | tf_op jit(solution)/shard_map/all_to_all | solution.py:63
  105.8 0.0 copy-done.6
  105.9 6.8 %all-to-all-done.5 = f32[16,2,8,128]{3,2,1,0:T(8,128)S(1)} async-done(((f32[16,2,8,128]{3,2,1,0:T(8,128)}), f32[16,2,8,128]{3,2,1,0:T(8,128)S(1)}, u32[]{:S(2)}, u32[]{:S(2)}) %all-to-all-start.5) | async-done | bytes 131104 | tf_op jit(solution)/shard_map/all_to_all | solution.py:63
  112.6 6.9 %collective-permute-start.1 = (f32[2,128,128]{2,1,0:T(8,128)S(1)}, f32[2,128,128]{2,1,0:T(8,128)S(1)}, u32[]{:S(2)}, u32[]{:S(2)}) collective-permute-start(f32[2,128,128]{2,1,0:T(8,128)S(1)} %bitcast.133), channel_id=1, source_target_pairs={{0,16},{16,0},{1,17},{17,1},{2,18},{18,2},{3,19},{19,3},{4,20},{20... | collective-permute-start | bytes 393224 | tf_op jit(solution)/shard_map/ppermute | solution.py:81
  119.7 0.9 collective-permute-done.1
  120.6 0.6 convolution_bitcast_fusion
  121.2 9.6 %all_to_all.50 = f32[16,2,8,128]{3,2,1,0:T(8,128)S(1)} all-to-all(f32[16,2,8,128]{3,2,1,0:T(8,128)S(1)} %copy.21), channel_id=1, replica_groups=mesh['z'=16,'core'=2,'col'=16] {'col'}, dimensions={0} | all-to-all | bytes 262144 | tf_op jit(solution)/shard_map/all_to_all | solution.py:63
  130.9 0.7 broadcast_in_dim.113
  131.5 1.2 broadcast_select_fusion.9
  132.7 1.3 broadcast_select_fusion.6
  134.0 8.1 %all-to-all-start.7 = ((f32[16,2,8,128]{3,2,1,0:T(8,128)}), f32[16,2,8,128]{3,2,1,0:T(8,128)S(1)}, u32[]{:S(2)}, u32[]{:S(2)}) async-start(f32[16,2,8,128]{3,2,1,0:T(8,128)} %broadcast_in_dim.113), calls=%async_computation.7 | async-start | bytes 262144 | tf_op jit(solution)/shard_map/all_to_all | solution.py:66
  142.1 10.5 %multiply_convert_fusion = (bf16[1024,512]{1,0:T(8,128)(2,1)}, bf16[1024,512]{1,0:T(8,128)(2,1)}) fusion(f32[1024]{0:T(1024)S(1)} %bitcast.136, f32[1024]{0:T(1024)S(1)} %bitcast.135, f32[]{:T(128)} %bitcast.113, f32[512]{0:T(512)S(1)} %bitcast.152, f32[512]{0:T(512)S(1)} %bitcast.146, f32[512]{0:T(512)S(1)} %bitcast.143, f32[512]{0:T(512)S(1)} %bitcast.149, ...), kind=kLoop, calls=%fused_computation.1 | loop fusion | flops 7340032 | bytes 2122244 | tf_op jit(solution)/shard_map/convert_element_type | solution.py:41
  152.6 1.5 all-to-all-done.7
  154.1 10.1 %all_to_all.51 = f32[16,2,8,128]{3,2,1,0:T(8,128)S(1)} all-to-all(f32[16,2,8,128]{3,2,1,0:T(8,128)S(1)} %all-to-all-done.7), channel_id=1, replica_groups=mesh['z'=16,'core'=2,'col'=16] {'col'}, dimensions={0} | all-to-all | bytes 262144 | tf_op jit(solution)/shard_map/all_to_all | solution.py:63
  164.2 7.3 %collective-permute-start.2 = (f32[2,128,128]{2,1,0:T(8,128)S(1)}, f32[2,128,128]{2,1,0:T(8,128)S(1)}, u32[]{:S(2)}, u32[]{:S(2)}) collective-permute-start(f32[2,128,128]{2,1,0:T(8,128)S(1)} %bitcast.134), channel_id=1, source_target_pairs={{0,16},{16,0},{1,17},{17,1},{2,18},{18,2},{3,19},{19,3},{4,20},{20... | collective-permute-start | bytes 393224 | tf_op jit(solution)/shard_map/ppermute | solution.py:81
  171.5 0.8 collective-permute-done.2
  172.3 0.9 fusion.19
  173.3 0.4 fusion.6
  173.7 0.0 copy-done.2
  173.7 0.4 fusion.7
  174.2 0.4 fusion.8
  174.6 0.3 copy-done.1
  175.0 0.4 convolution_add_fusion.1
  175.4 0.8 copy-done.3
  176.2 0.4 convolution_add_fusion
  176.6 0.4 convolution_add_fusion.2
  177.1 0.2 pad_maximum_fusion
  177.3 41.6 %all_to_all.52 = f32[16,192,256]{2,1,0:T(8,128)S(1)} all-to-all(f32[16,192,256]{2,1,0:T(8,128)S(1)} %bitcast.117), channel_id=1, replica_groups=mesh['z'=16,'core'=2,'col'=16] {'col'}, dimensions={0} | all-to-all | bytes 6291456 | tf_op jit(solution)/shard_map/all_to_all | solution.py:166
  218.9 0.9 reduce_sum.39
  219.8 1.7 reshape.80
  (51 shorter events, 0.6 us)
Async XLA Ops:
  0.6 2.1 copy-start
  0.6 11.8 %copy-start.9 = (f32[2,2,256]{2,1,0:T(2,128)S(1)}, f32[2,2,256]{2,1,0:T(2,128)}, u32[]{:S(2)}) copy-start(f32[2,2,256]{2,1,0:T(2,128)} %param.17) | copy-start | bytes 12292
  0.7 11.8 %copy-start.8 = (s32[3072]{0:T(1024)S(1)}, s32[3072]{0:T(1024)}, u32[]{:S(2)}) copy-start(s32[3072]{0:T(1024)} %param.21) | copy-start | bytes 36868
  0.7 11.8 %copy-start.7 = (f32[2,3072]{1,0:T(2,128)S(1)}, f32[2,3072]{1,0:T(2,128)}, u32[]{:S(2)}) copy-start(f32[2,3072]{1,0:T(2,128)} %param.20) | copy-start | bytes 73732
  0.7 11.8 %copy-start.12 = (f32[2,256]{1,0:T(2,128)S(1)}, f32[2,256]{1,0:T(2,128)}, u32[]{:S(2)}) copy-start(f32[2,256]{1,0:T(2,128)} %param.18) | copy-start | bytes 6148
  0.7 11.8 %copy-start.11 = (s32[2,256]{1,0:T(2,128)S(1)}, s32[2,256]{1,0:T(2,128)}, u32[]{:S(2)}) copy-start(s32[2,256]{1,0:T(2,128)} %param.19) | copy-start | bytes 6148
  0.7 11.9 %copy-start.10 = (f32[2,2]{1,0:T(2,128)S(1)}, f32[2,2]{1,0:T(2,128)}, u32[]{:S(2)}) copy-start(f32[2,2]{1,0:T(2,128)} %param.22) | copy-start | bytes 52
  4.0 45.8 %copy-start.5 = (f32[2,128,256]{2,1,0:T(8,128)S(1)}, f32[2,128,256]{2,1,0:T(8,128)}, u32[]{:S(2)}) copy-start(f32[2,128,256]{2,1,0:T(8,128)} %param.14) | copy-start | bytes 786436
  4.0 14.6 %all-to-all-start = ((f32[16,2,8,128]{3,2,1,0:T(8,128)}), f32[16,2,8,128]{3,2,1,0:T(8,128)S(1)}, u32[]{:S(2)}, u32[]{:S(2)}) async-start(f32[16,2,8,128]{3,2,1,0:T(8,128)} %copy.17), calls=%async_computation | async-start | bytes 262144 | tf_op jit(solution)/shard_map/all_to_all | solution.py:63
  19.3 27.0 %all-to-all-start.1 = ((f32[16,2,8,128]{3,2,1,0:T(8,128)}), f32[16,2,8,128]{3,2,1,0:T(8,128)}, u32[]{:S(2)}, u32[]{:S(2)}) async-start(f32[16,2,8,128]{3,2,1,0:T(8,128)} %broadcast_in_dim.102), calls=%async_computation.1 | async-start | bytes 262144 | tf_op jit(solution)/shard_map/all_to_all | solution.py:66
  46.3 10.3 %all-to-all-start.2 = ((f32[16,2,8,128]{3,2,1,0:T(8,128)}), f32[16,2,8,128]{3,2,1,0:T(8,128)S(1)}, u32[]{:S(2)}, u32[]{:S(2)}) async-start(f32[16,2,8,128]{3,2,1,0:T(8,128)} %all-to-all-done.1), calls=%async_computation.2 | async-start | bytes 262144 | tf_op jit(solution)/shard_map/all_to_all | solution.py:63
  56.7 8.2 %collective-permute-start = (f32[2,128,128]{2,1,0:T(8,128)S(1)}, f32[2,128,128]{2,1,0:T(8,128)S(1)}, u32[]{:S(2)}, u32[]{:S(2)}) collective-permute-start(f32[2,128,128]{2,1,0:T(8,128)S(1)} %bitcast.132), channel_id=1, source_target_pairs={{0,16},{16,0},{1,17},{17,1},{2,18},{18,2},{3,19},{19,3},{4,20},{20... | collective-permute-start | bytes 393224 | tf_op jit(solution)/shard_map/ppermute | solution.py:81
  66.1 39.7 %copy-start.6 = (f32[2,128,256]{2,1,0:T(8,128)S(1)}, f32[2,128,256]{2,1,0:T(8,128)}, u32[]{:S(2)}) copy-start(f32[2,128,256]{2,1,0:T(8,128)} %param.13) | copy-start | bytes 786436
  66.1 10.5 %all-to-all-start.3 = ((f32[16,2,8,128]{3,2,1,0:T(8,128)}), f32[16,2,8,128]{3,2,1,0:T(8,128)S(1)}, u32[]{:S(2)}, u32[]{:S(2)}) async-start(f32[16,2,8,128]{3,2,1,0:T(8,128)} %copy.19), calls=%async_computation.3 | async-start | bytes 262144 | tf_op jit(solution)/shard_map/all_to_all | solution.py:63
  80.5 21.8 %all-to-all-start.4 = ((f32[16,2,8,128]{3,2,1,0:T(8,128)}), f32[16,2,8,128]{3,2,1,0:T(8,128)}, u32[]{:S(2)}, u32[]{:S(2)}) async-start(f32[16,2,8,128]{3,2,1,0:T(8,128)} %broadcast_in_dim.110), calls=%async_computation.4 | async-start | bytes 262144 | tf_op jit(solution)/shard_map/all_to_all | solution.py:66
  102.3 10.3 %all-to-all-start.5 = ((f32[16,2,8,128]{3,2,1,0:T(8,128)}), f32[16,2,8,128]{3,2,1,0:T(8,128)S(1)}, u32[]{:S(2)}, u32[]{:S(2)}) async-start(f32[16,2,8,128]{3,2,1,0:T(8,128)} %all-to-all-done.4), calls=%async_computation.5 | async-start | bytes 262144 | tf_op jit(solution)/shard_map/all_to_all | solution.py:63
  112.6 7.9 %collective-permute-start.1 = (f32[2,128,128]{2,1,0:T(8,128)S(1)}, f32[2,128,128]{2,1,0:T(8,128)S(1)}, u32[]{:S(2)}, u32[]{:S(2)}) collective-permute-start(f32[2,128,128]{2,1,0:T(8,128)S(1)} %bitcast.133), channel_id=1, source_target_pairs={{0,16},{16,0},{1,17},{17,1},{2,18},{18,2},{3,19},{19,3},{4,20},{20... | collective-permute-start | bytes 393224 | tf_op jit(solution)/shard_map/ppermute | solution.py:81
  134.0 20.1 %all-to-all-start.7 = ((f32[16,2,8,128]{3,2,1,0:T(8,128)}), f32[16,2,8,128]{3,2,1,0:T(8,128)S(1)}, u32[]{:S(2)}, u32[]{:S(2)}) async-start(f32[16,2,8,128]{3,2,1,0:T(8,128)} %broadcast_in_dim.113), calls=%async_computation.7 | async-start | bytes 262144 | tf_op jit(solution)/shard_map/all_to_all | solution.py:66
  154.1 19.2 %copy-start.4 = (bf16[1024,512]{1,0:T(8,128)(2,1)S(1)}, bf16[1024,512]{1,0:T(8,128)(2,1)}, u32[]{:S(2)}) copy-start(bf16[1024,512]{1,0:T(8,128)(2,1)} %get-tuple-element.36) | copy-start | bytes 3145732
  164.2 8.1 %collective-permute-start.2 = (f32[2,128,128]{2,1,0:T(8,128)S(1)}, f32[2,128,128]{2,1,0:T(8,128)S(1)}, u32[]{:S(2)}, u32[]{:S(2)}) collective-permute-start(f32[2,128,128]{2,1,0:T(8,128)S(1)} %bitcast.134), channel_id=1, source_target_pairs={{0,16},{16,0},{1,17},{17,1},{2,18},{18,2},{3,19},{19,3},{4,20},{20... | collective-permute-start | bytes 393224 | tf_op jit(solution)/shard_map/ppermute | solution.py:81
  172.3 1.4 copy-start.2
  173.7 1.2 copy-start.1
  175.0 1.2 copy-start.3

commit v6 on v5

--- a/solution.py
+++ b/solution.py
@@ -25,16 +25,12 @@
     return product.reshape(parts, stacked.shape[0] // parts, right)
 
 
-def green_tile(
-    point_x, point_y, region, source_x, source_y, src_depth, src_label, lid_table, wave_value
-):
+def green_tile(point_x, point_y, lid_first, lid_second, source_x, source_y, depth_sq, depth_term, src_label, wave_value):
     delta_x = point_x[:, None] - source_x[None, :]
     delta_y = point_y[:, None] - source_y[None, :]
-    distance = jnp.sqrt(delta_x * delta_x + delta_y * delta_y + (src_depth * src_depth)[None, :])
-    lid_first = jnp.where(region == 1, lid_table[1, 0], lid_table[0, 0])
-    lid_second = jnp.where(region == 1, lid_table[1, 1], lid_table[0, 1])
+    distance = jnp.sqrt(delta_x * delta_x + delta_y * delta_y + depth_sq[None, :])
     factor = jnp.where(src_label[None, :] == 1, lid_second[:, None], lid_first[:, None])
-    amplitude = factor * jnp.exp(wave_value * src_depth)[None, :] / distance
+    amplitude = factor * depth_term[None, :] / distance
     phase_angle = wave_value * distance
     return (
         (amplitude * jnp.cos(phase_angle)).astype(jnp.bfloat16),
@@ -107,43 +103,50 @@
     src_label = body_label.reshape(-1)
     wave_value = wave_number[0]
 
-    def tile_chunk(point_xy, region):
-        tile_real, tile_imag = green_tile(
+    depth_sq = src_depth * src_depth
+    depth_term = jnp.exp(wave_value * src_depth)
+    lid_first = jnp.where(region_label == 1, lid_table[1, 0], lid_table[0, 0])
+    lid_second = jnp.where(region_label == 1, lid_table[1, 1], lid_table[0, 1])
+
+    def tile_chunk(point_xy, first, second):
+        return green_tile(
             point_xy[0],
             point_xy[1],
-            region,
+            first,
+            second,
             source_x,
             source_y,
-            src_depth,
+            depth_sq,
+            depth_term,
             src_label,
-            lid_table,
             wave_value,
         )
-        return tile_real, tile_imag
 
     field_rows = field_xy.shape[1]
-    n_chunks = 3
+    n_chunks = 6
     chunk_rows = field_rows // n_chunks
     works = [
         (
             (
                 field_xy[:, i * chunk_rows : (i + 1) * chunk_rows],
-                region_label[i * chunk_rows : (i + 1) * chunk_rows],
+                lid_first[i * chunk_rows : (i + 1) * chunk_rows],
+                lid_second[i * chunk_rows : (i + 1) * chunk_rows],
             ),
             tile_chunk,
         )
         for i in range(n_chunks)
     ]
     top_solved, tiles_a = col_sum_to_columns(
-        complex_product(stacked_matrix(inv_top), rhs_top), works=(None, works[0], None)
+        complex_product(stacked_matrix(inv_top), rhs_top), works=(works[0], None, works[1])
     )
     remainder_cols, tiles_b = col_sum_to_columns(
         complex_product(stacked_matrix(lower_panel), top_solved),
         rhs_bottom,
-        works=(None, works[1], None),
+        works=(works[2], None, works[3]),
     )
     bottom_solved, tiles_c = col_sum_to_columns(
-        complex_product(stacked_matrix(inv_bottom), remainder_cols), works=(None, works[2], None)
+        complex_product(stacked_matrix(inv_bottom), remainder_cols),
+        works=(works[4], None, works[5]),
     )
     tile_chunks = tiles_a + tiles_b + tiles_c
     strengths = jnp.stack([top_solved, bottom_solved])

time: 223 us -> 223 us (level)
  blocking collectives: 61.4 us -> 58.9 us
    all_to_all x3 -> x2, waiting for transfers between devices: 3.21 us -> 23.9 us  [z_step(): return lax.all_to_all(value, 'z', 0, 0, tiled=True)]
    all_to_all x4 -> x6, waiting for transfers between devices: 25.7 us -> 6.91 us  [col_step(): return lax.all_to_all(value, 'col', 0, 0, tiled=True)]
    all_to_all x4 -> x6, starting transfers between devices: 18.4 us -> 33.4 us  [col_step(): return lax.all_to_all(value, 'col', 0, 0, tiled=True)]
    all_to_all x3 -> x2, starting transfers between devices: 32.9 us -> 19.2 us  [z_step(): return lax.all_to_all(value, 'z', 0, 0, tiled=True)]
    select_n x6 -> x2, other arithmetic: 7.37 us -> 3.18 us  [the longest x1 1.89 us: per_device(): lid_second = jnp.where(region_label == 1, lid_table[1, 1], lid_table[0, 1])]
    all_to_all x2 -> x1, blocking collectives: 19.7 us -> 15.7 us  [z_step(): return lax.all_to_all(value, 'z', 0, 0, tiled=True)]
    convert_element_type x3 -> x6, other arithmetic: 30.3 us -> 33.3 us  [green_tile(): (amplitude * jnp.sin(phase_angle)).astype(jnp.bfloat16)]
  transfers between devices with their start and end apart: 10 -> 11, of which waited for: 10 -> 11; matrix products, arithmetic and copies ran while one was open for 15% -> 15% of each run, Pallas kernels for 0% -> 0%
where the time goes in v6:
time: 223 us; the launch traced here: 222 us
  starting transfers between devices  73.7 us (33%)
  blocking collectives  58.9 us (26%)
  other arithmetic  40.3 us (18%)
  waiting for transfers between devices  33.6 us (15%)
  local copies, waits for them, and re-layouts  8.61 us (4%)
  matrix products  5.29 us (2%)
    all_to_all x1, blocking collectives, per_device(): summed = lax.all_to_all(split, 'col', 0, 0, tiled=True).sum(0)  43.2 us
    all_to_all x6, starting transfers between devices, col_step(): return lax.all_to_all(value, 'col', 0, 0, tiled=True)  33.4 us
    convert_element_type x6, other arithmetic, green_tile(): (amplitude * jnp.sin(phase_angle)).astype(jnp.bfloat16)  33.3 us
    all_to_all x2, waiting for transfers between devices, z_step(): return lax.all_to_all(value, 'z', 0, 0, tiled=True)  23.9 us
    ppermute x3, starting transfers between devices, col_sum_to_columns(): other = lax.ppermute(block, 'core', [(0, 1), (1, 0)])  21.2 us
    all_to_all x2, starting transfers between devices, z_step(): return lax.all_to_all(value, 'z', 0, 0, tiled=True)  19.2 us
    all_to_all x1, blocking collectives, z_step(): return lax.all_to_all(value, 'z', 0, 0, tiled=True)  15.7 us
    all_to_all x6, waiting for transfers between devices, col_step(): return lax.all_to_all(value, 'col', 0, 0, tiled=True)  6.91 us
  transfers between devices with their start and end apart: 11, of which 11 were waited for; matrix products, arithmetic and copies ran while one was open for 15% of the time, Pallas kernels for 0%

profile of v6, /device:TPU:1, one launch (start us, length us, event | category | flops | bytes accessed | tf_op | source)
XLA Modules:
  0.0 222.3 jit_solution(10267748258862374301)
XLA Ops:
  0.6 0.0 copy-start
  0.6 0.0 copy-start.11
  0.7 0.0 copy-start.10
  0.7 1.0 fusion.18
  1.7 1.0 slice_bitcast_fusion.4
  2.6 1.5 fusion.39
  4.1 0.8 fusion.30
  4.9 1.9 broadcast_select_fusion.6
  6.8 1.3 broadcast_select_fusion.7
  8.2 0.6 convolution_bitcast_fusion.2
  8.8 0.7 copy.17
  9.4 7.6 %all-to-all-start = ((f32[16,2,8,128]{3,2,1,0:T(8,128)}), f32[16,2,8,128]{3,2,1,0:T(8,128)S(1)}, u32[]{:S(2)}, u32[]{:S(2)}) async-start(f32[16,2,8,128]{3,2,1,0:T(8,128)} %copy.17), calls=%async_computation | async-start | bytes 262144 | tf_op jit(solution)/shard_map/all_to_all | solution.py:59
  17.8 5.5 %multiply_convert_fusion.10 = (bf16[512,512]{1,0:T(8,128)(2,1)S(1)}, bf16[512,512]{1,0:T(8,128)(2,1)}) fusion(f32[]{:T(128)} %bitcast.126, f32[512]{0:T(512)S(1)} %bitcast.177, f32[512]{0:T(512)S(1)} %bitcast.165, f32[512]{0:T(512)S(1)} %bitcast.194, f32[512]{0:T(512)S(1)} %bitcast.159, f32[512]{0:T(512)S(1)} %bitcast.193, f32[512]{0:T(512)S(1)} %bitcast.171, ...), kind=kLoop, calls=%fused_computation.40 | loop fusion | flops 3670016 | bytes 1065476 | tf_op jit(solution)/shard_map/convert_element_type | solution.py:37
  23.3 0.5 all-to-all-done
  23.9 0.7 broadcast_in_dim.152
  24.5 15.0 %all-to-all-start.1 = ((f32[16,2,8,128]{3,2,1,0:T(8,128)}), f32[16,2,8,128]{3,2,1,0:T(8,128)}, u32[]{:S(2)}, u32[]{:S(2)}) async-start(f32[16,2,8,128]{3,2,1,0:T(8,128)} %broadcast_in_dim.152), calls=%async_computation.1 | async-start | bytes 262144 | tf_op jit(solution)/shard_map/all_to_all | solution.py:62
  39.6 12.0 %all-to-all-done.1 = f32[16,2,8,128]{3,2,1,0:T(8,128)} async-done(((f32[16,2,8,128]{3,2,1,0:T(8,128)}), f32[16,2,8,128]{3,2,1,0:T(8,128)}, u32[]{:S(2)}, u32[]{:S(2)}) %all-to-all-start.1) | async-done | bytes 131104 | tf_op jit(solution)/shard_map/all_to_all | solution.py:62
  51.6 6.1 %all-to-all-start.2 = ((f32[16,2,8,128]{3,2,1,0:T(8,128)}), f32[16,2,8,128]{3,2,1,0:T(8,128)S(1)}, u32[]{:S(2)}, u32[]{:S(2)}) async-start(f32[16,2,8,128]{3,2,1,0:T(8,128)} %all-to-all-done.1), calls=%async_computation.2 | async-start | bytes 262144 | tf_op jit(solution)/shard_map/all_to_all | solution.py:59
  57.7 5.5 %multiply_convert_fusion.8 = (bf16[512,512]{1,0:T(8,128)(2,1)S(1)}, bf16[512,512]{1,0:T(8,128)(2,1)}) fusion(f32[512]{0:T(512)S(1)} %bitcast.186, f32[512]{0:T(512)S(1)} %bitcast.185, f32[]{:T(128)} %bitcast.127, f32[512]{0:T(512)S(1)} %bitcast.178, f32[512]{0:T(512)S(1)} %bitcast.166, f32[512]{0:T(512)S(1)} %bitcast.160, f32[512]{0:T(512)S(1)} %bitcast.172, ...), kind=kLoop, calls=%fused_computation.35 | loop fusion | flops 3670016 | bytes 1065476 | tf_op jit(solution)/shard_map/convert_element_type | solution.py:37
  63.2 1.3 all-to-all-done.2
  64.6 7.3 %collective-permute-start = (f32[2,128,128]{2,1,0:T(8,128)S(1)}, f32[2,128,128]{2,1,0:T(8,128)S(1)}, u32[]{:S(2)}, u32[]{:S(2)}) collective-permute-start(f32[2,128,128]{2,1,0:T(8,128)S(1)} %bitcast.156), channel_id=1, source_target_pairs={{0,16},{16,0},{1,17},{17,1},{2,18},{18,2},{3,19},{19,3},{4,20},{20... | collective-permute-start | bytes 393224 | tf_op jit(solution)/shard_map/ppermute | solution.py:77
  71.9 0.9 collective-permute-done
  72.8 0.6 convolution_bitcast_fusion.1
  73.4 0.7 copy.19
  74.1 4.5 %all-to-all-start.3 = ((f32[16,2,8,128]{3,2,1,0:T(8,128)}), f32[16,2,8,128]{3,2,1,0:T(8,128)S(1)}, u32[]{:S(2)}, u32[]{:S(2)}) async-start(f32[16,2,8,128]{3,2,1,0:T(8,128)} %copy.19), calls=%async_computation.3 | async-start | bytes 262144 | tf_op jit(solution)/shard_map/all_to_all | solution.py:59
  78.6 5.5 %multiply_convert_fusion.6 = (bf16[512,512]{1,0:T(8,128)(2,1)S(1)}, bf16[512,512]{1,0:T(8,128)(2,1)}) fusion(f32[512]{0:T(512)S(1)} %bitcast.188, f32[512]{0:T(512)S(1)} %bitcast.187, f32[]{:T(128)} %bitcast.128, f32[512]{0:T(512)S(1)} %bitcast.179, f32[512]{0:T(512)S(1)} %bitcast.167, f32[512]{0:T(512)S(1)} %bitcast.161, f32[512]{0:T(512)S(1)} %bitcast.173, ...), kind=kLoop, calls=%fused_computation.30 | loop fusion | flops 3670016 | bytes 1065476 | tf_op jit(solution)/shard_map/convert_element_type | solution.py:37
  84.1 1.3 all-to-all-done.3
  85.5 0.7 dynamic-slice_subtract_fusion
  86.2 0.7 broadcast_in_dim.157
  86.8 4.2 %all-to-all-start.4 = ((f32[16,2,8,128]{3,2,1,0:T(8,128)}), f32[16,2,8,128]{3,2,1,0:T(8,128)}, u32[]{:S(2)}, u32[]{:S(2)}) async-start(f32[16,2,8,128]{3,2,1,0:T(8,128)} %broadcast_in_dim.157), calls=%async_computation.4 | async-start | bytes 262144 | tf_op jit(solution)/shard_map/all_to_all | solution.py:62
  91.1 11.9 %all-to-all-done.4 = f32[16,2,8,128]{3,2,1,0:T(8,128)} async-done(((f32[16,2,8,128]{3,2,1,0:T(8,128)}), f32[16,2,8,128]{3,2,1,0:T(8,128)}, u32[]{:S(2)}, u32[]{:S(2)}) %all-to-all-start.4) | async-done | bytes 131104 | tf_op jit(solution)/shard_map/all_to_all | solution.py:62
  103.0 5.3 %all-to-all-start.5 = ((f32[16,2,8,128]{3,2,1,0:T(8,128)}), f32[16,2,8,128]{3,2,1,0:T(8,128)S(1)}, u32[]{:S(2)}, u32[]{:S(2)}) async-start(f32[16,2,8,128]{3,2,1,0:T(8,128)} %all-to-all-done.4), calls=%async_computation.5 | async-start | bytes 262144 | tf_op jit(solution)/shard_map/all_to_all | solution.py:59
  108.3 5.6 %multiply_convert_fusion.4 = (bf16[512,512]{1,0:T(8,128)(2,1)S(1)}, bf16[512,512]{1,0:T(8,128)(2,1)}) fusion(f32[512]{0:T(512)S(1)} %bitcast.190, f32[512]{0:T(512)S(1)} %bitcast.189, f32[]{:T(128)} %bitcast.129, f32[512]{0:T(512)S(1)} %bitcast.180, f32[512]{0:T(512)S(1)} %bitcast.168, f32[512]{0:T(512)S(1)} %bitcast.162, f32[512]{0:T(512)S(1)} %bitcast.174, ...), kind=kLoop, calls=%fused_computation.25 | loop fusion | flops 3670016 | bytes 1065476 | tf_op jit(solution)/shard_map/convert_element_type | solution.py:37
  113.9 1.3 all-to-all-done.5
  115.2 6.8 %collective-permute-start.1 = (f32[2,128,128]{2,1,0:T(8,128)S(1)}, f32[2,128,128]{2,1,0:T(8,128)S(1)}, u32[]{:S(2)}, u32[]{:S(2)}) collective-permute-start(f32[2,128,128]{2,1,0:T(8,128)S(1)} %bitcast.157), channel_id=1, source_target_pairs={{0,16},{16,0},{1,17},{17,1},{2,18},{18,2},{3,19},{19,3},{4,20},{20... | collective-permute-start | bytes 393224 | tf_op jit(solution)/shard_map/ppermute | solution.py:77
  122.1 0.9 collective-permute-done.1
  123.0 0.6 convolution_bitcast_fusion
  123.6 0.7 copy.21
  124.3 4.5 %all-to-all-start.6 = ((f32[16,2,8,128]{3,2,1,0:T(8,128)}), f32[16,2,8,128]{3,2,1,0:T(8,128)S(1)}, u32[]{:S(2)}, u32[]{:S(2)}) async-start(f32[16,2,8,128]{3,2,1,0:T(8,128)} %copy.21), calls=%async_computation.6 | async-start | bytes 262144 | tf_op jit(solution)/shard_map/all_to_all | solution.py:59
  128.8 5.5 %multiply_convert_fusion.2 = (bf16[512,512]{1,0:T(8,128)(2,1)S(1)}, bf16[512,512]{1,0:T(8,128)(2,1)}) fusion(f32[512]{0:T(512)S(1)} %bitcast.192, f32[512]{0:T(512)S(1)} %bitcast.191, f32[]{:T(128)} %bitcast.130, f32[512]{0:T(512)S(1)} %bitcast.181, f32[512]{0:T(512)S(1)} %bitcast.169, f32[512]{0:T(512)S(1)} %bitcast.163, f32[512]{0:T(512)S(1)} %bitcast.175, ...), kind=kLoop, calls=%fused_computation.20 | loop fusion | flops 3670016 | bytes 1065476 | tf_op jit(solution)/shard_map/convert_element_type | solution.py:37
  134.3 1.3 all-to-all-done.6
  135.6 15.7 %all_to_all.50 = f32[16,2,8,128]{3,2,1,0:T(8,128)} all-to-all(f32[16,2,8,128]{3,2,1,0:T(8,128)S(1)} %broadcast_in_dim.162), channel_id=1, replica_groups=mesh['z'=16,'core'=2,'col'=16] {'z'}, dimensions={0} | all-to-all | bytes 262144 | tf_op jit(solution)/shard_map/all_to_all | solution.py:62
  151.3 5.4 %all-to-all-start.8 = ((f32[16,2,8,128]{3,2,1,0:T(8,128)}), f32[16,2,8,128]{3,2,1,0:T(8,128)S(1)}, u32[]{:S(2)}, u32[]{:S(2)}) async-start(f32[16,2,8,128]{3,2,1,0:T(8,128)} %all_to_all.50), calls=%async_computation.8 | async-start | bytes 262144 | tf_op jit(solution)/shard_map/all_to_all | solution.py:59
  156.7 5.6 %multiply_convert_fusion = (bf16[512,512]{1,0:T(8,128)(2,1)}, bf16[512,512]{1,0:T(8,128)(2,1)}) fusion(f32[512]{0:T(512)S(1)} %bitcast.184, f32[512]{0:T(512)S(1)} %bitcast.183, f32[]{:T(128)} %bitcast.125, f32[512]{0:T(512)S(1)} %bitcast.182, f32[512]{0:T(512)S(1)} %bitcast.170, f32[512]{0:T(512)S(1)} %bitcast.164, f32[512]{0:T(512)S(1)} %bitcast.176, ...), kind=kLoop, calls=%fused_computation.15 | loop fusion | flops 3670016 | bytes 1065476 | tf_op jit(solution)/shard_map/convert_element_type | solution.py:37
  162.3 1.2 all-to-all-done.8
  163.5 7.2 %collective-permute-start.2 = (f32[2,128,128]{2,1,0:T(8,128)S(1)}, f32[2,128,128]{2,1,0:T(8,128)S(1)}, u32[]{:S(2)}, u32[]{:S(2)}) collective-permute-start(f32[2,128,128]{2,1,0:T(8,128)S(1)} %bitcast.158), channel_id=1, source_target_pairs={{0,16},{16,0},{1,17},{17,1},{2,18},{18,2},{3,19},{19,3},{4,20},{20... | collective-permute-start | bytes 393224 | tf_op jit(solution)/shard_map/ppermute | solution.py:77
  170.7 1.0 collective-permute-done.2
  171.7 0.9 fusion.28
  172.7 0.3 fusion.26
  173.0 0.3 fusion.25
  173.3 0.3 fusion.24
  173.6 0.3 fusion.23
  173.9 0.3 fusion.22
  174.2 0.3 fusion.27
  174.5 0.3 fusion.5
  174.8 0.3 fusion.4
  175.2 0.3 fusion.3
  175.5 0.3 fusion.2
  175.8 0.3 fusion.1
  176.1 0.1 copy-done.3
  176.2 0.3 fusion
  176.5 43.2 %all_to_all.51 = f32[16,192,256]{2,1,0:T(8,128)S(1)} all-to-all(f32[16,192,256]{2,1,0:T(8,128)S(1)} %bitcast.150), channel_id=1, replica_groups=mesh['z'=16,'core'=2,'col'=16] {'col'}, dimensions={0} | all-to-all | bytes 6291456 | tf_op jit(solution)/shard_map/all_to_all | solution.py:169
  219.7 0.9 reduce_sum.39
  220.6 1.7 reshape.92
  (59 shorter events, 0.6 us)
Async XLA Ops:
  0.6 7.5 %copy-start = (f32[2,256,128]{2,1,0:T(8,128)S(1)}, f32[2,256,128]{2,1,0:T(8,128)}, u32[]{:S(2)}) copy-start(f32[2,256,128]{2,1,0:T(8,128)} %param.15) | copy-start | bytes 786436
  0.6 17.0 %copy-start.11 = (s32[2,256]{1,0:T(2,128)S(1)}, s32[2,256]{1,0:T(2,128)}, u32[]{:S(2)}) copy-start(s32[2,256]{1,0:T(2,128)} %param.19) | copy-start | bytes 6148
  0.7 17.0 %copy-start.10 = (f32[2,2,256]{2,1,0:T(2,128)S(1)}, f32[2,2,256]{2,1,0:T(2,128)}, u32[]{:S(2)}) copy-start(f32[2,2,256]{2,1,0:T(2,128)} %param.17) | copy-start | bytes 12292
  0.7 17.1 %copy-start.12 = (f32[2,256]{1,0:T(2,128)S(1)}, f32[2,256]{1,0:T(2,128)}, u32[]{:S(2)}) copy-start(f32[2,256]{1,0:T(2,128)} %param.18) | copy-start | bytes 6148
  0.7 38.9 %copy-start.1 = (f32[2,128,256]{2,1,0:T(8,128)S(1)}, f32[2,128,256]{2,1,0:T(8,128)}, u32[]{:S(2)}) copy-start(f32[2,128,256]{2,1,0:T(8,128)} %param.14) | copy-start | bytes 786436
  9.4 14.4 %all-to-all-start = ((f32[16,2,8,128]{3,2,1,0:T(8,128)}), f32[16,2,8,128]{3,2,1,0:T(8,128)S(1)}, u32[]{:S(2)}, u32[]{:S(2)}) async-start(f32[16,2,8,128]{3,2,1,0:T(8,128)} %copy.17), calls=%async_computation | async-start | bytes 262144 | tf_op jit(solution)/shard_map/all_to_all | solution.py:59
  24.5 27.0 %all-to-all-start.1 = ((f32[16,2,8,128]{3,2,1,0:T(8,128)}), f32[16,2,8,128]{3,2,1,0:T(8,128)}, u32[]{:S(2)}, u32[]{:S(2)}) async-start(f32[16,2,8,128]{3,2,1,0:T(8,128)} %broadcast_in_dim.152), calls=%async_computation.1 | async-start | bytes 262144 | tf_op jit(solution)/shard_map/all_to_all | solution.py:62
  51.6 13.0 %all-to-all-start.2 = ((f32[16,2,8,128]{3,2,1,0:T(8,128)}), f32[16,2,8,128]{3,2,1,0:T(8,128)S(1)}, u32[]{:S(2)}, u32[]{:S(2)}) async-start(f32[16,2,8,128]{3,2,1,0:T(8,128)} %all-to-all-done.1), calls=%async_computation.2 | async-start | bytes 262144 | tf_op jit(solution)/shard_map/all_to_all | solution.py:59
  64.5 26.5 %copy-start.2 = (f32[2,128,256]{2,1,0:T(8,128)S(1)}, f32[2,128,256]{2,1,0:T(8,128)}, u32[]{:S(2)}) copy-start(f32[2,128,256]{2,1,0:T(8,128)} %param.13) | copy-start | bytes 786436
  64.6 8.2 %collective-permute-start = (f32[2,128,128]{2,1,0:T(8,128)S(1)}, f32[2,128,128]{2,1,0:T(8,128)S(1)}, u32[]{:S(2)}, u32[]{:S(2)}) collective-permute-start(f32[2,128,128]{2,1,0:T(8,128)S(1)} %bitcast.156), channel_id=1, source_target_pairs={{0,16},{16,0},{1,17},{17,1},{2,18},{18,2},{3,19},{19,3},{4,20},{20... | collective-permute-start | bytes 393224 | tf_op jit(solution)/shard_map/ppermute | solution.py:77
  74.1 11.3 %all-to-all-start.3 = ((f32[16,2,8,128]{3,2,1,0:T(8,128)}), f32[16,2,8,128]{3,2,1,0:T(8,128)S(1)}, u32[]{:S(2)}, u32[]{:S(2)}) async-start(f32[16,2,8,128]{3,2,1,0:T(8,128)} %copy.19), calls=%async_computation.3 | async-start | bytes 262144 | tf_op jit(solution)/shard_map/all_to_all | solution.py:59
  86.8 16.2 %all-to-all-start.4 = ((f32[16,2,8,128]{3,2,1,0:T(8,128)}), f32[16,2,8,128]{3,2,1,0:T(8,128)}, u32[]{:S(2)}, u32[]{:S(2)}) async-start(f32[16,2,8,128]{3,2,1,0:T(8,128)} %broadcast_in_dim.157), calls=%async_computation.4 | async-start | bytes 262144 | tf_op jit(solution)/shard_map/all_to_all | solution.py:62
  103.0 12.2 %all-to-all-start.5 = ((f32[16,2,8,128]{3,2,1,0:T(8,128)}), f32[16,2,8,128]{3,2,1,0:T(8,128)S(1)}, u32[]{:S(2)}, u32[]{:S(2)}) async-start(f32[16,2,8,128]{3,2,1,0:T(8,128)} %all-to-all-done.4), calls=%async_computation.5 | async-start | bytes 262144 | tf_op jit(solution)/shard_map/all_to_all | solution.py:59
  115.2 7.8 %collective-permute-start.1 = (f32[2,128,128]{2,1,0:T(8,128)S(1)}, f32[2,128,128]{2,1,0:T(8,128)S(1)}, u32[]{:S(2)}, u32[]{:S(2)}) collective-permute-start(f32[2,128,128]{2,1,0:T(8,128)S(1)} %bitcast.157), channel_id=1, source_target_pairs={{0,16},{16,0},{1,17},{17,1},{2,18},{18,2},{3,19},{19,3},{4,20},{20... | collective-permute-start | bytes 393224 | tf_op jit(solution)/shard_map/ppermute | solution.py:77
  124.3 11.3 %all-to-all-start.6 = ((f32[16,2,8,128]{3,2,1,0:T(8,128)}), f32[16,2,8,128]{3,2,1,0:T(8,128)S(1)}, u32[]{:S(2)}, u32[]{:S(2)}) async-start(f32[16,2,8,128]{3,2,1,0:T(8,128)} %copy.21), calls=%async_computation.6 | async-start | bytes 262144 | tf_op jit(solution)/shard_map/all_to_all | solution.py:59
  151.3 12.2 %all-to-all-start.8 = ((f32[16,2,8,128]{3,2,1,0:T(8,128)}), f32[16,2,8,128]{3,2,1,0:T(8,128)S(1)}, u32[]{:S(2)}, u32[]{:S(2)}) async-start(f32[16,2,8,128]{3,2,1,0:T(8,128)} %all_to_all.50), calls=%async_computation.8 | async-start | bytes 262144 | tf_op jit(solution)/shard_map/all_to_all | solution.py:59
  163.5 9.1 %copy-start.5 = (bf16[512,512]{1,0:T(8,128)(2,1)S(1)}, bf16[512,512]{1,0:T(8,128)(2,1)}, u32[]{:S(2)}) copy-start(bf16[512,512]{1,0:T(8,128)(2,1)} %get-tuple-element.76) | copy-start | bytes 1572868
  163.5 9.5 %copy-start.6 = (bf16[512,512]{1,0:T(8,128)(2,1)S(1)}, bf16[512,512]{1,0:T(8,128)(2,1)}, u32[]{:S(2)}) copy-start(bf16[512,512]{1,0:T(8,128)(2,1)} %get-tuple-element.78) | copy-start | bytes 1572868
  163.5 9.8 %copy-start.7 = (bf16[512,512]{1,0:T(8,128)(2,1)S(1)}, bf16[512,512]{1,0:T(8,128)(2,1)}, u32[]{:S(2)}) copy-start(bf16[512,512]{1,0:T(8,128)(2,1)} %get-tuple-element.80) | copy-start | bytes 1572868
  163.5 8.1 %collective-permute-start.2 = (f32[2,128,128]{2,1,0:T(8,128)S(1)}, f32[2,128,128]{2,1,0:T(8,128)S(1)}, u32[]{:S(2)}, u32[]{:S(2)}) collective-permute-start(f32[2,128,128]{2,1,0:T(8,128)S(1)} %bitcast.158), channel_id=1, source_target_pairs={{0,16},{16,0},{1,17},{17,1},{2,18},{18,2},{3,19},{19,3},{4,20},{20... | collective-permute-start | bytes 393224 | tf_op jit(solution)/shard_map/ppermute | solution.py:77
  171.7 1.9 copy-start.8
  172.6 1.3 copy-start.9
  172.6 1.6 copy-start.4
  175.1 1.0 copy-start.3

commit v7 on v6

--- a/solution.py
+++ b/solution.py
@@ -82,6 +82,61 @@
     return vector, [o for o in outputs if o is not None]
 
 
+def col_sum_to_rows(partial, offset, work, gather_work):
+    n_col = lax.axis_size("col")
+    parts, rows, right = partial.shape
+    piece = rows // n_col
+    split = partial.reshape(parts, n_col, piece, right).transpose(1, 0, 2, 3)
+    scattered, done = beside(
+        lambda value: lax.all_to_all(value, "col", 0, 0, tiled=True), split, work
+    )
+    start = lax.axis_index("col") * piece
+    summed = lax.dynamic_slice_in_dim(offset, start, piece, 1) - scattered.sum(0)
+    spread = jnp.broadcast_to(summed[None], (n_col,) + summed.shape)
+    gathered, gather_done = beside(
+        lambda value: lax.all_to_all(value, "col", 0, 0, tiled=True), spread, gather_work
+    )
+    return gathered.transpose(1, 0, 2, 3).reshape(parts, rows, right), [done, gather_done]
+
+
+def row_sum(partial, works):
+    n_z = lax.axis_size("z")
+    parts, rows, right = partial.shape
+    piece = rows // n_z
+    chip = partial + lax.ppermute(partial, "core", [(0, 1), (1, 0)])
+    split = chip.reshape(parts, n_z, piece, right).transpose(1, 0, 2, 3)
+    def z_step(value):
+        return lax.all_to_all(value, "z", 0, 0, tiled=True)
+
+    scattered, first_done = beside(z_step, split, works[0])
+    summed = scattered.sum(0)
+    spread = jnp.broadcast_to(summed[None], (n_z,) + summed.shape)
+    gathered, second_done = beside(z_step, spread, works[1])
+    return gathered.transpose(1, 0, 2, 3).reshape(parts, rows, right), [first_done, second_done]
+
+
+def rows_of_column_block(block):
+    n_z = lax.axis_size("z")
+    n_col = lax.axis_size("col")
+    parts, rows, _ = block.shape
+    core = lax.axis_index("core")
+    halves = block.reshape(parts, rows, 2, rows)
+    own_half = jnp.where(core == 0, halves[:, :, 0], halves[:, :, 1])
+    other_half = jnp.where(core == 0, halves[:, :, 1], halves[:, :, 0])
+
+    def index(z, k, c):
+        return (z * 2 + k) * n_col + c
+
+    same = [(index(z, k, c), index(c, k, z)) for z in range(n_z) for k in range(2) for c in range(n_col)]
+    flip = [(index(z, k, c), index(c, 1 - k, z)) for z in range(n_z) for k in range(2) for c in range(n_col)]
+    axes = ("z", "core", "col")
+    from_same = lax.ppermute(own_half, axes, same)
+    from_flip = lax.ppermute(other_half, axes, flip)
+    first = jnp.where(core == 0, from_same, from_flip)
+    second = jnp.where(core == 0, from_flip, from_same)
+    return jnp.concatenate([first, second], axis=1)
+
+
 def per_device(
     inv_top,
     inv_bottom,
@@ -139,14 +194,12 @@
     top_solved, tiles_a = col_sum_to_columns(
         complex_product(stacked_matrix(inv_top), rhs_top), works=(works[0], None, works[1])
     )
-    remainder_cols, tiles_b = col_sum_to_columns(
-        complex_product(stacked_matrix(lower_panel), top_solved),
-        rhs_bottom,
-        works=(works[2], None, works[3]),
-    )
-    bottom_solved, tiles_c = col_sum_to_columns(
-        complex_product(stacked_matrix(inv_bottom), remainder_cols),
-        works=(works[4], None, works[5]),
+    bottom_moved = stacked_matrix(rows_of_column_block(inv_bottom))
+    remainder_rows, tiles_b = col_sum_to_rows(
+        complex_product(stacked_matrix(lower_panel), top_solved), rhs_bottom, works[2], works[3]
+    )
+    bottom_solved, tiles_c = row_sum(
+        complex_product(bottom_moved, remainder_rows), (works[4], works[5])
     )
     tile_chunks = tiles_a + tiles_b + tiles_c
     strengths = jnp.stack([top_solved, bottom_solved])

time: 223 us -> 244 us (1.094)
  the two profiles are of different devices: /device:TPU:1 before, /device:TPU:32 now
where the time goes in v7:
time: 244 us; the launch traced here: 243 us
  starting transfers between devices  85.1 us (35%)
  waiting for transfers between devices  52.6 us (22%)
  blocking collectives  43.7 us (18%)
  other arithmetic  40.5 us (17%)
  local copies, waits for them, and re-layouts  10.7 us (4%)
  matrix products  8.52 us (3%)
    all_to_all x1, blocking collectives, per_device(): summed = lax.all_to_all(split, 'col', 0, 0, tiled=True).sum(0)  43.7 us
    all_to_all x3, waiting for transfers between devices, z_step(): return lax.all_to_all(value, 'z', 0, 0, tiled=True)  39.6 us
    convert_element_type x6, other arithmetic, green_tile(): (amplitude * jnp.sin(phase_angle)).astype(jnp.bfloat16)  33.4 us
    all_to_all x2, starting transfers between devices, col_step(): return lax.all_to_all(value, 'col', 0, 0, tiled=True)  33.4 us
    all_to_all x3, starting transfers between devices, z_step(): return lax.all_to_all(value, 'z', 0, 0, tiled=True)  32.2 us
    all_to_all x2, starting transfers between devices, col_sum_to_rows(): lax.all_to_all(value, 'col', 0, 0, tiled=True)  9.54 us
    all_to_all x2, waiting for transfers between devices, col_step(): return lax.all_to_all(value, 'col', 0, 0, tiled=True)  5.35 us
    dot_general x6, matrix products, per_device(): jnp.dot(tile_real, for_real, preferred_element_type=jnp.float32)  4.98 us
  transfers between devices with their start and end apart: 11, of which 9 were waited for; matrix products, arithmetic and copies ran while one was open for 18% of the time, Pallas kernels for 0%

profile of v7, /device:TPU:32, one launch (start us, length us, event | category | flops | bytes accessed | tf_op | source)
XLA Modules:
  0.0 242.9 jit_solution(7935338366028087145)
XLA Ops:
  0.6 0.0 copy-start
  0.7 1.1 copy.35
  1.8 0.1 copy.45
  1.9 0.1 copy.44
  2.1 2.4 collective-permute-start.2
  4.5 3.8 %collective-permute-start.1 = (f32[2,128,128]{2,1,0:T(8,128)S(1)}, f32[2,128,128]{2,1,0:T(8,128)S(1)}, u32[]{:S(2)}, u32[]{:S(2)}) collective-permute-start(f32[2,128,128]{2,1,0:T(8,128)S(1)} %get-tuple-element.107), channel_id=1, source_target_pairs={{0,0},{1,32},{2,64},{3,96},{4,128},{5,160},{6,192},{7,224},{8,256}... | collective-permute-start | bytes 393224 | tf_op jit(solution)/shard_map/ppermute | solution.py:133
  8.3 0.9 fusion.21
  9.2 1.0 slice_bitcast_fusion.2
  10.2 1.5 fusion.44
  11.7 0.8 fusion.35
  12.4 2.0 broadcast_select_fusion.4
  14.4 1.3 broadcast_select_fusion.5
  15.8 0.6 convolution_bitcast_fusion.1
  16.4 0.7 copy.33
  17.1 17.6 %all-to-all-start = ((f32[16,2,8,128]{3,2,1,0:T(8,128)}), f32[16,2,8,128]{3,2,1,0:T(8,128)S(1)}, u32[]{:S(2)}, u32[]{:S(2)}) async-start(f32[16,2,8,128]{3,2,1,0:T(8,128)} %copy.33), calls=%async_computation | async-start | bytes 262144 | tf_op jit(solution)/shard_map/all_to_all | solution.py:59
  35.5 5.5 %multiply_convert_fusion.10 = (bf16[512,512]{1,0:T(8,128)(2,1)S(1)}, bf16[512,512]{1,0:T(8,128)(2,1)}) fusion(f32[]{:T(128)} %bitcast.115, f32[512]{0:T(512)S(1)} %bitcast.167, f32[512]{0:T(512)S(1)} %bitcast.155, f32[512]{0:T(512)S(1)} %bitcast.182, f32[512]{0:T(512)S(1)} %bitcast.149, f32[512]{0:T(512)S(1)} %bitcast.181, f32[512]{0:T(512)S(1)} %bitcast.161, ...), kind=kLoop, calls=%fused_computation.39 | loop fusion | flops 3670016 | bytes 1065476 | tf_op jit(solution)/shard_map/convert_element_type | solution.py:37
  41.0 2.9 %all-to-all-done = f32[16,2,8,128]{3,2,1,0:T(8,128)S(1)} async-done(((f32[16,2,8,128]{3,2,1,0:T(8,128)}), f32[16,2,8,128]{3,2,1,0:T(8,128)S(1)}, u32[]{:S(2)}, u32[]{:S(2)}) %all-to-all-start) | async-done | bytes 131104 | tf_op jit(solution)/shard_map/all_to_all | solution.py:59
  44.0 0.7 broadcast_in_dim.152
  44.6 21.9 %all-to-all-start.1 = ((f32[16,2,8,128]{3,2,1,0:T(8,128)}), f32[16,2,8,128]{3,2,1,0:T(8,128)}, u32[]{:S(2)}, u32[]{:S(2)}) async-start(f32[16,2,8,128]{3,2,1,0:T(8,128)} %broadcast_in_dim.152), calls=%async_computation.1 | async-start | bytes 262144 | tf_op jit(solution)/shard_map/all_to_all | solution.py:62
  66.7 14.4 %all-to-all-done.1 = f32[16,2,8,128]{3,2,1,0:T(8,128)} async-done(((f32[16,2,8,128]{3,2,1,0:T(8,128)}), f32[16,2,8,128]{3,2,1,0:T(8,128)}, u32[]{:S(2)}, u32[]{:S(2)}) %all-to-all-start.1) | async-done | bytes 131104 | tf_op jit(solution)/shard_map/all_to_all | solution.py:62
  81.1 15.8 %all-to-all-start.2 = ((f32[16,2,8,128]{3,2,1,0:T(8,128)}), f32[16,2,8,128]{3,2,1,0:T(8,128)S(1)}, u32[]{:S(2)}, u32[]{:S(2)}) async-start(f32[16,2,8,128]{3,2,1,0:T(8,128)} %all-to-all-done.1), calls=%async_computation.2 | async-start | bytes 262144 | tf_op jit(solution)/shard_map/all_to_all | solution.py:59
  96.9 5.5 %multiply_convert_fusion.8 = (bf16[512,512]{1,0:T(8,128)(2,1)S(1)}, bf16[512,512]{1,0:T(8,128)(2,1)}) fusion(f32[512]{0:T(512)S(1)} %bitcast.176, f32[512]{0:T(512)S(1)} %bitcast.175, f32[]{:T(128)} %bitcast.116, f32[512]{0:T(512)S(1)} %bitcast.168, f32[512]{0:T(512)S(1)} %bitcast.156, f32[512]{0:T(512)S(1)} %bitcast.150, f32[512]{0:T(512)S(1)} %bitcast.162, ...), kind=kLoop, calls=%fused_computation.34 | loop fusion | flops 3670016 | bytes 1065476 | tf_op jit(solution)/shard_map/convert_element_type | solution.py:37
  102.4 2.4 %all-to-all-done.2 = f32[16,2,8,128]{3,2,1,0:T(8,128)S(1)} async-done(((f32[16,2,8,128]{3,2,1,0:T(8,128)}), f32[16,2,8,128]{3,2,1,0:T(8,128)S(1)}, u32[]{:S(2)}, u32[]{:S(2)}) %all-to-all-start.2) | async-done | bytes 131104 | tf_op jit(solution)/shard_map/all_to_all | solution.py:59
  104.9 1.9 collective-permute-start
  106.9 1.3 collective-permute-done
  108.2 0.6 convolution_bitcast_fusion
  108.8 0.7 copy.38
  109.5 4.8 %all-to-all-start.3 = ((f32[16,2,8,128]{3,2,1,0:T(8,128)}), f32[16,2,8,128]{3,2,1,0:T(8,128)S(1)}, u32[]{:S(2)}, u32[]{:S(2)}) async-start(f32[16,2,8,128]{3,2,1,0:T(8,128)} %copy.38), calls=%async_computation.3 | async-start | bytes 262144 | tf_op jit(solution)/shard_map/all_to_all | solution.py:91
  114.2 5.5 %multiply_convert_fusion.6 = (bf16[512,512]{1,0:T(8,128)(2,1)S(1)}, bf16[512,512]{1,0:T(8,128)(2,1)}) fusion(f32[512]{0:T(512)S(1)} %bitcast.178, f32[512]{0:T(512)S(1)} %bitcast.177, f32[]{:T(128)} %bitcast.117, f32[512]{0:T(512)S(1)} %bitcast.169, f32[512]{0:T(512)S(1)} %bitcast.157, f32[512]{0:T(512)S(1)} %bitcast.151, f32[512]{0:T(512)S(1)} %bitcast.163, ...), kind=kLoop, calls=%fused_computation.29 | loop fusion | flops 3670016 | bytes 1065476 | tf_op jit(solution)/shard_map/convert_element_type | solution.py:37
  119.8 2.4 %all-to-all-done.3 = f32[16,2,8,128]{3,2,1,0:T(8,128)S(1)} async-done(((f32[16,2,8,128]{3,2,1,0:T(8,128)}), f32[16,2,8,128]{3,2,1,0:T(8,128)S(1)}, u32[]{:S(2)}, u32[]{:S(2)}) %all-to-all-start.3) | async-done | bytes 131104 | tf_op jit(solution)/shard_map/all_to_all | solution.py:91
  122.2 0.7 dynamic-slice_subtract_fusion
  123.0 0.7 broadcast_in_dim.157
  123.6 4.8 %all-to-all-start.4 = ((f32[16,2,8,128]{3,2,1,0:T(8,128)}), f32[16,2,8,128]{3,2,1,0:T(8,128)S(1)}, u32[]{:S(2)}, u32[]{:S(2)}) async-start(f32[16,2,8,128]{3,2,1,0:T(8,128)} %broadcast_in_dim.157), calls=%async_computation.4 | async-start | bytes 262144 | tf_op jit(solution)/shard_map/all_to_all | solution.py:97
  128.4 5.5 %multiply_convert_fusion.4 = (bf16[512,512]{1,0:T(8,128)(2,1)S(1)}, bf16[512,512]{1,0:T(8,128)(2,1)}) fusion(f32[512]{0:T(512)S(1)} %bitcast.180, f32[512]{0:T(512)S(1)} %bitcast.179, f32[]{:T(128)} %bitcast.118, f32[512]{0:T(512)S(1)} %bitcast.170, f32[512]{0:T(512)S(1)} %bitcast.158, f32[512]{0:T(512)S(1)} %bitcast.152, f32[512]{0:T(512)S(1)} %bitcast.164, ...), kind=kLoop, calls=%fused_computation.24 | loop fusion | flops 3670016 | bytes 1065476 | tf_op jit(solution)/shard_map/convert_element_type | solution.py:37
  134.0 2.4 %all-to-all-done.4 = f32[16,2,8,128]{3,2,1,0:T(8,128)S(1)} async-done(((f32[16,2,8,128]{3,2,1,0:T(8,128)}), f32[16,2,8,128]{3,2,1,0:T(8,128)S(1)}, u32[]{:S(2)}, u32[]{:S(2)}) %all-to-all-start.4) | async-done | bytes 131104 | tf_op jit(solution)/shard_map/all_to_all | solution.py:97
  136.4 0.6 fusion.45
  137.0 1.9 collective-permute-start.3
  138.9 1.5 collective-permute-done.3
  140.5 0.7 copy.56
  141.2 4.2 %all-to-all-start.5 = ((f32[16,2,16,128]{3,2,1,0:T(8,128)}), f32[16,2,16,128]{3,2,1,0:T(8,128)S(1)}, u32[]{:S(2)}, u32[]{:S(2)}) async-start(f32[16,2,16,128]{3,2,1,0:T(8,128)} %bitcast.111), calls=%async_computation.5 | async-start | bytes 524288 | tf_op jit(solution)/shard_map/all_to_all | solution.py:109
  145.4 5.6 %multiply_convert_fusion.2 = (bf16[512,512]{1,0:T(8,128)(2,1)}, bf16[512,512]{1,0:T(8,128)(2,1)}) fusion(f32[512]{0:T(512)S(1)} %bitcast.184, f32[512]{0:T(512)S(1)} %bitcast.183, f32[]{:T(128)} %bitcast.119, f32[512]{0:T(512)S(1)} %bitcast.171, f32[512]{0:T(512)S(1)} %bitcast.159, f32[512]{0:T(512)S(1)} %bitcast.153, f32[512]{0:T(512)S(1)} %bitcast.165, ...), kind=kLoop, calls=%fused_computation.19 | loop fusion | flops 3670016 | bytes 1065476 | tf_op jit(solution)/shard_map/convert_element_type | solution.py:37
  151.0 12.7 %all-to-all-done.5 = f32[16,2,16,128]{3,2,1,0:T(8,128)S(1)} async-done(((f32[16,2,16,128]{3,2,1,0:T(8,128)}), f32[16,2,16,128]{3,2,1,0:T(8,128)S(1)}, u32[]{:S(2)}, u32[]{:S(2)}) %all-to-all-start.5) | async-done | bytes 262176 | tf_op jit(solution)/shard_map/all_to_all | solution.py:109
  163.8 0.7 broadcast_in_dim.162
  164.5 6.1 %all-to-all-start.6 = ((f32[16,2,16,128]{3,2,1,0:T(8,128)}), f32[16,2,16,128]{3,2,1,0:T(8,128)S(1)}, u32[]{:S(2)}, u32[]{:S(2)}) async-start(f32[16,2,16,128]{3,2,1,0:T(8,128)} %broadcast_in_dim.162), calls=%async_computation.6 | async-start | bytes 524288 | tf_op jit(solution)/shard_map/all_to_all | solution.py:109
  170.6 5.6 %multiply_convert_fusion = (bf16[512,512]{1,0:T(8,128)(2,1)}, bf16[512,512]{1,0:T(8,128)(2,1)}) fusion(f32[512]{0:T(512)S(1)} %bitcast.174, f32[512]{0:T(512)S(1)} %bitcast.173, f32[]{:T(128)} %bitcast.114, f32[512]{0:T(512)S(1)} %bitcast.172, f32[512]{0:T(512)S(1)} %bitcast.160, f32[512]{0:T(512)S(1)} %bitcast.154, f32[512]{0:T(512)S(1)} %bitcast.166, ...), kind=kLoop, calls=%fused_computation.14 | loop fusion | flops 3670016 | bytes 1065476 | tf_op jit(solution)/shard_map/convert_element_type | solution.py:37
  176.2 12.4 %all-to-all-done.6 = f32[16,2,16,128]{3,2,1,0:T(8,128)S(1)} async-done(((f32[16,2,16,128]{3,2,1,0:T(8,128)}), f32[16,2,16,128]{3,2,1,0:T(8,128)S(1)}, u32[]{:S(2)}, u32[]{:S(2)}) %all-to-all-start.6) | async-done | bytes 262176 | tf_op jit(solution)/shard_map/all_to_all | solution.py:109
  188.7 0.9 fusion.30
  189.6 1.4 fusion.28
  191.0 1.3 fusion.27
  192.4 1.3 fusion.26
  193.7 0.3 fusion.25
  194.0 0.3 fusion.24
  194.4 0.3 fusion.29
  194.7 0.3 fusion.5
  195.0 0.3 fusion.4
  195.3 0.3 fusion.3
  195.6 0.3 fusion.2
  195.9 0.1 copy-done.2
  196.0 0.3 fusion.1
  196.3 0.1 copy-done.3
  196.4 0.3 fusion
  196.7 43.7 %all_to_all.40 = f32[16,192,256]{2,1,0:T(8,128)S(1)} all-to-all(f32[16,192,256]{2,1,0:T(8,128)S(1)} %bitcast.139), channel_id=1, replica_groups=mesh['z'=16,'core'=2,'col'=16] {'col'}, dimensions={0} | all-to-all | bytes 6291456 | tf_op jit(solution)/shard_map/all_to_all | solution.py:222
  240.3 0.9 reduce_sum.39
  241.2 1.7 reshape.93
  (55 shorter events, 0.6 us)
Async XLA Ops:
  0.6 15.2 %copy-start = (f32[2,256,128]{2,1,0:T(8,128)S(1)}, f32[2,256,128]{2,1,0:T(8,128)}, u32[]{:S(2)}) copy-start(f32[2,256,128]{2,1,0:T(8,128)} %param.15) | copy-start | bytes 786436
  0.6 34.7 %copy-start.8 = (s32[2,256]{1,0:T(2,128)S(1)}, s32[2,256]{1,0:T(2,128)}, u32[]{:S(2)}) copy-start(s32[2,256]{1,0:T(2,128)} %param.19) | copy-start | bytes 6148
  0.7 34.7 %copy-start.7 = (f32[2,2,256]{2,1,0:T(2,128)S(1)}, f32[2,2,256]{2,1,0:T(2,128)}, u32[]{:S(2)}) copy-start(f32[2,2,256]{2,1,0:T(2,128)} %param.17) | copy-start | bytes 12292
  0.7 34.7 %copy-start.9 = (f32[2,256]{1,0:T(2,128)S(1)}, f32[2,256]{1,0:T(2,128)}, u32[]{:S(2)}) copy-start(f32[2,256]{1,0:T(2,128)} %param.18) | copy-start | bytes 6148
  1.8 39.2 %copy-start.1 = (f32[2,128,256]{2,1,0:T(8,128)S(1)}, f32[2,128,256]{2,1,0:T(8,128)}, u32[]{:S(2)}) copy-start(f32[2,128,256]{2,1,0:T(8,128)} %param.14) | copy-start | bytes 786436
  2.1 64.5 %collective-permute-start.2 = (f32[2,128,128]{2,1,0:T(8,128)S(1)}, f32[2,128,128]{2,1,0:T(8,128)S(1)}, u32[]{:S(2)}, u32[]{:S(2)}) collective-permute-start(f32[2,128,128]{2,1,0:T(8,128)S(1)} %get-tuple-element.106), channel_id=1, source_target_pairs={{0,16},{1,48},{2,80},{3,112},{4,144},{5,176},{6,208},{7,240},{8,27... | collective-permute-start | bytes 393224 | tf_op jit(solution)/shard_map/ppermute | solution.py:134
  4.5 62.1 %collective-permute-start.1 = (f32[2,128,128]{2,1,0:T(8,128)S(1)}, f32[2,128,128]{2,1,0:T(8,128)S(1)}, u32[]{:S(2)}, u32[]{:S(2)}) collective-permute-start(f32[2,128,128]{2,1,0:T(8,128)S(1)} %get-tuple-element.107), channel_id=1, source_target_pairs={{0,0},{1,32},{2,64},{3,96},{4,128},{5,160},{6,192},{7,224},{8,256}... | collective-permute-start | bytes 393224 | tf_op jit(solution)/shard_map/ppermute | solution.py:133
  17.1 26.9 %all-to-all-start = ((f32[16,2,8,128]{3,2,1,0:T(8,128)}), f32[16,2,8,128]{3,2,1,0:T(8,128)S(1)}, u32[]{:S(2)}, u32[]{:S(2)}) async-start(f32[16,2,8,128]{3,2,1,0:T(8,128)} %copy.33), calls=%async_computation | async-start | bytes 262144 | tf_op jit(solution)/shard_map/all_to_all | solution.py:59
  44.6 36.5 %all-to-all-start.1 = ((f32[16,2,8,128]{3,2,1,0:T(8,128)}), f32[16,2,8,128]{3,2,1,0:T(8,128)}, u32[]{:S(2)}, u32[]{:S(2)}) async-start(f32[16,2,8,128]{3,2,1,0:T(8,128)} %broadcast_in_dim.152), calls=%async_computation.1 | async-start | bytes 262144 | tf_op jit(solution)/shard_map/all_to_all | solution.py:62
  81.1 23.8 %all-to-all-start.2 = ((f32[16,2,8,128]{3,2,1,0:T(8,128)}), f32[16,2,8,128]{3,2,1,0:T(8,128)S(1)}, u32[]{:S(2)}, u32[]{:S(2)}) async-start(f32[16,2,8,128]{3,2,1,0:T(8,128)} %all-to-all-done.1), calls=%async_computation.2 | async-start | bytes 262144 | tf_op jit(solution)/shard_map/all_to_all | solution.py:59
  104.9 3.2 %collective-permute-start = (f32[2,128,128]{2,1,0:T(8,128)S(1)}, f32[2,128,128]{2,1,0:T(8,128)S(1)}, u32[]{:S(2)}, u32[]{:S(2)}) collective-permute-start(f32[2,128,128]{2,1,0:T(8,128)S(1)} %bitcast.148), channel_id=1, source_target_pairs={{0,16},{16,0},{1,17},{17,1},{2,18},{18,2},{3,19},{19,3},{4,20},{20... | collective-permute-start | bytes 393224 | tf_op jit(solution)/shard_map/ppermute | solution.py:77
  109.5 12.8 %all-to-all-start.3 = ((f32[16,2,8,128]{3,2,1,0:T(8,128)}), f32[16,2,8,128]{3,2,1,0:T(8,128)S(1)}, u32[]{:S(2)}, u32[]{:S(2)}) async-start(f32[16,2,8,128]{3,2,1,0:T(8,128)} %copy.38), calls=%async_computation.3 | async-start | bytes 262144 | tf_op jit(solution)/shard_map/all_to_all | solution.py:91
  123.6 12.8 %all-to-all-start.4 = ((f32[16,2,8,128]{3,2,1,0:T(8,128)}), f32[16,2,8,128]{3,2,1,0:T(8,128)S(1)}, u32[]{:S(2)}, u32[]{:S(2)}) async-start(f32[16,2,8,128]{3,2,1,0:T(8,128)} %broadcast_in_dim.157), calls=%async_computation.4 | async-start | bytes 262144 | tf_op jit(solution)/shard_map/all_to_all | solution.py:97
  137.0 3.4 %collective-permute-start.3 = (f32[2,256,128]{2,1,0:T(8,128)S(1)}, f32[2,256,128]{2,1,0:T(8,128)S(1)}, u32[]{:S(2)}, u32[]{:S(2)}) collective-permute-start(f32[2,256,128]{2,1,0:T(8,128)S(1)} %fusion.45), channel_id=1, source_target_pairs={{0,16},{16,0},{1,17},{17,1},{2,18},{18,2},{3,19},{19,3},{4,20},{20... | collective-permute-start | bytes 786440 | tf_op jit(solution)/shard_map/ppermute | solution.py:106
  141.2 22.5 %all-to-all-start.5 = ((f32[16,2,16,128]{3,2,1,0:T(8,128)}), f32[16,2,16,128]{3,2,1,0:T(8,128)S(1)}, u32[]{:S(2)}, u32[]{:S(2)}) async-start(f32[16,2,16,128]{3,2,1,0:T(8,128)} %bitcast.111), calls=%async_computation.5 | async-start | bytes 524288 | tf_op jit(solution)/shard_map/all_to_all | solution.py:109
  164.5 24.1 %all-to-all-start.6 = ((f32[16,2,16,128]{3,2,1,0:T(8,128)}), f32[16,2,16,128]{3,2,1,0:T(8,128)S(1)}, u32[]{:S(2)}, u32[]{:S(2)}) async-start(f32[16,2,16,128]{3,2,1,0:T(8,128)} %broadcast_in_dim.162), calls=%async_computation.6 | async-start | bytes 524288 | tf_op jit(solution)/shard_map/all_to_all | solution.py:109
  188.7 5.1 %copy-start.5 = (bf16[512,512]{1,0:T(8,128)(2,1)S(1)}, bf16[512,512]{1,0:T(8,128)(2,1)}, u32[]{:S(2)}) copy-start(bf16[512,512]{1,0:T(8,128)(2,1)} %get-tuple-element.82) | copy-start | bytes 1572868
  189.5 4.5 %copy-start.6 = (bf16[512,512]{1,0:T(8,128)(2,1)S(1)}, bf16[512,512]{1,0:T(8,128)(2,1)}, u32[]{:S(2)}) copy-start(bf16[512,512]{1,0:T(8,128)(2,1)} %get-tuple-element.84) | copy-start | bytes 1572868
  189.6 4.8 %copy-start.4 = (bf16[512,512]{1,0:T(8,128)(2,1)S(1)}, bf16[512,512]{1,0:T(8,128)(2,1)}, u32[]{:S(2)}) copy-start(bf16[512,512]{1,0:T(8,128)(2,1)} %get-tuple-element.74) | copy-start | bytes 1572868
  195.0 1.0 copy-start.2
  195.3 1.1 copy-start.3

commit v8 on v7

--- a/solution.py
+++ b/solution.py
@@ -194,6 +194,7 @@
     top_solved, tiles_a = col_sum_to_columns(
         complex_product(stacked_matrix(inv_top), rhs_top), works=(works[0], None, works[1])
     )
+    inv_bottom, top_solved = lax.optimization_barrier((inv_bottom, top_solved))
     bottom_moved = stacked_matrix(rows_of_column_block(inv_bottom))
     remainder_rows, tiles_b = col_sum_to_rows(
         complex_product(stacked_matrix(lower_panel), top_solved), rhs_bottom, works[2], works[3]

time: 244 us -> 251 us (1.029)
  waiting for transfers between devices: 52.6 us -> 66.6 us
  starting transfers between devices: 85.1 us -> 71.5 us
  blocking collectives: 43.7 us -> 49.1 us
    ppermute x1, waiting for transfers between devices: 0.01 us -> 22.7 us  [rows_of_column_block(): from_same = lax.ppermute(own_half, axes, same)]
    all_to_all x2, starting transfers between devices: 33.4 us -> 13.6 us  [col_step(): return lax.all_to_all(value, 'col', 0, 0, tiled=True)]
    all_to_all x2, starting transfers between devices: 9.54 us -> 22.2 us  [col_sum_to_rows(): lax.all_to_all(value, 'col', 0, 0, tiled=True)]
    all_to_all x3, starting transfers between devices: 32.2 us -> 25.6 us  [z_step(): return lax.all_to_all(value, 'z', 0, 0, tiled=True)]
    all_to_all x1, blocking collectives: 43.7 us -> 49.1 us  [per_device(): summed = lax.all_to_all(split, 'col', 0, 0, tiled=True).sum(0)]
    all_to_all x2, waiting for transfers between devices: 4.88 us -> 0.01 us  [col_sum_to_rows(): lax.all_to_all(value, 'col', 0, 0, tiled=True)]
    all_to_all x3, waiting for transfers between devices: 39.6 us -> 37.1 us  [z_step(): return lax.all_to_all(value, 'z', 0, 0, tiled=True)]
  transfers between devices with their start and end apart: 11 -> 11, of which waited for: 9 -> 8; matrix products, arithmetic and copies ran while one was open for 18% -> 15% of each run, Pallas kernels for 0% -> 0%
where the time goes in v8:
time: 251 us; the launch traced here: 250 us
  starting transfers between devices  71.5 us (28%)
  waiting for transfers between devices  66.6 us (27%)
  blocking collectives  49.1 us (20%)
  other arithmetic  42 us (17%)
  local copies, waits for them, and re-layouts  10.4 us (4%)
  matrix products  8.52 us (3%)
    all_to_all x1, blocking collectives, per_device(): summed = lax.all_to_all(split, 'col', 0, 0, tiled=True).sum(0)  49.1 us
    all_to_all x3, waiting for transfers between devices, z_step(): return lax.all_to_all(value, 'z', 0, 0, tiled=True)  37.1 us
    convert_element_type x6, other arithmetic, green_tile(): (amplitude * jnp.sin(phase_angle)).astype(jnp.bfloat16)  34.9 us
    all_to_all x3, starting transfers between devices, z_step(): return lax.all_to_all(value, 'z', 0, 0, tiled=True)  25.6 us
    ppermute x1, waiting for transfers between devices, rows_of_column_block(): from_same = lax.ppermute(own_half, axes, same)  22.7 us
    all_to_all x2, starting transfers between devices, col_sum_to_rows(): lax.all_to_all(value, 'col', 0, 0, tiled=True)  22.2 us
    all_to_all x2, starting transfers between devices, col_step(): return lax.all_to_all(value, 'col', 0, 0, tiled=True)  13.6 us
  transfers between devices with their start and end apart: 11, of which 8 were waited for; matrix products, arithmetic and copies ran while one was open for 15% of the time, Pallas kernels for 0%

profile of v8, /device:TPU:32, one launch (start us, length us, event | category | flops | bytes accessed | tf_op | source)
XLA Modules:
  0.0 250.0 jit_solution(3142611726723314961)
XLA Ops:
  0.6 0.0 copy-start
  0.7 1.0 fusion.21
  1.7 1.0 slice_bitcast_fusion.2
  2.6 1.5 fusion.43
  4.1 0.8 fusion.34
  4.9 2.0 broadcast_select_fusion.4
  6.9 1.3 broadcast_select_fusion.5
  8.2 0.6 fusion.35
  8.9 0.6 convolution_bitcast_fusion.1
  9.4 0.7 copy.32
  10.1 7.0 %all-to-all-start = ((f32[16,2,8,128]{3,2,1,0:T(8,128)}), f32[16,2,8,128]{3,2,1,0:T(8,128)S(1)}, u32[]{:S(2)}, u32[]{:S(2)}) async-start(f32[16,2,8,128]{3,2,1,0:T(8,128)} %copy.32), calls=%async_computation | async-start | bytes 262144 | tf_op jit(solution)/shard_map/all_to_all | solution.py:59
  18.0 5.5 %multiply_convert_fusion.10 = (bf16[512,512]{1,0:T(8,128)(2,1)S(1)}, bf16[512,512]{1,0:T(8,128)(2,1)}) fusion(f32[]{:T(128)} %bitcast.114, f32[512]{0:T(512)S(1)} %bitcast.167, f32[512]{0:T(512)S(1)} %bitcast.155, f32[512]{0:T(512)S(1)} %bitcast.182, f32[512]{0:T(512)S(1)} %bitcast.149, f32[512]{0:T(512)S(1)} %bitcast.181, f32[512]{0:T(512)S(1)} %bitcast.161, ...), kind=kLoop, calls=%fused_computation.39 | loop fusion | flops 3670016 | bytes 1065476 | tf_op jit(solution)/shard_map/convert_element_type | solution.py:37
  23.5 1.6 all-to-all-done
  25.2 0.7 broadcast_in_dim.152
  25.8 15.2 %all-to-all-start.1 = ((f32[16,2,8,128]{3,2,1,0:T(8,128)}), f32[16,2,8,128]{3,2,1,0:T(8,128)}, u32[]{:S(2)}, u32[]{:S(2)}) async-start(f32[16,2,8,128]{3,2,1,0:T(8,128)} %broadcast_in_dim.152), calls=%async_computation.1 | async-start | bytes 262144 | tf_op jit(solution)/shard_map/all_to_all | solution.py:62
  41.1 12.6 %all-to-all-done.1 = f32[16,2,8,128]{3,2,1,0:T(8,128)} async-done(((f32[16,2,8,128]{3,2,1,0:T(8,128)}), f32[16,2,8,128]{3,2,1,0:T(8,128)}, u32[]{:S(2)}, u32[]{:S(2)}) %all-to-all-start.1) | async-done | bytes 131104 | tf_op jit(solution)/shard_map/all_to_all | solution.py:62
  53.7 6.6 %all-to-all-start.2 = ((f32[16,2,8,128]{3,2,1,0:T(8,128)}), f32[16,2,8,128]{3,2,1,0:T(8,128)S(1)}, u32[]{:S(2)}, u32[]{:S(2)}) async-start(f32[16,2,8,128]{3,2,1,0:T(8,128)} %all-to-all-done.1), calls=%async_computation.2 | async-start | bytes 262144 | tf_op jit(solution)/shard_map/all_to_all | solution.py:59
  60.3 5.5 %multiply_convert_fusion.8 = (bf16[512,512]{1,0:T(8,128)(2,1)S(1)}, bf16[512,512]{1,0:T(8,128)(2,1)}) fusion(f32[512]{0:T(512)S(1)} %bitcast.178, f32[512]{0:T(512)S(1)} %bitcast.177, f32[]{:T(128)} %bitcast.115, f32[512]{0:T(512)S(1)} %bitcast.168, f32[512]{0:T(512)S(1)} %bitcast.156, f32[512]{0:T(512)S(1)} %bitcast.150, f32[512]{0:T(512)S(1)} %bitcast.162, ...), kind=kLoop, calls=%fused_computation.34 | loop fusion | flops 3670016 | bytes 1065476 | tf_op jit(solution)/shard_map/convert_element_type | solution.py:37
  65.8 2.4 all-to-all-done.2
  68.3 1.9 collective-permute-start
  70.3 1.2 collective-permute-done
  71.6 0.6 convolution_bitcast_fusion
  72.2 0.7 copy.37
  72.8 4.8 %all-to-all-start.3 = ((f32[16,2,8,128]{3,2,1,0:T(8,128)}), f32[16,2,8,128]{3,2,1,0:T(8,128)S(1)}, u32[]{:S(2)}, u32[]{:S(2)}) async-start(f32[16,2,8,128]{3,2,1,0:T(8,128)} %copy.37), calls=%async_computation.3 | async-start | bytes 262144 | tf_op jit(solution)/shard_map/all_to_all | solution.py:91
  77.6 0.1 copy.34
  77.8 0.1 copy.44
  77.9 0.1 copy.43
  78.0 3.3 %collective-permute-start.2 = (f32[2,128,128]{2,1,0:T(8,128)S(1)}, f32[2,128,128]{2,1,0:T(8,128)S(1)}, u32[]{:S(2)}, u32[]{:S(2)}) collective-permute-start(f32[2,128,128]{2,1,0:T(8,128)S(1)} %get-tuple-element.104), channel_id=1, source_target_pairs={{0,16},{1,48},{2,80},{3,112},{4,144},{5,176},{6,208},{7,240},{8,27... | collective-permute-start | bytes 393224 | tf_op jit(solution)/shard_map/ppermute | solution.py:134
  81.3 2.9 %collective-permute-start.1 = (f32[2,128,128]{2,1,0:T(8,128)S(1)}, f32[2,128,128]{2,1,0:T(8,128)S(1)}, u32[]{:S(2)}, u32[]{:S(2)}) collective-permute-start(f32[2,128,128]{2,1,0:T(8,128)S(1)} %get-tuple-element.105), channel_id=1, source_target_pairs={{0,0},{1,32},{2,64},{3,96},{4,128},{5,160},{6,192},{7,224},{8,256}... | collective-permute-start | bytes 393224 | tf_op jit(solution)/shard_map/ppermute | solution.py:133
  84.3 5.5 %multiply_convert_fusion.6 = (bf16[512,512]{1,0:T(8,128)(2,1)S(1)}, bf16[512,512]{1,0:T(8,128)(2,1)}) fusion(f32[512]{0:T(512)S(1)} %bitcast.174, f32[512]{0:T(512)S(1)} %bitcast.173, f32[]{:T(128)} %bitcast.116, f32[512]{0:T(512)S(1)} %bitcast.169, f32[512]{0:T(512)S(1)} %bitcast.157, f32[512]{0:T(512)S(1)} %bitcast.151, f32[512]{0:T(512)S(1)} %bitcast.163, ...), kind=kLoop, calls=%fused_computation.29 | loop fusion | flops 3670016 | bytes 1065476 | tf_op jit(solution)/shard_map/convert_element_type | solution.py:37
  89.9 0.7 dynamic-slice_subtract_fusion
  90.6 0.7 broadcast_in_dim.157
  91.2 17.5 %all-to-all-start.4 = ((f32[16,2,8,128]{3,2,1,0:T(8,128)}), f32[16,2,8,128]{3,2,1,0:T(8,128)S(1)}, u32[]{:S(2)}, u32[]{:S(2)}) async-start(f32[16,2,8,128]{3,2,1,0:T(8,128)} %broadcast_in_dim.157), calls=%async_computation.4 | async-start | bytes 262144 | tf_op jit(solution)/shard_map/all_to_all | solution.py:97
  108.7 6.3 %multiply_convert_fusion.4 = (bf16[512,512]{1,0:T(8,128)(2,1)S(1)}, bf16[512,512]{1,0:T(8,128)(2,1)}) fusion(f32[512]{0:T(512)S(1)} %bitcast.180, f32[512]{0:T(512)S(1)} %bitcast.179, f32[]{:T(128)} %bitcast.117, f32[512]{0:T(512)} %bitcast.170, f32[512]{0:T(512)} %bitcast.158, f32[512]{0:T(512)} %bitcast.152, f32[512]{0:T(512)} %bitcast.164, ...), kind=kLoop, calls=%fused_computation.24 | loop fusion | flops 3670016 | bytes 1065476 | tf_op jit(solution)/shard_map/convert_element_type | solution.py:37
  115.0 22.7 %collective-permute-done.1 = f32[2,128,128]{2,1,0:T(8,128)S(1)} collective-permute-done((f32[2,128,128]{2,1,0:T(8,128)S(1)}, f32[2,128,128]{2,1,0:T(8,128)S(1)}, u32[]{:S(2)}, u32[]{:S(2)}) %collective-permute-start.1) | collective-permute-done | bytes 131104 | tf_op jit(solution)/shard_map/ppermute | solution.py:133
  137.9 0.6 fusion.44
  138.5 1.9 collective-permute-start.3
  140.4 1.5 collective-permute-done.3
  142.0 0.7 copy.55
  142.7 4.3 %all-to-all-start.5 = ((f32[16,2,16,128]{3,2,1,0:T(8,128)}), f32[16,2,16,128]{3,2,1,0:T(8,128)S(1)}, u32[]{:S(2)}, u32[]{:S(2)}) async-start(f32[16,2,16,128]{3,2,1,0:T(8,128)} %bitcast.110), calls=%async_computation.5 | async-start | bytes 524288 | tf_op jit(solution)/shard_map/all_to_all | solution.py:109
  147.0 6.3 %multiply_convert_fusion.2 = (bf16[512,512]{1,0:T(8,128)(2,1)}, bf16[512,512]{1,0:T(8,128)(2,1)}) fusion(f32[512]{0:T(512)S(1)} %bitcast.184, f32[512]{0:T(512)S(1)} %bitcast.183, f32[]{:T(128)} %bitcast.118, f32[512]{0:T(512)} %bitcast.171, f32[512]{0:T(512)} %bitcast.159, f32[512]{0:T(512)} %bitcast.153, f32[512]{0:T(512)} %bitcast.165, ...), kind=kLoop, calls=%fused_computation.19 | loop fusion | flops 3670016 | bytes 1065476 | tf_op jit(solution)/shard_map/convert_element_type | solution.py:37
  153.3 12.0 %all-to-all-done.5 = f32[16,2,16,128]{3,2,1,0:T(8,128)S(1)} async-done(((f32[16,2,16,128]{3,2,1,0:T(8,128)}), f32[16,2,16,128]{3,2,1,0:T(8,128)S(1)}, u32[]{:S(2)}, u32[]{:S(2)}) %all-to-all-start.5) | async-done | bytes 262176 | tf_op jit(solution)/shard_map/all_to_all | solution.py:109
  165.4 0.7 broadcast_in_dim.162
  166.1 6.1 %all-to-all-start.6 = ((f32[16,2,16,128]{3,2,1,0:T(8,128)}), f32[16,2,16,128]{3,2,1,0:T(8,128)S(1)}, u32[]{:S(2)}, u32[]{:S(2)}) async-start(f32[16,2,16,128]{3,2,1,0:T(8,128)} %broadcast_in_dim.162), calls=%async_computation.6 | async-start | bytes 524288 | tf_op jit(solution)/shard_map/all_to_all | solution.py:109
  172.3 5.6 %multiply_convert_fusion = (bf16[512,512]{1,0:T(8,128)(2,1)}, bf16[512,512]{1,0:T(8,128)(2,1)}) fusion(f32[512]{0:T(512)S(1)} %bitcast.176, f32[512]{0:T(512)S(1)} %bitcast.175, f32[]{:T(128)} %bitcast.113, f32[512]{0:T(512)S(1)} %bitcast.172, f32[512]{0:T(512)S(1)} %bitcast.160, f32[512]{0:T(512)S(1)} %bitcast.154, f32[512]{0:T(512)S(1)} %bitcast.166, ...), kind=kLoop, calls=%fused_computation.14 | loop fusion | flops 3670016 | bytes 1065476 | tf_op jit(solution)/shard_map/convert_element_type | solution.py:37
  177.9 12.4 %all-to-all-done.6 = f32[16,2,16,128]{3,2,1,0:T(8,128)S(1)} async-done(((f32[16,2,16,128]{3,2,1,0:T(8,128)}), f32[16,2,16,128]{3,2,1,0:T(8,128)S(1)}, u32[]{:S(2)}, u32[]{:S(2)}) %all-to-all-start.6) | async-done | bytes 262176 | tf_op jit(solution)/shard_map/all_to_all | solution.py:109
  190.4 0.9 fusion.29
  191.3 1.4 fusion.27
  192.7 1.3 fusion.26
  194.1 1.3 fusion.25
  195.4 0.3 fusion.24
  195.7 0.3 fusion.23
  196.1 0.3 fusion.28
  196.4 0.3 fusion.5
  196.7 0.3 fusion.4
  197.0 0.3 fusion.3
  197.3 0.3 fusion.2
  197.6 0.1 copy-done.2
  197.7 0.3 fusion.1
  198.0 0.1 copy-done.3
  198.1 0.3 fusion
  198.4 49.1 %all_to_all.40 = f32[16,192,256]{2,1,0:T(8,128)S(1)} all-to-all(f32[16,192,256]{2,1,0:T(8,128)S(1)} %bitcast.138), channel_id=1, replica_groups=mesh['z'=16,'core'=2,'col'=16] {'col'}, dimensions={0} | all-to-all | bytes 6291456 | tf_op jit(solution)/shard_map/all_to_all | solution.py:223
  247.5 0.9 reduce_sum.39
  248.3 1.7 reshape.93
  (77 shorter events, 0.6 us)
Async XLA Ops:
  0.6 8.2 %copy-start = (f32[2,256,128]{2,1,0:T(8,128)S(1)}, f32[2,256,128]{2,1,0:T(8,128)}, u32[]{:S(2)}) copy-start(f32[2,256,128]{2,1,0:T(8,128)} %param.15) | copy-start | bytes 786436
  0.6 17.2 %copy-start.9 = (s32[2,256]{1,0:T(2,128)S(1)}, s32[2,256]{1,0:T(2,128)}, u32[]{:S(2)}) copy-start(s32[2,256]{1,0:T(2,128)} %param.19) | copy-start | bytes 6148
  0.7 17.2 %copy-start.8 = (f32[2,2,256]{2,1,0:T(2,128)S(1)}, f32[2,2,256]{2,1,0:T(2,128)}, u32[]{:S(2)}) copy-start(f32[2,2,256]{2,1,0:T(2,128)} %param.17) | copy-start | bytes 12292
  0.7 17.2 %copy-start.10 = (f32[2,256]{1,0:T(2,128)S(1)}, f32[2,256]{1,0:T(2,128)}, u32[]{:S(2)}) copy-start(f32[2,256]{1,0:T(2,128)} %param.18) | copy-start | bytes 6148
  0.7 40.4 %copy-start.1 = (f32[2,128,256]{2,1,0:T(8,128)S(1)}, f32[2,128,256]{2,1,0:T(8,128)}, u32[]{:S(2)}) copy-start(f32[2,128,256]{2,1,0:T(8,128)} %param.14) | copy-start | bytes 786436
  10.1 15.0 %all-to-all-start = ((f32[16,2,8,128]{3,2,1,0:T(8,128)}), f32[16,2,8,128]{3,2,1,0:T(8,128)S(1)}, u32[]{:S(2)}, u32[]{:S(2)}) async-start(f32[16,2,8,128]{3,2,1,0:T(8,128)} %copy.32), calls=%async_computation | async-start | bytes 262144 | tf_op jit(solution)/shard_map/all_to_all | solution.py:59
  17.9 66.4 %copy-start.19 = (pred[512]{0:T(512)(128)(4,1)}, pred[512]{0:T(512)(128)(4,1)S(1)}, u32[]{:S(2)}) copy-start(pred[512]{0:T(512)(128)(4,1)S(1)} %eq.30) | copy-start | bytes 1540
  17.9 66.4 %copy-start.11 = (f32[1,2,2,128]{3,1,2,0:T(2,128)}, f32[1,2,2,128]{3,1,2,0:T(2,128)S(1)}, u32[]{:S(2)}) copy-start(f32[1,2,2,128]{3,1,2,0:T(2,128)S(1)} %copy.46) | copy-start | bytes 6148
  17.9 66.4 %copy-start.13 = (f32[1,2,2,128]{3,1,2,0:T(2,128)}, f32[1,2,2,128]{3,1,2,0:T(2,128)S(1)}, u32[]{:S(2)}) copy-start(f32[1,2,2,128]{3,1,2,0:T(2,128)S(1)} %copy.47) | copy-start | bytes 6148
  17.9 66.3 %copy-start.15 = (f32[1,2,2,128]{3,1,2,0:T(2,128)}, f32[1,2,2,128]{3,1,2,0:T(2,128)S(1)}, u32[]{:S(2)}) copy-start(f32[1,2,2,128]{3,1,2,0:T(2,128)S(1)} %copy.45) | copy-start | bytes 6148
  18.0 66.3 %copy-start.17 = (f32[1,2,2,128]{3,1,2,0:T(2,128)}, f32[1,2,2,128]{3,1,2,0:T(2,128)S(1)}, u32[]{:S(2)}) copy-start(f32[1,2,2,128]{3,1,2,0:T(2,128)S(1)} %copy.48) | copy-start | bytes 6148
  25.8 27.9 %all-to-all-start.1 = ((f32[16,2,8,128]{3,2,1,0:T(8,128)}), f32[16,2,8,128]{3,2,1,0:T(8,128)}, u32[]{:S(2)}, u32[]{:S(2)}) async-start(f32[16,2,8,128]{3,2,1,0:T(8,128)} %broadcast_in_dim.152), calls=%async_computation.1 | async-start | bytes 262144 | tf_op jit(solution)/shard_map/all_to_all | solution.py:62
  41.0 36.6 %copy-start.7 = (f32[2,128,256]{2,1,0:T(8,128)S(1)}, f32[2,128,256]{2,1,0:T(8,128)}, u32[]{:S(2)}) copy-start(f32[2,128,256]{2,1,0:T(8,128)} %param.13) | copy-start | bytes 786436
  53.7 14.6 %all-to-all-start.2 = ((f32[16,2,8,128]{3,2,1,0:T(8,128)}), f32[16,2,8,128]{3,2,1,0:T(8,128)S(1)}, u32[]{:S(2)}, u32[]{:S(2)}) async-start(f32[16,2,8,128]{3,2,1,0:T(8,128)} %all-to-all-done.1), calls=%async_computation.2 | async-start | bytes 262144 | tf_op jit(solution)/shard_map/all_to_all | solution.py:59
  68.3 3.2 %collective-permute-start = (f32[2,128,128]{2,1,0:T(8,128)S(1)}, f32[2,128,128]{2,1,0:T(8,128)S(1)}, u32[]{:S(2)}, u32[]{:S(2)}) collective-permute-start(f32[2,128,128]{2,1,0:T(8,128)S(1)} %bitcast.148), channel_id=1, source_target_pairs={{0,16},{16,0},{1,17},{17,1},{2,18},{18,2},{3,19},{19,3},{4,20},{20... | collective-permute-start | bytes 393224 | tf_op jit(solution)/shard_map/ppermute | solution.py:77
  72.8 17.0 %all-to-all-start.3 = ((f32[16,2,8,128]{3,2,1,0:T(8,128)}), f32[16,2,8,128]{3,2,1,0:T(8,128)S(1)}, u32[]{:S(2)}, u32[]{:S(2)}) async-start(f32[16,2,8,128]{3,2,1,0:T(8,128)} %copy.37), calls=%async_computation.3 | async-start | bytes 262144 | tf_op jit(solution)/shard_map/all_to_all | solution.py:91
  78.0 37.0 %collective-permute-start.2 = (f32[2,128,128]{2,1,0:T(8,128)S(1)}, f32[2,128,128]{2,1,0:T(8,128)S(1)}, u32[]{:S(2)}, u32[]{:S(2)}) collective-permute-start(f32[2,128,128]{2,1,0:T(8,128)S(1)} %get-tuple-element.104), channel_id=1, source_target_pairs={{0,16},{1,48},{2,80},{3,112},{4,144},{5,176},{6,208},{7,240},{8,27... | collective-permute-start | bytes 393224 | tf_op jit(solution)/shard_map/ppermute | solution.py:134
  81.3 56.4 %collective-permute-start.1 = (f32[2,128,128]{2,1,0:T(8,128)S(1)}, f32[2,128,128]{2,1,0:T(8,128)S(1)}, u32[]{:S(2)}, u32[]{:S(2)}) collective-permute-start(f32[2,128,128]{2,1,0:T(8,128)S(1)} %get-tuple-element.105), channel_id=1, source_target_pairs={{0,0},{1,32},{2,64},{3,96},{4,128},{5,160},{6,192},{7,224},{8,256}... | collective-permute-start | bytes 393224 | tf_op jit(solution)/shard_map/ppermute | solution.py:133
  91.2 46.6 %all-to-all-start.4 = ((f32[16,2,8,128]{3,2,1,0:T(8,128)}), f32[16,2,8,128]{3,2,1,0:T(8,128)S(1)}, u32[]{:S(2)}, u32[]{:S(2)}) async-start(f32[16,2,8,128]{3,2,1,0:T(8,128)} %broadcast_in_dim.157), calls=%async_computation.4 | async-start | bytes 262144 | tf_op jit(solution)/shard_map/all_to_all | solution.py:97
  137.8 34.5 %copy-start.12 = (f32[1,2,2,128]{3,1,2,0:T(2,128)S(1)}, f32[1,2,2,128]{3,1,2,0:T(2,128)}, u32[]{:S(2)}) copy-start(f32[1,2,2,128]{3,1,2,0:T(2,128)} %copy-done.11) | copy-start | bytes 6148
  137.8 34.5 %copy-start.14 = (f32[1,2,2,128]{3,1,2,0:T(2,128)S(1)}, f32[1,2,2,128]{3,1,2,0:T(2,128)}, u32[]{:S(2)}) copy-start(f32[1,2,2,128]{3,1,2,0:T(2,128)} %copy-done.13) | copy-start | bytes 6148
  137.8 34.5 %copy-start.16 = (f32[1,2,2,128]{3,1,2,0:T(2,128)S(1)}, f32[1,2,2,128]{3,1,2,0:T(2,128)}, u32[]{:S(2)}) copy-start(f32[1,2,2,128]{3,1,2,0:T(2,128)} %copy-done.15) | copy-start | bytes 6148
  137.8 34.5 %copy-start.18 = (f32[1,2,2,128]{3,1,2,0:T(2,128)S(1)}, f32[1,2,2,128]{3,1,2,0:T(2,128)}, u32[]{:S(2)}) copy-start(f32[1,2,2,128]{3,1,2,0:T(2,128)} %copy-done.17) | copy-start | bytes 6148
  137.8 34.5 %copy-start.20 = (pred[512]{0:T(512)(128)(4,1)S(1)}, pred[512]{0:T(512)(128)(4,1)}, u32[]{:S(2)}) copy-start(pred[512]{0:T(512)(128)(4,1)} %copy-done.19) | copy-start | bytes 1540
  138.5 3.4 %collective-permute-start.3 = (f32[2,256,128]{2,1,0:T(8,128)S(1)}, f32[2,256,128]{2,1,0:T(8,128)S(1)}, u32[]{:S(2)}, u32[]{:S(2)}) collective-permute-start(f32[2,256,128]{2,1,0:T(8,128)S(1)} %fusion.44), channel_id=1, source_target_pairs={{0,16},{16,0},{1,17},{17,1},{2,18},{18,2},{3,19},{19,3},{4,20},{20... | collective-permute-start | bytes 786440 | tf_op jit(solution)/shard_map/ppermute | solution.py:106
  142.7 22.7 %all-to-all-start.5 = ((f32[16,2,16,128]{3,2,1,0:T(8,128)}), f32[16,2,16,128]{3,2,1,0:T(8,128)S(1)}, u32[]{:S(2)}, u32[]{:S(2)}) async-start(f32[16,2,16,128]{3,2,1,0:T(8,128)} %bitcast.110), calls=%async_computation.5 | async-start | bytes 524288 | tf_op jit(solution)/shard_map/all_to_all | solution.py:109
  166.1 24.2 %all-to-all-start.6 = ((f32[16,2,16,128]{3,2,1,0:T(8,128)}), f32[16,2,16,128]{3,2,1,0:T(8,128)S(1)}, u32[]{:S(2)}, u32[]{:S(2)}) async-start(f32[16,2,16,128]{3,2,1,0:T(8,128)} %broadcast_in_dim.162), calls=%async_computation.6 | async-start | bytes 524288 | tf_op jit(solution)/shard_map/all_to_all | solution.py:109
  190.4 5.1 %copy-start.5 = (bf16[512,512]{1,0:T(8,128)(2,1)S(1)}, bf16[512,512]{1,0:T(8,128)(2,1)}, u32[]{:S(2)}) copy-start(bf16[512,512]{1,0:T(8,128)(2,1)} %get-tuple-element.86) | copy-start | bytes 1572868
  191.2 4.5 %copy-start.6 = (bf16[512,512]{1,0:T(8,128)(2,1)S(1)}, bf16[512,512]{1,0:T(8,128)(2,1)}, u32[]{:S(2)}) copy-start(bf16[512,512]{1,0:T(8,128)(2,1)} %get-tuple-element.88) | copy-start | bytes 1572868
  191.3 4.8 %copy-start.4 = (bf16[512,512]{1,0:T(8,128)(2,1)S(1)}, bf16[512,512]{1,0:T(8,128)(2,1)}, u32[]{:S(2)}) copy-start(bf16[512,512]{1,0:T(8,128)(2,1)} %get-tuple-element.78) | copy-start | bytes 1572868
  196.7 1.0 copy-start.2
  197.0 1.1 copy-start.3

commit v9 on v6

--- a/solution.py
+++ b/solution.py
@@ -71,7 +71,8 @@
     spread = jnp.broadcast_to(summed[None], (n_z,) + summed.shape)
     gathered, out = beside(z_step, spread, works[1])
     outputs.append(out)
-    moved, out = beside(col_step, gathered, works[2])
+    last_work = works[2](outputs) if callable(works[2]) else works[2]
+    moved, out = beside(col_step, gathered, last_work)
     outputs.append(out)
     block = moved.transpose(1, 0, 2, 3).reshape(parts, rows, right)
     other = lax.ppermute(block, "core", [(0, 1), (1, 0)])
@@ -105,8 +106,11 @@
 
     depth_sq = src_depth * src_depth
     depth_term = jnp.exp(wave_value * src_depth)
-    lid_first = jnp.where(region_label == 1, lid_table[1, 0], lid_table[0, 0])
-    lid_second = jnp.where(region_label == 1, lid_table[1, 1], lid_table[0, 1])
+    def lids(region):
+        return (
+            jnp.where(region == 1, lid_table[1, 0], lid_table[0, 0]),
+            jnp.where(region == 1, lid_table[1, 1], lid_table[0, 1]),
+        )
 
     def tile_chunk(point_xy, first, second):
         return green_tile(
@@ -125,20 +129,24 @@
     field_rows = field_xy.shape[1]
     n_chunks = 6
     chunk_rows = field_rows // n_chunks
-    works = [
-        (
-            (
-                field_xy[:, i * chunk_rows : (i + 1) * chunk_rows],
-                lid_first[i * chunk_rows : (i + 1) * chunk_rows],
-                lid_second[i * chunk_rows : (i + 1) * chunk_rows],
-            ),
-            tile_chunk,
-        )
-        for i in range(n_chunks)
-    ]
+    def first_chunk(point_xy, region):
+        lid_first, lid_second = lids(region)
+        tile = tile_chunk(point_xy[:, :chunk_rows], lid_first[:chunk_rows], lid_second[:chunk_rows])
+        return tile, (lid_first, lid_second)
+
+    top_partial = complex_product(stacked_matrix(inv_top), rhs_top)
+    works = [((field_xy, region_label), first_chunk)] + [None] * (n_chunks - 1)
+
+    def chunk_work(i, lid_pair):
+        rows = slice(i * chunk_rows, (i + 1) * chunk_rows)
+        return ((field_xy[:, rows], lid_pair[0][rows], lid_pair[1][rows]), tile_chunk)
+
     top_solved, tiles_a = col_sum_to_columns(
-        complex_product(stacked_matrix(inv_top), rhs_top), works=(works[0], None, works[1])
-    )
+        top_partial, works=(works[0], None, lambda done: chunk_work(1, done[0][1]))
+    )
+    lid_pair = tiles_a[0][1]
+    tiles_a = [tiles_a[0][0], tiles_a[1]]
+    works = [None] + [chunk_work(i, lid_pair) for i in range(1, n_chunks)]
     remainder_cols, tiles_b = col_sum_to_columns(
         complex_product(stacked_matrix(lower_panel), top_solved),
         rhs_bottom,

time: 223 us -> 221 us (level)
  transfers between devices with their start and end apart: 11 -> 11, of which waited for: 11 -> 10; matrix products, arithmetic and copies ran while one was open for 15% -> 17% of each run, Pallas kernels for 0% -> 0%
where the time goes in v9:
time: 221 us; the launch traced here: 220 us
  starting transfers between devices  74.2 us (34%)
  blocking collectives  58.8 us (27%)
  other arithmetic  39.7 us (18%)
  waiting for transfers between devices  33.1 us (15%)
  local copies, waits for them, and re-layouts  7.01 us (3%)
  matrix products  5.31 us (2%)
    all_to_all x1, blocking collectives, per_device(): summed = lax.all_to_all(split, 'col', 0, 0, tiled=True).sum(0)  43.2 us
    all_to_all x6, starting transfers between devices, col_step(): return lax.all_to_all(value, 'col', 0, 0, tiled=True)  33.9 us
    convert_element_type x6, other arithmetic, green_tile(): (amplitude * jnp.sin(phase_angle)).astype(jnp.bfloat16)  33.3 us
    all_to_all x2, waiting for transfers between devices, z_step(): return lax.all_to_all(value, 'z', 0, 0, tiled=True)  23.9 us
    ppermute x3, starting transfers between devices, col_sum_to_columns(): other = lax.ppermute(block, 'core', [(0, 1), (1, 0)])  21.2 us
    all_to_all x2, starting transfers between devices, z_step(): return lax.all_to_all(value, 'z', 0, 0, tiled=True)  19.1 us
    all_to_all x1, blocking collectives, z_step(): return lax.all_to_all(value, 'z', 0, 0, tiled=True)  15.7 us
    all_to_all x6, waiting for transfers between devices, col_step(): return lax.all_to_all(value, 'col', 0, 0, tiled=True)  6.42 us
  transfers between devices with their start and end apart: 11, of which 10 were waited for; matrix products, arithmetic and copies ran while one was open for 17% of the time, Pallas kernels for 0%

profile of v9, /device:TPU:1, one launch (start us, length us, event | category | flops | bytes accessed | tf_op | source)
XLA Modules:
  0.0 220.1 jit_solution(12461880581456538877)
XLA Ops:
  0.6 0.0 copy-start
  0.6 0.0 copy-start.10
  0.7 0.0 copy-start.11
  0.7 0.0 copy-start.14
  0.7 1.0 fusion.18
  1.7 1.0 slice_bitcast_fusion.4
  2.8 0.6 convolution_bitcast_fusion.2
  3.4 0.7 copy.17
  4.1 7.6 %all-to-all-start = ((f32[16,2,8,128]{3,2,1,0:T(8,128)}), f32[16,2,8,128]{3,2,1,0:T(8,128)S(1)}, u32[]{:S(2)}, u32[]{:S(2)}) async-start(f32[16,2,8,128]{3,2,1,0:T(8,128)} %copy.17), calls=%async_computation | async-start | bytes 262144 | tf_op jit(solution)/shard_map/all_to_all | solution.py:59
  12.3 0.6 fusion.39
  13.1 1.3 broadcast_select_fusion.7
  14.4 1.2 broadcast_select_fusion.6
  15.6 5.5 %multiply_convert_fusion.10 = (bf16[512,512]{1,0:T(8,128)(2,1)S(1)}, bf16[512,512]{1,0:T(8,128)(2,1)}) fusion(f32[]{:T(128)} %bitcast.126, f32[512]{0:T(512)S(1)} %bitcast.177, f32[512]{0:T(512)S(1)} %bitcast.165, f32[512]{0:T(512)S(1)} %bitcast.186, f32[512]{0:T(512)S(1)} %bitcast.159, f32[512]{0:T(512)S(1)} %bitcast.185, f32[512]{0:T(512)S(1)} %bitcast.171, ...), kind=kLoop, calls=%fused_computation.40 | loop fusion | flops 3670016 | bytes 1065476 | tf_op jit(solution)/shard_map/convert_element_type | solution.py:37
  21.1 0.0 all-to-all-done
  21.1 0.7 broadcast_in_dim.152
  21.8 15.0 %all-to-all-start.1 = ((f32[16,2,8,128]{3,2,1,0:T(8,128)}), f32[16,2,8,128]{3,2,1,0:T(8,128)}, u32[]{:S(2)}, u32[]{:S(2)}) async-start(f32[16,2,8,128]{3,2,1,0:T(8,128)} %broadcast_in_dim.152), calls=%async_computation.1 | async-start | bytes 262144 | tf_op jit(solution)/shard_map/all_to_all | solution.py:62
  36.8 11.9 %all-to-all-done.1 = f32[16,2,8,128]{3,2,1,0:T(8,128)} async-done(((f32[16,2,8,128]{3,2,1,0:T(8,128)}), f32[16,2,8,128]{3,2,1,0:T(8,128)}, u32[]{:S(2)}, u32[]{:S(2)}) %all-to-all-start.1) | async-done | bytes 131104 | tf_op jit(solution)/shard_map/all_to_all | solution.py:62
  48.8 6.7 %all-to-all-start.2 = ((f32[16,2,8,128]{3,2,1,0:T(8,128)}), f32[16,2,8,128]{3,2,1,0:T(8,128)S(1)}, u32[]{:S(2)}, u32[]{:S(2)}) async-start(f32[16,2,8,128]{3,2,1,0:T(8,128)} %all-to-all-done.1), calls=%async_computation.2 | async-start | bytes 262144 | tf_op jit(solution)/shard_map/all_to_all | solution.py:59
  55.5 5.5 %multiply_convert_fusion.8 = (bf16[512,512]{1,0:T(8,128)(2,1)S(1)}, bf16[512,512]{1,0:T(8,128)(2,1)}) fusion(f32[512]{0:T(512)S(1)} %bitcast.188, f32[512]{0:T(512)S(1)} %bitcast.187, f32[]{:T(128)} %bitcast.127, f32[512]{0:T(512)S(1)} %bitcast.178, f32[512]{0:T(512)S(1)} %bitcast.166, f32[512]{0:T(512)S(1)} %bitcast.160, f32[512]{0:T(512)S(1)} %bitcast.172, ...), kind=kLoop, calls=%fused_computation.35 | loop fusion | flops 3670016 | bytes 1065476 | tf_op jit(solution)/shard_map/convert_element_type | solution.py:37
  61.0 1.3 all-to-all-done.2
  62.3 7.3 %collective-permute-start = (f32[2,128,128]{2,1,0:T(8,128)S(1)}, f32[2,128,128]{2,1,0:T(8,128)S(1)}, u32[]{:S(2)}, u32[]{:S(2)}) collective-permute-start(f32[2,128,128]{2,1,0:T(8,128)S(1)} %bitcast.156), channel_id=1, source_target_pairs={{0,16},{16,0},{1,17},{17,1},{2,18},{18,2},{3,19},{19,3},{4,20},{20... | collective-permute-start | bytes 393224 | tf_op jit(solution)/shard_map/ppermute | solution.py:78
  69.7 0.9 collective-permute-done
  70.6 0.6 convolution_bitcast_fusion.1
  71.2 0.7 copy.19
  71.9 4.5 %all-to-all-start.3 = ((f32[16,2,8,128]{3,2,1,0:T(8,128)}), f32[16,2,8,128]{3,2,1,0:T(8,128)S(1)}, u32[]{:S(2)}, u32[]{:S(2)}) async-start(f32[16,2,8,128]{3,2,1,0:T(8,128)} %copy.19), calls=%async_computation.3 | async-start | bytes 262144 | tf_op jit(solution)/shard_map/all_to_all | solution.py:59
  76.4 5.5 %multiply_convert_fusion.6 = (bf16[512,512]{1,0:T(8,128)(2,1)S(1)}, bf16[512,512]{1,0:T(8,128)(2,1)}) fusion(f32[512]{0:T(512)S(1)} %bitcast.190, f32[512]{0:T(512)S(1)} %bitcast.189, f32[]{:T(128)} %bitcast.128, f32[512]{0:T(512)S(1)} %bitcast.179, f32[512]{0:T(512)S(1)} %bitcast.167, f32[512]{0:T(512)S(1)} %bitcast.161, f32[512]{0:T(512)S(1)} %bitcast.173, ...), kind=kLoop, calls=%fused_computation.30 | loop fusion | flops 3670016 | bytes 1065476 | tf_op jit(solution)/shard_map/convert_element_type | solution.py:37
  81.9 1.3 all-to-all-done.3
  83.2 0.7 dynamic-slice_subtract_fusion
  84.0 0.7 broadcast_in_dim.157
  84.6 4.2 %all-to-all-start.4 = ((f32[16,2,8,128]{3,2,1,0:T(8,128)}), f32[16,2,8,128]{3,2,1,0:T(8,128)}, u32[]{:S(2)}, u32[]{:S(2)}) async-start(f32[16,2,8,128]{3,2,1,0:T(8,128)} %broadcast_in_dim.157), calls=%async_computation.4 | async-start | bytes 262144 | tf_op jit(solution)/shard_map/all_to_all | solution.py:62
  88.8 11.9 %all-to-all-done.4 = f32[16,2,8,128]{3,2,1,0:T(8,128)} async-done(((f32[16,2,8,128]{3,2,1,0:T(8,128)}), f32[16,2,8,128]{3,2,1,0:T(8,128)}, u32[]{:S(2)}, u32[]{:S(2)}) %all-to-all-start.4) | async-done | bytes 131104 | tf_op jit(solution)/shard_map/all_to_all | solution.py:62
  100.8 5.3 %all-to-all-start.5 = ((f32[16,2,8,128]{3,2,1,0:T(8,128)}), f32[16,2,8,128]{3,2,1,0:T(8,128)S(1)}, u32[]{:S(2)}, u32[]{:S(2)}) async-start(f32[16,2,8,128]{3,2,1,0:T(8,128)} %all-to-all-done.4), calls=%async_computation.5 | async-start | bytes 262144 | tf_op jit(solution)/shard_map/all_to_all | solution.py:59
  106.1 5.5 %multiply_convert_fusion.4 = (bf16[512,512]{1,0:T(8,128)(2,1)S(1)}, bf16[512,512]{1,0:T(8,128)(2,1)}) fusion(f32[512]{0:T(512)S(1)} %bitcast.192, f32[512]{0:T(512)S(1)} %bitcast.191, f32[]{:T(128)} %bitcast.129, f32[512]{0:T(512)S(1)} %bitcast.180, f32[512]{0:T(512)S(1)} %bitcast.168, f32[512]{0:T(512)S(1)} %bitcast.162, f32[512]{0:T(512)S(1)} %bitcast.174, ...), kind=kLoop, calls=%fused_computation.25 | loop fusion | flops 3670016 | bytes 1065476 | tf_op jit(solution)/shard_map/convert_element_type | solution.py:37
  111.7 1.3 all-to-all-done.5
  113.0 6.8 %collective-permute-start.1 = (f32[2,128,128]{2,1,0:T(8,128)S(1)}, f32[2,128,128]{2,1,0:T(8,128)S(1)}, u32[]{:S(2)}, u32[]{:S(2)}) collective-permute-start(f32[2,128,128]{2,1,0:T(8,128)S(1)} %bitcast.157), channel_id=1, source_target_pairs={{0,16},{16,0},{1,17},{17,1},{2,18},{18,2},{3,19},{19,3},{4,20},{20... | collective-permute-start | bytes 393224 | tf_op jit(solution)/shard_map/ppermute | solution.py:78
  119.8 0.9 collective-permute-done.1
  120.8 0.6 convolution_bitcast_fusion
  121.4 0.7 copy.21
  122.0 4.5 %all-to-all-start.6 = ((f32[16,2,8,128]{3,2,1,0:T(8,128)}), f32[16,2,8,128]{3,2,1,0:T(8,128)S(1)}, u32[]{:S(2)}, u32[]{:S(2)}) async-start(f32[16,2,8,128]{3,2,1,0:T(8,128)} %copy.21), calls=%async_computation.6 | async-start | bytes 262144 | tf_op jit(solution)/shard_map/all_to_all | solution.py:59
  126.5 5.5 %multiply_convert_fusion.2 = (bf16[512,512]{1,0:T(8,128)(2,1)S(1)}, bf16[512,512]{1,0:T(8,128)(2,1)}) fusion(f32[512]{0:T(512)S(1)} %bitcast.194, f32[512]{0:T(512)S(1)} %bitcast.193, f32[]{:T(128)} %bitcast.130, f32[512]{0:T(512)S(1)} %bitcast.181, f32[512]{0:T(512)S(1)} %bitcast.169, f32[512]{0:T(512)S(1)} %bitcast.163, f32[512]{0:T(512)S(1)} %bitcast.175, ...), kind=kLoop, calls=%fused_computation.20 | loop fusion | flops 3670016 | bytes 1065476 | tf_op jit(solution)/shard_map/convert_element_type | solution.py:37
  132.1 1.3 all-to-all-done.6
  133.4 15.7 %all_to_all.50 = f32[16,2,8,128]{3,2,1,0:T(8,128)} all-to-all(f32[16,2,8,128]{3,2,1,0:T(8,128)S(1)} %broadcast_in_dim.162), channel_id=1, replica_groups=mesh['z'=16,'core'=2,'col'=16] {'z'}, dimensions={0} | all-to-all | bytes 262144 | tf_op jit(solution)/shard_map/all_to_all | solution.py:62
  149.1 5.4 %all-to-all-start.8 = ((f32[16,2,8,128]{3,2,1,0:T(8,128)}), f32[16,2,8,128]{3,2,1,0:T(8,128)S(1)}, u32[]{:S(2)}, u32[]{:S(2)}) async-start(f32[16,2,8,128]{3,2,1,0:T(8,128)} %all_to_all.50), calls=%async_computation.8 | async-start | bytes 262144 | tf_op jit(solution)/shard_map/all_to_all | solution.py:59
  154.5 5.6 %multiply_convert_fusion = (bf16[512,512]{1,0:T(8,128)(2,1)}, bf16[512,512]{1,0:T(8,128)(2,1)}) fusion(f32[512]{0:T(512)S(1)} %bitcast.184, f32[512]{0:T(512)S(1)} %bitcast.183, f32[]{:T(128)} %bitcast.125, f32[512]{0:T(512)S(1)} %bitcast.182, f32[512]{0:T(512)S(1)} %bitcast.170, f32[512]{0:T(512)S(1)} %bitcast.164, f32[512]{0:T(512)S(1)} %bitcast.176, ...), kind=kLoop, calls=%fused_computation.15 | loop fusion | flops 3670016 | bytes 1065476 | tf_op jit(solution)/shard_map/convert_element_type | solution.py:37
  160.1 1.2 all-to-all-done.8
  161.3 7.2 %collective-permute-start.2 = (f32[2,128,128]{2,1,0:T(8,128)S(1)}, f32[2,128,128]{2,1,0:T(8,128)S(1)}, u32[]{:S(2)}, u32[]{:S(2)}) collective-permute-start(f32[2,128,128]{2,1,0:T(8,128)S(1)} %bitcast.158), channel_id=1, source_target_pairs={{0,16},{16,0},{1,17},{17,1},{2,18},{18,2},{3,19},{19,3},{4,20},{20... | collective-permute-start | bytes 393224 | tf_op jit(solution)/shard_map/ppermute | solution.py:78
  168.5 1.0 collective-permute-done.2
  169.5 0.9 fusion.28
  170.4 0.3 fusion.26
  170.8 0.3 fusion.25
  171.1 0.3 fusion.24
  171.4 0.3 fusion.23
  171.7 0.3 fusion.22
  172.0 0.3 fusion.27
  172.3 0.3 fusion.5
  172.6 0.3 fusion.4
  172.9 0.3 fusion.3
  173.2 0.3 fusion.2
  173.5 0.3 fusion.1
  173.9 0.1 copy-done.3
  174.0 0.3 fusion
  174.3 43.2 %all_to_all.51 = f32[16,192,256]{2,1,0:T(8,128)S(1)} all-to-all(f32[16,192,256]{2,1,0:T(8,128)S(1)} %bitcast.150), channel_id=1, replica_groups=mesh['z'=16,'core'=2,'col'=16] {'col'}, dimensions={0} | all-to-all | bytes 6291456 | tf_op jit(solution)/shard_map/all_to_all | solution.py:177
  217.5 0.9 reduce_sum.39
  218.3 1.7 reshape.92
  (67 shorter events, 0.6 us)
Async XLA Ops:
  0.6 2.2 copy-start
  0.6 12.4 %copy-start.10 = (f32[2,3072]{1,0:T(2,128)S(1)}, f32[2,3072]{1,0:T(2,128)}, u32[]{:S(2)}) copy-start(f32[2,3072]{1,0:T(2,128)} %param.20) | copy-start | bytes 73732
  0.7 12.4 %copy-start.11 = (s32[3072]{0:T(1024)S(1)}, s32[3072]{0:T(1024)}, u32[]{:S(2)}) copy-start(s32[3072]{0:T(1024)} %param.21) | copy-start | bytes 36868
  0.7 11.6 %copy-start.14 = (s32[2,256]{1,0:T(2,128)S(1)}, s32[2,256]{1,0:T(2,128)}, u32[]{:S(2)}) copy-start(s32[2,256]{1,0:T(2,128)} %param.19) | copy-start | bytes 6148
  0.7 11.7 %copy-start.13 = (f32[2,2]{1,0:T(2,128)S(1)}, f32[2,2]{1,0:T(2,128)}, u32[]{:S(2)}) copy-start(f32[2,2]{1,0:T(2,128)} %param.22) | copy-start | bytes 52
  0.7 12.3 %copy-start.12 = (f32[2,2,256]{2,1,0:T(2,128)S(1)}, f32[2,2,256]{2,1,0:T(2,128)}, u32[]{:S(2)}) copy-start(f32[2,2,256]{2,1,0:T(2,128)} %param.17) | copy-start | bytes 12292
  0.7 12.3 %copy-start.15 = (f32[2,256]{1,0:T(2,128)S(1)}, f32[2,256]{1,0:T(2,128)}, u32[]{:S(2)}) copy-start(f32[2,256]{1,0:T(2,128)} %param.18) | copy-start | bytes 6148
  0.7 36.1 %copy-start.1 = (f32[2,128,256]{2,1,0:T(8,128)S(1)}, f32[2,128,256]{2,1,0:T(8,128)}, u32[]{:S(2)}) copy-start(f32[2,128,256]{2,1,0:T(8,128)} %param.14) | copy-start | bytes 786436
  4.1 17.0 %all-to-all-start = ((f32[16,2,8,128]{3,2,1,0:T(8,128)}), f32[16,2,8,128]{3,2,1,0:T(8,128)S(1)}, u32[]{:S(2)}, u32[]{:S(2)}) async-start(f32[16,2,8,128]{3,2,1,0:T(8,128)} %copy.17), calls=%async_computation | async-start | bytes 262144 | tf_op jit(solution)/shard_map/all_to_all | solution.py:59
  21.8 27.0 %all-to-all-start.1 = ((f32[16,2,8,128]{3,2,1,0:T(8,128)}), f32[16,2,8,128]{3,2,1,0:T(8,128)}, u32[]{:S(2)}, u32[]{:S(2)}) async-start(f32[16,2,8,128]{3,2,1,0:T(8,128)} %broadcast_in_dim.152), calls=%async_computation.1 | async-start | bytes 262144 | tf_op jit(solution)/shard_map/all_to_all | solution.py:62
  48.8 13.5 %all-to-all-start.2 = ((f32[16,2,8,128]{3,2,1,0:T(8,128)}), f32[16,2,8,128]{3,2,1,0:T(8,128)S(1)}, u32[]{:S(2)}, u32[]{:S(2)}) async-start(f32[16,2,8,128]{3,2,1,0:T(8,128)} %all-to-all-done.1), calls=%async_computation.2 | async-start | bytes 262144 | tf_op jit(solution)/shard_map/all_to_all | solution.py:59
  62.3 26.5 %copy-start.2 = (f32[2,128,256]{2,1,0:T(8,128)S(1)}, f32[2,128,256]{2,1,0:T(8,128)}, u32[]{:S(2)}) copy-start(f32[2,128,256]{2,1,0:T(8,128)} %param.13) | copy-start | bytes 786436
  62.3 8.2 %collective-permute-start = (f32[2,128,128]{2,1,0:T(8,128)S(1)}, f32[2,128,128]{2,1,0:T(8,128)S(1)}, u32[]{:S(2)}, u32[]{:S(2)}) collective-permute-start(f32[2,128,128]{2,1,0:T(8,128)S(1)} %bitcast.156), channel_id=1, source_target_pairs={{0,16},{16,0},{1,17},{17,1},{2,18},{18,2},{3,19},{19,3},{4,20},{20... | collective-permute-start | bytes 393224 | tf_op jit(solution)/shard_map/ppermute | solution.py:78
  71.9 11.3 %all-to-all-start.3 = ((f32[16,2,8,128]{3,2,1,0:T(8,128)}), f32[16,2,8,128]{3,2,1,0:T(8,128)S(1)}, u32[]{:S(2)}, u32[]{:S(2)}) async-start(f32[16,2,8,128]{3,2,1,0:T(8,128)} %copy.19), calls=%async_computation.3 | async-start | bytes 262144 | tf_op jit(solution)/shard_map/all_to_all | solution.py:59
  84.6 16.2 %all-to-all-start.4 = ((f32[16,2,8,128]{3,2,1,0:T(8,128)}), f32[16,2,8,128]{3,2,1,0:T(8,128)}, u32[]{:S(2)}, u32[]{:S(2)}) async-start(f32[16,2,8,128]{3,2,1,0:T(8,128)} %broadcast_in_dim.157), calls=%async_computation.4 | async-start | bytes 262144 | tf_op jit(solution)/shard_map/all_to_all | solution.py:62
  100.8 12.2 %all-to-all-start.5 = ((f32[16,2,8,128]{3,2,1,0:T(8,128)}), f32[16,2,8,128]{3,2,1,0:T(8,128)S(1)}, u32[]{:S(2)}, u32[]{:S(2)}) async-start(f32[16,2,8,128]{3,2,1,0:T(8,128)} %all-to-all-done.4), calls=%async_computation.5 | async-start | bytes 262144 | tf_op jit(solution)/shard_map/all_to_all | solution.py:59
  113.0 7.8 %collective-permute-start.1 = (f32[2,128,128]{2,1,0:T(8,128)S(1)}, f32[2,128,128]{2,1,0:T(8,128)S(1)}, u32[]{:S(2)}, u32[]{:S(2)}) collective-permute-start(f32[2,128,128]{2,1,0:T(8,128)S(1)} %bitcast.157), channel_id=1, source_target_pairs={{0,16},{16,0},{1,17},{17,1},{2,18},{18,2},{3,19},{19,3},{4,20},{20... | collective-permute-start | bytes 393224 | tf_op jit(solution)/shard_map/ppermute | solution.py:78
  122.0 11.3 %all-to-all-start.6 = ((f32[16,2,8,128]{3,2,1,0:T(8,128)}), f32[16,2,8,128]{3,2,1,0:T(8,128)S(1)}, u32[]{:S(2)}, u32[]{:S(2)}) async-start(f32[16,2,8,128]{3,2,1,0:T(8,128)} %copy.21), calls=%async_computation.6 | async-start | bytes 262144 | tf_op jit(solution)/shard_map/all_to_all | solution.py:59
  149.1 12.2 %all-to-all-start.8 = ((f32[16,2,8,128]{3,2,1,0:T(8,128)}), f32[16,2,8,128]{3,2,1,0:T(8,128)S(1)}, u32[]{:S(2)}, u32[]{:S(2)}) async-start(f32[16,2,8,128]{3,2,1,0:T(8,128)} %all_to_all.50), calls=%async_computation.8 | async-start | bytes 262144 | tf_op jit(solution)/shard_map/all_to_all | solution.py:59
  161.3 9.1 %copy-start.5 = (bf16[512,512]{1,0:T(8,128)(2,1)S(1)}, bf16[512,512]{1,0:T(8,128)(2,1)}, u32[]{:S(2)}) copy-start(bf16[512,512]{1,0:T(8,128)(2,1)} %get-tuple-element.78) | copy-start | bytes 1572868
  161.3 9.4 %copy-start.6 = (bf16[512,512]{1,0:T(8,128)(2,1)S(1)}, bf16[512,512]{1,0:T(8,128)(2,1)}, u32[]{:S(2)}) copy-start(bf16[512,512]{1,0:T(8,128)(2,1)} %get-tuple-element.80) | copy-start | bytes 1572868
  161.3 9.8 %copy-start.7 = (bf16[512,512]{1,0:T(8,128)(2,1)S(1)}, bf16[512,512]{1,0:T(8,128)(2,1)}, u32[]{:S(2)}) copy-start(bf16[512,512]{1,0:T(8,128)(2,1)} %get-tuple-element.82) | copy-start | bytes 1572868
  161.3 8.1 %collective-permute-start.2 = (f32[2,128,128]{2,1,0:T(8,128)S(1)}, f32[2,128,128]{2,1,0:T(8,128)S(1)}, u32[]{:S(2)}, u32[]{:S(2)}) collective-permute-start(f32[2,128,128]{2,1,0:T(8,128)S(1)} %bitcast.158), channel_id=1, source_target_pairs={{0,16},{16,0},{1,17},{17,1},{2,18},{18,2},{3,19},{19,3},{4,20},{20... | collective-permute-start | bytes 393224 | tf_op jit(solution)/shard_map/ppermute | solution.py:78
  169.5 1.9 copy-start.8
  170.4 1.3 copy-start.9
  170.4 1.6 copy-start.4
  172.9 1.0 copy-start.3

commit v10 on v9

--- a/solution.py
+++ b/solution.py
@@ -69,7 +69,8 @@
         start = lax.axis_index("col") * piece
         summed = lax.dynamic_slice_in_dim(offset, start, piece, 1) - summed
     spread = jnp.broadcast_to(summed[None], (n_z,) + summed.shape)
-    gathered, out = beside(z_step, spread, works[1])
+    middle_work = works[1](outputs) if callable(works[1]) else works[1]
+    gathered, out = beside(z_step, spread, middle_work)
     outputs.append(out)
     last_work = works[2](outputs) if callable(works[2]) else works[2]
     moved, out = beside(col_step, gathered, last_work)
@@ -137,24 +138,27 @@
     top_partial = complex_product(stacked_matrix(inv_top), rhs_top)
     works = [((field_xy, region_label), first_chunk)] + [None] * (n_chunks - 1)
 
-    def chunk_work(i, lid_pair):
-        rows = slice(i * chunk_rows, (i + 1) * chunk_rows)
+    def chunk_work(first, last, lid_pair):
+        rows = slice(first * chunk_rows, last * chunk_rows)
         return ((field_xy[:, rows], lid_pair[0][rows], lid_pair[1][rows]), tile_chunk)
 
     top_solved, tiles_a = col_sum_to_columns(
-        top_partial, works=(works[0], None, lambda done: chunk_work(1, done[0][1]))
+        top_partial,
+        works=(
+            works[0],
+            lambda done: chunk_work(1, 3, done[0][1]),
+            lambda done: chunk_work(3, 4, done[0][1]),
+        ),
     )
     lid_pair = tiles_a[0][1]
-    tiles_a = [tiles_a[0][0], tiles_a[1]]
-    works = [None] + [chunk_work(i, lid_pair) for i in range(1, n_chunks)]
+    tiles_a = [tiles_a[0][0]] + tiles_a[1:]
     remainder_cols, tiles_b = col_sum_to_columns(
         complex_product(stacked_matrix(lower_panel), top_solved),
         rhs_bottom,
-        works=(works[2], None, works[3]),
+        works=(chunk_work(4, 5, lid_pair), None, chunk_work(5, 6, lid_pair)),
     )
     bottom_solved, tiles_c = col_sum_to_columns(
-        complex_product(stacked_matrix(inv_bottom), remainder_cols),
-        works=(works[4], None, works[5]),
+        complex_product(stacked_matrix(inv_bottom), remainder_cols)
     )
     tile_chunks = tiles_a + tiles_b + tiles_c
     strengths = jnp.stack([top_solved, bottom_solved])

time: 221 us -> 226 us (1.023)
  blocking collectives: 58.8 us -> 78.9 us
  waiting for transfers between devices: 33.1 us -> 17.1 us
  starting transfers between devices: 74.2 us -> 68.3 us
  local copies, waits for them, and re-layouts: 7.01 us -> 11.4 us
  other arithmetic: 39.7 us -> 42.6 us
    all_to_all x0 -> x2, blocking collectives: none -> 21.9 us  [col_step(): return lax.all_to_all(value, 'col', 0, 0, tiled=True)]
    all_to_all x2, waiting for transfers between devices: 23.9 us -> 13.9 us  [z_step(): return lax.all_to_all(value, 'z', 0, 0, tiled=True)]
    all_to_all x6 -> x4, starting transfers between devices: 33.9 us -> 25.1 us  [col_step(): return lax.all_to_all(value, 'col', 0, 0, tiled=True)]
    all_to_all x6 -> x4, waiting for transfers between devices: 6.42 us -> 2.03 us  [col_step(): return lax.all_to_all(value, 'col', 0, 0, tiled=True)]
    all_to_all x2, starting transfers between devices: 19.1 us -> 21.8 us  [z_step(): return lax.all_to_all(value, 'z', 0, 0, tiled=True)]
    convert_element_type x6 -> x5, other arithmetic: 33.3 us -> 33.3 us  [green_tile(): (amplitude * jnp.sin(phase_angle)).astype(jnp.bfloat16)]
  transfers between devices with their start and end apart: 11 -> 9, of which waited for: 10 -> 7; matrix products, arithmetic and copies ran while one was open for 17% -> 18% of each run, Pallas kernels for 0% -> 0%
where the time goes in v10:
time: 226 us; the launch traced here: 225 us
  blocking collectives  78.9 us (35%)
  starting transfers between devices  68.3 us (30%)
  other arithmetic  42.6 us (19%)
  waiting for transfers between devices  17.1 us (8%)
  local copies, waits for them, and re-layouts  11.4 us (5%)
  matrix products  4.98 us (2%)
    all_to_all x1, blocking collectives, per_device(): summed = lax.all_to_all(split, 'col', 0, 0, tiled=True).sum(0)  41.6 us
    convert_element_type x5, other arithmetic, green_tile(): (amplitude * jnp.sin(phase_angle)).astype(jnp.bfloat16)  33.3 us
    all_to_all x4, starting transfers between devices, col_step(): return lax.all_to_all(value, 'col', 0, 0, tiled=True)  25.1 us
    all_to_all x2, blocking collectives, col_step(): return lax.all_to_all(value, 'col', 0, 0, tiled=True)  21.9 us
    all_to_all x2, starting transfers between devices, z_step(): return lax.all_to_all(value, 'z', 0, 0, tiled=True)  21.8 us
    ppermute x3, starting transfers between devices, col_sum_to_columns(): other = lax.ppermute(block, 'core', [(0, 1), (1, 0)])  21.4 us
    all_to_all x1, blocking collectives, z_step(): return lax.all_to_all(value, 'z', 0, 0, tiled=True)  15.3 us
    all_to_all x2, waiting for transfers between devices, z_step(): return lax.all_to_all(value, 'z', 0, 0, tiled=True)  13.9 us
  transfers between devices with their start and end apart: 9, of which 7 were waited for; matrix products, arithmetic and copies ran while one was open for 18% of the time, Pallas kernels for 0%

profile of v10, /device:TPU:1, one launch (start us, length us, event | category | flops | bytes accessed | tf_op | source)
XLA Modules:
  0.0 225.3 jit_solution(2927414134499902479)
XLA Ops:
  0.6 0.0 copy-start
  0.7 1.0 fusion.15
  1.7 1.0 slice_bitcast_fusion.4
  2.8 0.6 convolution_bitcast_fusion.2
  3.4 0.7 copy.17
  4.1 7.6 %all-to-all-start = ((f32[16,2,8,128]{3,2,1,0:T(8,128)}), f32[16,2,8,128]{3,2,1,0:T(8,128)S(1)}, u32[]{:S(2)}, u32[]{:S(2)}) async-start(f32[16,2,8,128]{3,2,1,0:T(8,128)} %copy.17), calls=%async_computation | async-start | bytes 262144 | tf_op jit(solution)/shard_map/all_to_all | solution.py:59
  12.4 0.6 fusion.34
  13.1 1.2 broadcast_select_fusion.7
  14.4 1.3 broadcast_select_fusion.6
  15.7 0.7 slice_bitcast_fusion
  16.4 5.5 %multiply_convert_fusion.8 = (bf16[512,512]{1,0:T(8,128)(2,1)S(1)}, bf16[512,512]{1,0:T(8,128)(2,1)}) fusion(f32[]{:T(128)} %bitcast.124, f32[512]{0:T(512)S(1)} %bitcast.167, f32[512]{0:T(512)S(1)} %bitcast.157, f32[512]{0:T(512)S(1)} %bitcast.173, f32[512]{0:T(512)S(1)} %bitcast.152, f32[512]{0:T(512)S(1)} %bitcast.172, f32[512]{0:T(512)S(1)} %bitcast.162, ...), kind=kLoop, calls=%fused_computation.33 | loop fusion | flops 3670016 | bytes 1065476 | tf_op jit(solution)/shard_map/convert_element_type | solution.py:37
  21.9 0.6 fusion.28
  22.6 0.7 broadcast_in_dim.146
  23.2 15.0 %all-to-all-start.1 = ((f32[16,2,8,128]{3,2,1,0:T(8,128)}), f32[16,2,8,128]{3,2,1,0:T(8,128)}, u32[]{:S(2)}, u32[]{:S(2)}) async-start(f32[16,2,8,128]{3,2,1,0:T(8,128)} %broadcast_in_dim.146), calls=%async_computation.1 | async-start | bytes 262144 | tf_op jit(solution)/shard_map/all_to_all | solution.py:62
  38.2 9.3 %multiply_convert_fusion = (bf16[1024,512]{1,0:T(8,128)(2,1)S(1)}, bf16[1024,512]{1,0:T(8,128)(2,1)S(1)}) fusion(f32[]{:T(128)} %bitcast.123, f32[512]{0:T(512)S(1)} %bitcast.168, f32[512]{0:T(512)S(1)} %bitcast.158, f32[1024]{0:T(1024)S(1)} %bitcast.151, f32[512]{0:T(512)S(1)} %bitcast.153, f32[1024]{0:T(1024)S(1)} %bitcast.150, f32[512]{0:T(512)S(1)} %bitcast.163, ...), kind=kLoop, calls=%fused_computation | loop fusion | flops 7340032 | bytes 2122244 | tf_op jit(solution)/shard_map/convert_element_type | solution.py:37
  47.6 2.7 %all-to-all-done.1 = f32[16,2,8,128]{3,2,1,0:T(8,128)} async-done(((f32[16,2,8,128]{3,2,1,0:T(8,128)}), f32[16,2,8,128]{3,2,1,0:T(8,128)}, u32[]{:S(2)}, u32[]{:S(2)}) %all-to-all-start.1) | async-done | bytes 131104 | tf_op jit(solution)/shard_map/all_to_all | solution.py:62
  50.2 6.7 %all-to-all-start.2 = ((f32[16,2,8,128]{3,2,1,0:T(8,128)}), f32[16,2,8,128]{3,2,1,0:T(8,128)S(1)}, u32[]{:S(2)}, u32[]{:S(2)}) async-start(f32[16,2,8,128]{3,2,1,0:T(8,128)} %all-to-all-done.1), calls=%async_computation.2 | async-start | bytes 262144 | tf_op jit(solution)/shard_map/all_to_all | solution.py:59
  57.0 5.6 %multiply_convert_fusion.6 = (bf16[512,512]{1,0:T(8,128)(2,1)}, bf16[512,512]{1,0:T(8,128)(2,1)}) fusion(f32[512]{0:T(512)S(1)} %bitcast.177, f32[512]{0:T(512)S(1)} %bitcast.176, f32[]{:T(128)} %bitcast.125, f32[512]{0:T(512)S(1)} %bitcast.169, f32[512]{0:T(512)S(1)} %bitcast.159, f32[512]{0:T(512)S(1)} %bitcast.154, f32[512]{0:T(512)S(1)} %bitcast.164, ...), kind=kLoop, calls=%fused_computation.28 | loop fusion | flops 3670016 | bytes 1065476 | tf_op jit(solution)/shard_map/convert_element_type | solution.py:37
  62.6 1.2 all-to-all-done.2
  63.8 0.7 copy.47
  64.4 7.1 %collective-permute-start = (f32[2,128,128]{2,1,0:T(8,128)}, f32[2,128,128]{2,1,0:T(8,128)}, u32[]{:S(2)}, u32[]{:S(2)}) collective-permute-start(f32[2,128,128]{2,1,0:T(8,128)} %bitcast.119), channel_id=1, source_target_pairs={{0,16},{16,0},{1,17},{17,1},{2,18},{18,2},{3,19},{19,3},{4,20},{20... | collective-permute-start | bytes 393224 | tf_op jit(solution)/shard_map/ppermute | solution.py:79
  71.6 1.0 maximum_maximum_fusion.2
  72.6 0.2 collective-permute-done
  72.9 0.9 broadcast_select_fusion.5
  73.8 0.6 convolution_bitcast_fusion.1
  74.4 0.7 copy.19
  75.1 0.6 fusion.32
  75.7 4.6 %all-to-all-start.3 = ((f32[16,2,8,128]{3,2,1,0:T(8,128)}), f32[16,2,8,128]{3,2,1,0:T(8,128)S(1)}, u32[]{:S(2)}, u32[]{:S(2)}) async-start(f32[16,2,8,128]{3,2,1,0:T(8,128)} %copy.19), calls=%async_computation.3 | async-start | bytes 262144 | tf_op jit(solution)/shard_map/all_to_all | solution.py:59
  80.3 6.4 %multiply_convert_fusion.4 = (bf16[512,512]{1,0:T(8,128)(2,1)}, bf16[512,512]{1,0:T(8,128)(2,1)}) fusion(f32[512]{0:T(512)} %bitcast.179, f32[512]{0:T(512)} %bitcast.178, f32[]{:T(128)} %bitcast.121, f32[512]{0:T(512)} %bitcast.170, f32[512]{0:T(512)} %bitcast.160, f32[512]{0:T(512)} %bitcast.155, f32[512]{0:T(512)} %bitcast.165, f32[512]{0:T(512)} %get-tuple-element.56, ...), kind=kLoop, calls=%fused_computation.23 | loop fusion | flops 3670016 | bytes 1065476 | tf_op jit(solution)/shard_map/convert_element_type | solution.py:37
  86.7 0.4 all-to-all-done.3
  87.1 0.7 dynamic-slice_subtract_fusion
  87.8 0.7 broadcast_in_dim.154
  88.5 6.8 %all-to-all-start.4 = ((f32[16,2,8,128]{3,2,1,0:T(8,128)}), f32[16,2,8,128]{3,2,1,0:T(8,128)S(1)}, u32[]{:S(2)}, u32[]{:S(2)}) async-start(f32[16,2,8,128]{3,2,1,0:T(8,128)} %broadcast_in_dim.154), calls=%async_computation.4 | async-start | bytes 262144 | tf_op jit(solution)/shard_map/all_to_all | solution.py:62
  95.3 0.7 slice_bitcast_fusion.2
  96.0 11.2 %all-to-all-done.4 = f32[16,2,8,128]{3,2,1,0:T(8,128)S(1)} async-done(((f32[16,2,8,128]{3,2,1,0:T(8,128)}), f32[16,2,8,128]{3,2,1,0:T(8,128)S(1)}, u32[]{:S(2)}, u32[]{:S(2)}) %all-to-all-start.4) | async-done | bytes 131104 | tf_op jit(solution)/shard_map/all_to_all | solution.py:62
  107.2 0.6 copy-done.10
  107.9 6.3 %all-to-all-start.5 = ((f32[16,2,8,128]{3,2,1,0:T(8,128)}), f32[16,2,8,128]{3,2,1,0:T(8,128)S(1)}, u32[]{:S(2)}, u32[]{:S(2)}) async-start(f32[16,2,8,128]{3,2,1,0:T(8,128)} %copy-done.10), calls=%async_computation.5 | async-start | bytes 262144 | tf_op jit(solution)/shard_map/all_to_all | solution.py:59
  114.2 6.4 %multiply_convert_fusion.2 = (bf16[512,512]{1,0:T(8,128)(2,1)}, bf16[512,512]{1,0:T(8,128)(2,1)}) fusion(f32[512]{0:T(512)S(1)} %bitcast.175, f32[512]{0:T(512)S(1)} %bitcast.174, f32[]{:T(128)} %bitcast.122, f32[512]{0:T(512)} %bitcast.171, f32[512]{0:T(512)} %bitcast.161, f32[512]{0:T(512)} %bitcast.156, f32[512]{0:T(512)} %bitcast.166, ...), kind=kLoop, calls=%fused_computation.18 | loop fusion | flops 3670016 | bytes 1065476 | tf_op jit(solution)/shard_map/convert_element_type | solution.py:37
  120.6 0.4 all-to-all-done.5
  121.0 7.2 %collective-permute-start.1 = (f32[2,128,128]{2,1,0:T(8,128)S(1)}, f32[2,128,128]{2,1,0:T(8,128)S(1)}, u32[]{:S(2)}, u32[]{:S(2)}) collective-permute-start(f32[2,128,128]{2,1,0:T(8,128)S(1)} %bitcast.148), channel_id=1, source_target_pairs={{0,16},{16,0},{1,17},{17,1},{2,18},{18,2},{3,19},{19,3},{4,20},{20... | collective-permute-start | bytes 393224 | tf_op jit(solution)/shard_map/ppermute | solution.py:79
  128.3 1.1 maximum_maximum_fusion.1
  129.4 0.6 convolution_bitcast_fusion
  130.0 12.3 %all_to_all.50 = f32[16,2,8,128]{3,2,1,0:T(8,128)S(1)} all-to-all(f32[16,2,8,128]{3,2,1,0:T(8,128)S(1)} %copy.21), channel_id=1, replica_groups=mesh['z'=16,'core'=2,'col'=16] {'col'}, dimensions={0} | all-to-all | bytes 262144 | tf_op jit(solution)/shard_map/all_to_all | solution.py:59
  142.4 15.3 %all_to_all.51 = f32[16,2,8,128]{3,2,1,0:T(8,128)S(1)} all-to-all(f32[16,2,8,128]{3,2,1,0:T(8,128)S(1)} %broadcast_in_dim.157), channel_id=1, replica_groups=mesh['z'=16,'core'=2,'col'=16] {'z'}, dimensions={0} | all-to-all | bytes 262144 | tf_op jit(solution)/shard_map/all_to_all | solution.py:62
  157.7 9.6 %all_to_all.52 = f32[16,2,8,128]{3,2,1,0:T(8,128)S(1)} all-to-all(f32[16,2,8,128]{3,2,1,0:T(8,128)S(1)} %all_to_all.51), channel_id=1, replica_groups=mesh['z'=16,'core'=2,'col'=16] {'col'}, dimensions={0} | all-to-all | bytes 262144 | tf_op jit(solution)/shard_map/all_to_all | solution.py:59
  167.3 7.1 %collective-permute-start.2 = (f32[2,128,128]{2,1,0:T(8,128)S(1)}, f32[2,128,128]{2,1,0:T(8,128)S(1)}, u32[]{:S(2)}, u32[]{:S(2)}) collective-permute-start(f32[2,128,128]{2,1,0:T(8,128)S(1)} %bitcast.149), channel_id=1, source_target_pairs={{0,16},{16,0},{1,17},{17,1},{2,18},{18,2},{3,19},{19,3},{4,20},{20... | collective-permute-start | bytes 393224 | tf_op jit(solution)/shard_map/ppermute | solution.py:79
  174.5 1.0 collective-permute-done.2
  175.5 0.9 fusion.24
  176.4 0.4 fusion.22
  176.9 0.3 fusion.21
  177.2 0.3 copy-done.8
  177.5 0.3 fusion.20
  177.8 0.3 fusion.19
  178.1 0.3 fusion.23
  178.4 0.3 fusion.6
  178.7 0.4 fusion.2
  179.2 0.6 copy-done.3
  179.7 0.3 fusion.5
  180.1 0.3 fusion.4
  180.4 0.5 copy-done.5
  180.8 0.3 fusion.3
  181.1 41.6 %all_to_all.53 = f32[16,192,256]{2,1,0:T(8,128)S(1)} all-to-all(f32[16,192,256]{2,1,0:T(8,128)S(1)} %bitcast.142), channel_id=1, replica_groups=mesh['z'=16,'core'=2,'col'=16] {'col'}, dimensions={0} | all-to-all | bytes 6291456 | tf_op jit(solution)/shard_map/all_to_all | solution.py:181
  222.8 0.9 reduce_sum.39
  223.6 1.7 reshape.88
  (79 shorter events, 0.5 us)
Async XLA Ops:
  0.6 2.2 copy-start
  0.6 12.5 %copy-start.11 = (f32[2,3072]{1,0:T(2,128)S(1)}, f32[2,3072]{1,0:T(2,128)}, u32[]{:S(2)}) copy-start(f32[2,3072]{1,0:T(2,128)} %param.20) | copy-start | bytes 73732
  0.7 12.5 %copy-start.12 = (s32[3072]{0:T(1024)S(1)}, s32[3072]{0:T(1024)}, u32[]{:S(2)}) copy-start(s32[3072]{0:T(1024)} %param.21) | copy-start | bytes 36868
  0.7 11.6 %copy-start.16 = (s32[2,256]{1,0:T(2,128)S(1)}, s32[2,256]{1,0:T(2,128)}, u32[]{:S(2)}) copy-start(s32[2,256]{1,0:T(2,128)} %param.19) | copy-start | bytes 6148
  0.7 11.7 %copy-start.14 = (f32[2,2]{1,0:T(2,128)S(1)}, f32[2,2]{1,0:T(2,128)}, u32[]{:S(2)}) copy-start(f32[2,2]{1,0:T(2,128)} %param.22) | copy-start | bytes 52
  0.7 12.3 %copy-start.13 = (f32[2,2,256]{2,1,0:T(2,128)S(1)}, f32[2,2,256]{2,1,0:T(2,128)}, u32[]{:S(2)}) copy-start(f32[2,2,256]{2,1,0:T(2,128)} %param.17) | copy-start | bytes 12292
  0.7 12.3 %copy-start.17 = (f32[2,256]{1,0:T(2,128)S(1)}, f32[2,256]{1,0:T(2,128)}, u32[]{:S(2)}) copy-start(f32[2,256]{1,0:T(2,128)} %param.18) | copy-start | bytes 6148
  0.7 15.0 %copy-start.1 = (f32[2,128,256]{2,1,0:T(8,128)S(1)}, f32[2,128,256]{2,1,0:T(8,128)}, u32[]{:S(2)}) copy-start(f32[2,128,256]{2,1,0:T(8,128)} %param.14) | copy-start | bytes 786436
  2.8 20.4 %slice-start = ((f32[2,3072]{1,0:T(2,128)}), f32[2,1024]{1,0:T(2,128)S(1)}, s32[]{:S(2)}) async-start(f32[2,3072]{1,0:T(2,128)} %param.20), calls=%async_computation.10 | async-start | bytes 16384 | tf_op jit(solution)/shard_map/slice | solution.py:143
  4.1 17.9 %all-to-all-start = ((f32[16,2,8,128]{3,2,1,0:T(8,128)}), f32[16,2,8,128]{3,2,1,0:T(8,128)S(1)}, u32[]{:S(2)}, u32[]{:S(2)}) async-start(f32[16,2,8,128]{3,2,1,0:T(8,128)} %copy.17), calls=%async_computation | async-start | bytes 262144 | tf_op jit(solution)/shard_map/all_to_all | solution.py:59
  12.3 44.6 %copy-start.22 = (pred[512]{0:T(512)(128)(4,1)}, pred[512]{0:T(512)(128)(4,1)S(1)}, u32[]{:S(2)}) copy-start(pred[512]{0:T(512)(128)(4,1)S(1)} %eq.26) | copy-start | bytes 1540
  13.0 43.9 %copy-start.18 = (f32[1,2,2,128]{3,1,2,0:T(2,128)}, f32[1,2,2,128]{3,1,2,0:T(2,128)S(1)}, u32[]{:S(2)}) copy-start(f32[1,2,2,128]{3,1,2,0:T(2,128)S(1)} %copy.27) | copy-start | bytes 6148
  13.0 43.9 %copy-start.19 = (f32[1,2,2,128]{3,1,2,0:T(2,128)}, f32[1,2,2,128]{3,1,2,0:T(2,128)S(1)}, u32[]{:S(2)}) copy-start(f32[1,2,2,128]{3,1,2,0:T(2,128)S(1)} %copy.28) | copy-start | bytes 6148
  13.1 43.9 %copy-start.20 = (f32[1,2,2,128]{3,1,2,0:T(2,128)}, f32[1,2,2,128]{3,1,2,0:T(2,128)S(1)}, u32[]{:S(2)}) copy-start(f32[1,2,2,128]{3,1,2,0:T(2,128)S(1)} %copy.26) | copy-start | bytes 6148
  13.1 43.9 %copy-start.21 = (f32[1,2,2,128]{3,1,2,0:T(2,128)}, f32[1,2,2,128]{3,1,2,0:T(2,128)S(1)}, u32[]{:S(2)}) copy-start(f32[1,2,2,128]{3,1,2,0:T(2,128)S(1)} %copy.29) | copy-start | bytes 6148
  23.2 27.0 %all-to-all-start.1 = ((f32[16,2,8,128]{3,2,1,0:T(8,128)}), f32[16,2,8,128]{3,2,1,0:T(8,128)}, u32[]{:S(2)}, u32[]{:S(2)}) async-start(f32[16,2,8,128]{3,2,1,0:T(8,128)} %broadcast_in_dim.146), calls=%async_computation.1 | async-start | bytes 262144 | tf_op jit(solution)/shard_map/all_to_all | solution.py:62
  50.2 13.5 %all-to-all-start.2 = ((f32[16,2,8,128]{3,2,1,0:T(8,128)}), f32[16,2,8,128]{3,2,1,0:T(8,128)S(1)}, u32[]{:S(2)}, u32[]{:S(2)}) async-start(f32[16,2,8,128]{3,2,1,0:T(8,128)} %all-to-all-done.1), calls=%async_computation.2 | async-start | bytes 262144 | tf_op jit(solution)/shard_map/all_to_all | solution.py:59
  63.8 16.5 %copy-start.15 = (f32[512]{0:T(512)S(1)}, f32[512]{0:T(512)}, u32[]{:S(2)}) copy-start(f32[512]{0:T(512)} %get-tuple-element.55) | copy-start | bytes 6148
  64.4 8.4 %collective-permute-start = (f32[2,128,128]{2,1,0:T(8,128)}, f32[2,128,128]{2,1,0:T(8,128)}, u32[]{:S(2)}, u32[]{:S(2)}) collective-permute-start(f32[2,128,128]{2,1,0:T(8,128)} %bitcast.119), channel_id=1, source_target_pairs={{0,16},{16,0},{1,17},{17,1},{2,18},{18,2},{3,19},{19,3},{4,20},{20... | collective-permute-start | bytes 393224 | tf_op jit(solution)/shard_map/ppermute | solution.py:79
  73.8 21.5 %copy-start.2 = (f32[2,128,256]{2,1,0:T(8,128)S(1)}, f32[2,128,256]{2,1,0:T(8,128)}, u32[]{:S(2)}) copy-start(f32[2,128,256]{2,1,0:T(8,128)} %param.13) | copy-start | bytes 786436
  75.7 11.4 %all-to-all-start.3 = ((f32[16,2,8,128]{3,2,1,0:T(8,128)}), f32[16,2,8,128]{3,2,1,0:T(8,128)S(1)}, u32[]{:S(2)}, u32[]{:S(2)}) async-start(f32[16,2,8,128]{3,2,1,0:T(8,128)} %copy.19), calls=%async_computation.3 | async-start | bytes 262144 | tf_op jit(solution)/shard_map/all_to_all | solution.py:59
  88.5 18.8 %all-to-all-start.4 = ((f32[16,2,8,128]{3,2,1,0:T(8,128)}), f32[16,2,8,128]{3,2,1,0:T(8,128)S(1)}, u32[]{:S(2)}, u32[]{:S(2)}) async-start(f32[16,2,8,128]{3,2,1,0:T(8,128)} %broadcast_in_dim.154), calls=%async_computation.4 | async-start | bytes 262144 | tf_op jit(solution)/shard_map/all_to_all | solution.py:62
  107.2 0.6 copy-start.10
  107.9 13.1 %all-to-all-start.5 = ((f32[16,2,8,128]{3,2,1,0:T(8,128)}), f32[16,2,8,128]{3,2,1,0:T(8,128)S(1)}, u32[]{:S(2)}, u32[]{:S(2)}) async-start(f32[16,2,8,128]{3,2,1,0:T(8,128)} %copy-done.10), calls=%async_computation.5 | async-start | bytes 262144 | tf_op jit(solution)/shard_map/all_to_all | solution.py:59
  121.0 8.3 %collective-permute-start.1 = (f32[2,128,128]{2,1,0:T(8,128)S(1)}, f32[2,128,128]{2,1,0:T(8,128)S(1)}, u32[]{:S(2)}, u32[]{:S(2)}) collective-permute-start(f32[2,128,128]{2,1,0:T(8,128)S(1)} %bitcast.148), channel_id=1, source_target_pairs={{0,16},{16,0},{1,17},{17,1},{2,18},{18,2},{3,19},{19,3},{4,20},{20... | collective-permute-start | bytes 393224 | tf_op jit(solution)/shard_map/ppermute | solution.py:79
  167.3 8.1 %collective-permute-start.2 = (f32[2,128,128]{2,1,0:T(8,128)S(1)}, f32[2,128,128]{2,1,0:T(8,128)S(1)}, u32[]{:S(2)}, u32[]{:S(2)}) collective-permute-start(f32[2,128,128]{2,1,0:T(8,128)S(1)} %bitcast.149), channel_id=1, source_target_pairs={{0,16},{16,0},{1,17},{17,1},{2,18},{18,2},{3,19},{19,3},{4,20},{20... | collective-permute-start | bytes 393224 | tf_op jit(solution)/shard_map/ppermute | solution.py:79
  175.5 1.4 copy-start.7
  176.4 1.1 copy-start.8
  176.4 1.3 copy-start.9
  176.9 1.2 copy-start.6
  178.7 1.0 copy-start.3
  178.7 1.3 copy-start.4
  179.7 1.1 copy-start.5

commit v11 on v9

--- a/solution.py
+++ b/solution.py
@@ -150,11 +150,11 @@
     remainder_cols, tiles_b = col_sum_to_columns(
         complex_product(stacked_matrix(lower_panel), top_solved),
         rhs_bottom,
-        works=(works[2], None, works[3]),
+        works=(works[2], works[3], None),
     )
     bottom_solved, tiles_c = col_sum_to_columns(
         complex_product(stacked_matrix(inv_bottom), remainder_cols),
-        works=(works[4], None, works[5]),
+        works=(works[4], works[5], None),
     )
     tile_chunks = tiles_a + tiles_b + tiles_c
     strengths = jnp.stack([top_solved, bottom_solved])

time: 221 us -> 219 us (level)
  blocking collectives: 58.8 us -> 53.7 us
  waiting for transfers between devices: 33.1 us -> 38.1 us
  starting transfers between devices: 74.2 us -> 71.5 us
    all_to_all x6 -> x5, starting transfers between devices: 33.9 us -> 27.6 us  [col_step(): return lax.all_to_all(value, 'col', 0, 0, tiled=True)]
    all_to_all x6 -> x5, waiting for transfers between devices: 6.42 us -> 10.7 us  [col_step(): return lax.all_to_all(value, 'col', 0, 0, tiled=True)]
    all_to_all x2 -> x3, starting transfers between devices: 19.1 us -> 22.9 us  [z_step(): return lax.all_to_all(value, 'z', 0, 0, tiled=True)]
    all_to_all x1, blocking collectives: 15.7 us -> 12.1 us  [col_step(): return lax.all_to_all(value, 'col', 0, 0, tiled=True)]
    all_to_all x2 -> x3, waiting for transfers between devices: 23.9 us -> 24.7 us  [z_step(): return lax.all_to_all(value, 'z', 0, 0, tiled=True)]
where the time goes in v11:
time: 219 us; the launch traced here: 218 us
  starting transfers between devices  71.5 us (33%)
  blocking collectives  53.7 us (25%)
  other arithmetic  39.7 us (18%)
  waiting for transfers between devices  38.1 us (17%)
  local copies, waits for them, and re-layouts  7.67 us (4%)
  matrix products  5.32 us (2%)
    all_to_all x1, blocking collectives, per_device(): summed = lax.all_to_all(split, 'col', 0, 0, tiled=True).sum(0)  41.6 us
    convert_element_type x6, other arithmetic, green_tile(): (amplitude * jnp.sin(phase_angle)).astype(jnp.bfloat16)  33.3 us
    all_to_all x5, starting transfers between devices, col_step(): return lax.all_to_all(value, 'col', 0, 0, tiled=True)  27.6 us
    all_to_all x3, waiting for transfers between devices, z_step(): return lax.all_to_all(value, 'z', 0, 0, tiled=True)  24.7 us
    all_to_all x3, starting transfers between devices, z_step(): return lax.all_to_all(value, 'z', 0, 0, tiled=True)  22.9 us
    ppermute x3, starting transfers between devices, col_sum_to_columns(): other = lax.ppermute(block, 'core', [(0, 1), (1, 0)])  21 us
    all_to_all x1, blocking collectives, col_step(): return lax.all_to_all(value, 'col', 0, 0, tiled=True)  12.1 us
    all_to_all x5, waiting for transfers between devices, col_step(): return lax.all_to_all(value, 'col', 0, 0, tiled=True)  10.7 us
  transfers between devices with their start and end apart: 11, of which 10 were waited for; matrix products, arithmetic and copies ran while one was open for 17% of the time, Pallas kernels for 0%

profile of v11, /device:TPU:1, one launch (start us, length us, event | category | flops | bytes accessed | tf_op | source)
XLA Modules:
  0.0 217.9 jit_solution(5716059888311953933)
XLA Ops:
  0.6 0.0 copy-start
  0.6 0.0 copy-start.10
  0.7 1.0 fusion.18
  1.7 1.0 slice_bitcast_fusion.4
  2.8 0.6 convolution_bitcast_fusion.2
  3.4 0.7 copy.17
  4.1 7.6 %all-to-all-start = ((f32[16,2,8,128]{3,2,1,0:T(8,128)}), f32[16,2,8,128]{3,2,1,0:T(8,128)S(1)}, u32[]{:S(2)}, u32[]{:S(2)}) async-start(f32[16,2,8,128]{3,2,1,0:T(8,128)} %copy.17), calls=%async_computation | async-start | bytes 262144 | tf_op jit(solution)/shard_map/all_to_all | solution.py:59
  12.3 0.6 fusion.39
  13.1 1.3 broadcast_select_fusion.7
  14.4 1.2 broadcast_select_fusion.6
  15.6 5.5 %multiply_convert_fusion.10 = (bf16[512,512]{1,0:T(8,128)(2,1)S(1)}, bf16[512,512]{1,0:T(8,128)(2,1)}) fusion(f32[]{:T(128)} %bitcast.126, f32[512]{0:T(512)S(1)} %bitcast.177, f32[512]{0:T(512)S(1)} %bitcast.165, f32[512]{0:T(512)S(1)} %bitcast.184, f32[512]{0:T(512)S(1)} %bitcast.159, f32[512]{0:T(512)S(1)} %bitcast.183, f32[512]{0:T(512)S(1)} %bitcast.171, ...), kind=kLoop, calls=%fused_computation.40 | loop fusion | flops 3670016 | bytes 1065476 | tf_op jit(solution)/shard_map/convert_element_type | solution.py:37
  21.1 0.0 all-to-all-done
  21.1 0.7 broadcast_in_dim.152
  21.8 15.0 %all-to-all-start.1 = ((f32[16,2,8,128]{3,2,1,0:T(8,128)}), f32[16,2,8,128]{3,2,1,0:T(8,128)}, u32[]{:S(2)}, u32[]{:S(2)}) async-start(f32[16,2,8,128]{3,2,1,0:T(8,128)} %broadcast_in_dim.152), calls=%async_computation.1 | async-start | bytes 262144 | tf_op jit(solution)/shard_map/all_to_all | solution.py:62
  36.8 11.9 %all-to-all-done.1 = f32[16,2,8,128]{3,2,1,0:T(8,128)} async-done(((f32[16,2,8,128]{3,2,1,0:T(8,128)}), f32[16,2,8,128]{3,2,1,0:T(8,128)}, u32[]{:S(2)}, u32[]{:S(2)}) %all-to-all-start.1) | async-done | bytes 131104 | tf_op jit(solution)/shard_map/all_to_all | solution.py:62
  48.8 6.7 %all-to-all-start.2 = ((f32[16,2,8,128]{3,2,1,0:T(8,128)}), f32[16,2,8,128]{3,2,1,0:T(8,128)S(1)}, u32[]{:S(2)}, u32[]{:S(2)}) async-start(f32[16,2,8,128]{3,2,1,0:T(8,128)} %all-to-all-done.1), calls=%async_computation.2 | async-start | bytes 262144 | tf_op jit(solution)/shard_map/all_to_all | solution.py:59
  55.5 5.5 %multiply_convert_fusion.8 = (bf16[512,512]{1,0:T(8,128)(2,1)S(1)}, bf16[512,512]{1,0:T(8,128)(2,1)}) fusion(f32[512]{0:T(512)S(1)} %bitcast.188, f32[512]{0:T(512)S(1)} %bitcast.187, f32[]{:T(128)} %bitcast.127, f32[512]{0:T(512)S(1)} %bitcast.178, f32[512]{0:T(512)S(1)} %bitcast.166, f32[512]{0:T(512)S(1)} %bitcast.160, f32[512]{0:T(512)S(1)} %bitcast.172, ...), kind=kLoop, calls=%fused_computation.35 | loop fusion | flops 3670016 | bytes 1065476 | tf_op jit(solution)/shard_map/convert_element_type | solution.py:37
  61.0 1.3 all-to-all-done.2
  62.3 7.1 %collective-permute-start = (f32[2,128,128]{2,1,0:T(8,128)S(1)}, f32[2,128,128]{2,1,0:T(8,128)S(1)}, u32[]{:S(2)}, u32[]{:S(2)}) collective-permute-start(f32[2,128,128]{2,1,0:T(8,128)S(1)} %bitcast.156), channel_id=1, source_target_pairs={{0,16},{16,0},{1,17},{17,1},{2,18},{18,2},{3,19},{19,3},{4,20},{20... | collective-permute-start | bytes 393224 | tf_op jit(solution)/shard_map/ppermute | solution.py:78
  69.5 0.9 collective-permute-done
  70.4 0.0 copy-start.2
  70.5 0.6 convolution_bitcast_fusion.1
  71.1 0.7 copy.19
  71.8 4.5 %all-to-all-start.3 = ((f32[16,2,8,128]{3,2,1,0:T(8,128)}), f32[16,2,8,128]{3,2,1,0:T(8,128)S(1)}, u32[]{:S(2)}, u32[]{:S(2)}) async-start(f32[16,2,8,128]{3,2,1,0:T(8,128)} %copy.19), calls=%async_computation.3 | async-start | bytes 262144 | tf_op jit(solution)/shard_map/all_to_all | solution.py:59
  76.3 5.5 %multiply_convert_fusion.6 = (bf16[512,512]{1,0:T(8,128)(2,1)S(1)}, bf16[512,512]{1,0:T(8,128)(2,1)}) fusion(f32[512]{0:T(512)S(1)} %bitcast.190, f32[512]{0:T(512)S(1)} %bitcast.189, f32[]{:T(128)} %bitcast.128, f32[512]{0:T(512)S(1)} %bitcast.179, f32[512]{0:T(512)S(1)} %bitcast.167, f32[512]{0:T(512)S(1)} %bitcast.161, f32[512]{0:T(512)S(1)} %bitcast.173, ...), kind=kLoop, calls=%fused_computation.30 | loop fusion | flops 3670016 | bytes 1065476 | tf_op jit(solution)/shard_map/convert_element_type | solution.py:37
  81.8 1.3 all-to-all-done.3
  83.1 0.7 dynamic-slice_subtract_fusion
  83.8 0.7 broadcast_in_dim.157
  84.5 4.2 %all-to-all-start.4 = ((f32[16,2,8,128]{3,2,1,0:T(8,128)}), f32[16,2,8,128]{3,2,1,0:T(8,128)}, u32[]{:S(2)}, u32[]{:S(2)}) async-start(f32[16,2,8,128]{3,2,1,0:T(8,128)} %broadcast_in_dim.157), calls=%async_computation.4 | async-start | bytes 262144 | tf_op jit(solution)/shard_map/all_to_all | solution.py:62
  88.7 5.5 %multiply_convert_fusion.4 = (bf16[512,512]{1,0:T(8,128)(2,1)S(1)}, bf16[512,512]{1,0:T(8,128)(2,1)}) fusion(f32[512]{0:T(512)S(1)} %bitcast.194, f32[512]{0:T(512)S(1)} %bitcast.193, f32[]{:T(128)} %bitcast.129, f32[512]{0:T(512)S(1)} %bitcast.180, f32[512]{0:T(512)S(1)} %bitcast.168, f32[512]{0:T(512)S(1)} %bitcast.162, f32[512]{0:T(512)S(1)} %bitcast.174, ...), kind=kLoop, calls=%fused_computation.25 | loop fusion | flops 3670016 | bytes 1065476 | tf_op jit(solution)/shard_map/convert_element_type | solution.py:37
  94.2 6.4 %all-to-all-done.4 = f32[16,2,8,128]{3,2,1,0:T(8,128)} async-done(((f32[16,2,8,128]{3,2,1,0:T(8,128)}), f32[16,2,8,128]{3,2,1,0:T(8,128)}, u32[]{:S(2)}, u32[]{:S(2)}) %all-to-all-start.4) | async-done | bytes 131104 | tf_op jit(solution)/shard_map/all_to_all | solution.py:62
  100.7 5.3 %all-to-all-start.5 = ((f32[16,2,8,128]{3,2,1,0:T(8,128)}), f32[16,2,8,128]{3,2,1,0:T(8,128)S(1)}, u32[]{:S(2)}, u32[]{:S(2)}) async-start(f32[16,2,8,128]{3,2,1,0:T(8,128)} %all-to-all-done.4), calls=%async_computation.5 | async-start | bytes 262144 | tf_op jit(solution)/shard_map/all_to_all | solution.py:59
  106.0 6.8 %all-to-all-done.5 = f32[16,2,8,128]{3,2,1,0:T(8,128)S(1)} async-done(((f32[16,2,8,128]{3,2,1,0:T(8,128)}), f32[16,2,8,128]{3,2,1,0:T(8,128)S(1)}, u32[]{:S(2)}, u32[]{:S(2)}) %all-to-all-start.5) | async-done | bytes 131104 | tf_op jit(solution)/shard_map/all_to_all | solution.py:59
  112.8 6.8 %collective-permute-start.1 = (f32[2,128,128]{2,1,0:T(8,128)S(1)}, f32[2,128,128]{2,1,0:T(8,128)S(1)}, u32[]{:S(2)}, u32[]{:S(2)}) collective-permute-start(f32[2,128,128]{2,1,0:T(8,128)S(1)} %bitcast.157), channel_id=1, source_target_pairs={{0,16},{16,0},{1,17},{17,1},{2,18},{18,2},{3,19},{19,3},{4,20},{20... | collective-permute-start | bytes 393224 | tf_op jit(solution)/shard_map/ppermute | solution.py:78
  119.7 0.9 collective-permute-done.1
  120.7 0.6 convolution_bitcast_fusion
  121.2 0.7 copy.21
  121.9 3.5 %all-to-all-start.6 = ((f32[16,2,8,128]{3,2,1,0:T(8,128)}), f32[16,2,8,128]{3,2,1,0:T(8,128)S(1)}, u32[]{:S(2)}, u32[]{:S(2)}) async-start(f32[16,2,8,128]{3,2,1,0:T(8,128)} %copy.21), calls=%async_computation.6 | async-start | bytes 262144 | tf_op jit(solution)/shard_map/all_to_all | solution.py:59
  125.4 5.5 %multiply_convert_fusion.2 = (bf16[512,512]{1,0:T(8,128)(2,1)S(1)}, bf16[512,512]{1,0:T(8,128)(2,1)}) fusion(f32[512]{0:T(512)S(1)} %bitcast.192, f32[512]{0:T(512)S(1)} %bitcast.191, f32[]{:T(128)} %bitcast.130, f32[512]{0:T(512)S(1)} %bitcast.181, f32[512]{0:T(512)S(1)} %bitcast.169, f32[512]{0:T(512)S(1)} %bitcast.163, f32[512]{0:T(512)S(1)} %bitcast.175, ...), kind=kLoop, calls=%fused_computation.20 | loop fusion | flops 3670016 | bytes 1065476 | tf_op jit(solution)/shard_map/convert_element_type | solution.py:37
  131.0 1.3 all-to-all-done.6
  132.3 0.7 broadcast_in_dim.162
  132.9 3.8 %all-to-all-start.7 = ((f32[16,2,8,128]{3,2,1,0:T(8,128)}), f32[16,2,8,128]{3,2,1,0:T(8,128)S(1)}, u32[]{:S(2)}, u32[]{:S(2)}) async-start(f32[16,2,8,128]{3,2,1,0:T(8,128)} %broadcast_in_dim.162), calls=%async_computation.7 | async-start | bytes 262144 | tf_op jit(solution)/shard_map/all_to_all | solution.py:62
  136.7 5.6 %multiply_convert_fusion = (bf16[512,512]{1,0:T(8,128)(2,1)}, bf16[512,512]{1,0:T(8,128)(2,1)}) fusion(f32[512]{0:T(512)S(1)} %bitcast.186, f32[512]{0:T(512)S(1)} %bitcast.185, f32[]{:T(128)} %bitcast.125, f32[512]{0:T(512)S(1)} %bitcast.182, f32[512]{0:T(512)S(1)} %bitcast.170, f32[512]{0:T(512)S(1)} %bitcast.164, f32[512]{0:T(512)S(1)} %bitcast.176, ...), kind=kLoop, calls=%fused_computation.15 | loop fusion | flops 3670016 | bytes 1065476 | tf_op jit(solution)/shard_map/convert_element_type | solution.py:37
  142.4 6.3 %all-to-all-done.7 = f32[16,2,8,128]{3,2,1,0:T(8,128)S(1)} async-done(((f32[16,2,8,128]{3,2,1,0:T(8,128)}), f32[16,2,8,128]{3,2,1,0:T(8,128)S(1)}, u32[]{:S(2)}, u32[]{:S(2)}) %all-to-all-start.7) | async-done | bytes 131104 | tf_op jit(solution)/shard_map/all_to_all | solution.py:62
  148.7 12.1 %all_to_all.50 = f32[16,2,8,128]{3,2,1,0:T(8,128)S(1)} all-to-all(f32[16,2,8,128]{3,2,1,0:T(8,128)S(1)} %all-to-all-done.7), channel_id=1, replica_groups=mesh['z'=16,'core'=2,'col'=16] {'col'}, dimensions={0} | all-to-all | bytes 262144 | tf_op jit(solution)/shard_map/all_to_all | solution.py:59
  160.8 7.1 %collective-permute-start.2 = (f32[2,128,128]{2,1,0:T(8,128)S(1)}, f32[2,128,128]{2,1,0:T(8,128)S(1)}, u32[]{:S(2)}, u32[]{:S(2)}) collective-permute-start(f32[2,128,128]{2,1,0:T(8,128)S(1)} %bitcast.158), channel_id=1, source_target_pairs={{0,16},{16,0},{1,17},{17,1},{2,18},{18,2},{3,19},{19,3},{4,20},{20... | collective-permute-start | bytes 393224 | tf_op jit(solution)/shard_map/ppermute | solution.py:78
  167.9 1.0 collective-permute-done.2
  168.9 0.9 fusion.28
  169.9 0.3 fusion.26
  170.2 0.3 fusion.25
  170.5 0.3 fusion.24
  170.8 0.3 fusion.23
  171.1 0.3 fusion.22
  171.4 0.3 fusion.27
  171.7 0.3 fusion.5
  172.0 0.3 fusion.4
  172.4 0.3 fusion.3
  172.7 0.3 fusion.2
  173.0 0.3 fusion.1
  173.3 0.1 copy-done.3
  173.4 0.3 fusion
  173.7 41.6 %all_to_all.51 = f32[16,192,256]{2,1,0:T(8,128)S(1)} all-to-all(f32[16,192,256]{2,1,0:T(8,128)S(1)} %bitcast.150), channel_id=1, replica_groups=mesh['z'=16,'core'=2,'col'=16] {'col'}, dimensions={0} | all-to-all | bytes 6291456 | tf_op jit(solution)/shard_map/all_to_all | solution.py:177
  215.3 0.9 reduce_sum.39
  216.2 1.7 reshape.92
  (67 shorter events, 0.6 us)
Async XLA Ops:
  0.6 2.2 copy-start
  0.6 12.4 %copy-start.10 = (f32[2,3072]{1,0:T(2,128)S(1)}, f32[2,3072]{1,0:T(2,128)}, u32[]{:S(2)}) copy-start(f32[2,3072]{1,0:T(2,128)} %param.20) | copy-start | bytes 73732
  0.7 12.4 %copy-start.11 = (s32[3072]{0:T(1024)S(1)}, s32[3072]{0:T(1024)}, u32[]{:S(2)}) copy-start(s32[3072]{0:T(1024)} %param.21) | copy-start | bytes 36868
  0.7 11.6 %copy-start.14 = (s32[2,256]{1,0:T(2,128)S(1)}, s32[2,256]{1,0:T(2,128)}, u32[]{:S(2)}) copy-start(s32[2,256]{1,0:T(2,128)} %param.19) | copy-start | bytes 6148
  0.7 11.7 %copy-start.13 = (f32[2,2]{1,0:T(2,128)S(1)}, f32[2,2]{1,0:T(2,128)}, u32[]{:S(2)}) copy-start(f32[2,2]{1,0:T(2,128)} %param.22) | copy-start | bytes 52
  0.7 12.3 %copy-start.12 = (f32[2,2,256]{2,1,0:T(2,128)S(1)}, f32[2,2,256]{2,1,0:T(2,128)}, u32[]{:S(2)}) copy-start(f32[2,2,256]{2,1,0:T(2,128)} %param.17) | copy-start | bytes 12292
  0.7 12.3 %copy-start.15 = (f32[2,256]{1,0:T(2,128)S(1)}, f32[2,256]{1,0:T(2,128)}, u32[]{:S(2)}) copy-start(f32[2,256]{1,0:T(2,128)} %param.18) | copy-start | bytes 6148
  0.7 36.1 %copy-start.1 = (f32[2,128,256]{2,1,0:T(8,128)S(1)}, f32[2,128,256]{2,1,0:T(8,128)}, u32[]{:S(2)}) copy-start(f32[2,128,256]{2,1,0:T(8,128)} %param.14) | copy-start | bytes 786436
  4.1 17.0 %all-to-all-start = ((f32[16,2,8,128]{3,2,1,0:T(8,128)}), f32[16,2,8,128]{3,2,1,0:T(8,128)S(1)}, u32[]{:S(2)}, u32[]{:S(2)}) async-start(f32[16,2,8,128]{3,2,1,0:T(8,128)} %copy.17), calls=%async_computation | async-start | bytes 262144 | tf_op jit(solution)/shard_map/all_to_all | solution.py:59
  21.8 27.0 %all-to-all-start.1 = ((f32[16,2,8,128]{3,2,1,0:T(8,128)}), f32[16,2,8,128]{3,2,1,0:T(8,128)}, u32[]{:S(2)}, u32[]{:S(2)}) async-start(f32[16,2,8,128]{3,2,1,0:T(8,128)} %broadcast_in_dim.152), calls=%async_computation.1 | async-start | bytes 262144 | tf_op jit(solution)/shard_map/all_to_all | solution.py:62
  48.8 13.5 %all-to-all-start.2 = ((f32[16,2,8,128]{3,2,1,0:T(8,128)}), f32[16,2,8,128]{3,2,1,0:T(8,128)S(1)}, u32[]{:S(2)}, u32[]{:S(2)}) async-start(f32[16,2,8,128]{3,2,1,0:T(8,128)} %all-to-all-done.1), calls=%async_computation.2 | async-start | bytes 262144 | tf_op jit(solution)/shard_map/all_to_all | solution.py:59
  62.3 8.1 %collective-permute-start = (f32[2,128,128]{2,1,0:T(8,128)S(1)}, f32[2,128,128]{2,1,0:T(8,128)S(1)}, u32[]{:S(2)}, u32[]{:S(2)}) collective-permute-start(f32[2,128,128]{2,1,0:T(8,128)S(1)} %bitcast.156), channel_id=1, source_target_pairs={{0,16},{16,0},{1,17},{17,1},{2,18},{18,2},{3,19},{19,3},{4,20},{20... | collective-permute-start | bytes 393224 | tf_op jit(solution)/shard_map/ppermute | solution.py:78
  70.4 35.6 %copy-start.2 = (f32[2,128,256]{2,1,0:T(8,128)S(1)}, f32[2,128,256]{2,1,0:T(8,128)}, u32[]{:S(2)}) copy-start(f32[2,128,256]{2,1,0:T(8,128)} %param.13) | copy-start | bytes 786436
  71.8 11.3 %all-to-all-start.3 = ((f32[16,2,8,128]{3,2,1,0:T(8,128)}), f32[16,2,8,128]{3,2,1,0:T(8,128)S(1)}, u32[]{:S(2)}, u32[]{:S(2)}) async-start(f32[16,2,8,128]{3,2,1,0:T(8,128)} %copy.19), calls=%async_computation.3 | async-start | bytes 262144 | tf_op jit(solution)/shard_map/all_to_all | solution.py:59
  84.5 16.2 %all-to-all-start.4 = ((f32[16,2,8,128]{3,2,1,0:T(8,128)}), f32[16,2,8,128]{3,2,1,0:T(8,128)}, u32[]{:S(2)}, u32[]{:S(2)}) async-start(f32[16,2,8,128]{3,2,1,0:T(8,128)} %broadcast_in_dim.157), calls=%async_computation.4 | async-start | bytes 262144 | tf_op jit(solution)/shard_map/all_to_all | solution.py:62
  100.7 12.2 %all-to-all-start.5 = ((f32[16,2,8,128]{3,2,1,0:T(8,128)}), f32[16,2,8,128]{3,2,1,0:T(8,128)S(1)}, u32[]{:S(2)}, u32[]{:S(2)}) async-start(f32[16,2,8,128]{3,2,1,0:T(8,128)} %all-to-all-done.4), calls=%async_computation.5 | async-start | bytes 262144 | tf_op jit(solution)/shard_map/all_to_all | solution.py:59
  112.8 7.8 %collective-permute-start.1 = (f32[2,128,128]{2,1,0:T(8,128)S(1)}, f32[2,128,128]{2,1,0:T(8,128)S(1)}, u32[]{:S(2)}, u32[]{:S(2)}) collective-permute-start(f32[2,128,128]{2,1,0:T(8,128)S(1)} %bitcast.157), channel_id=1, source_target_pairs={{0,16},{16,0},{1,17},{17,1},{2,18},{18,2},{3,19},{19,3},{4,20},{20... | collective-permute-start | bytes 393224 | tf_op jit(solution)/shard_map/ppermute | solution.py:78
  121.9 10.3 %all-to-all-start.6 = ((f32[16,2,8,128]{3,2,1,0:T(8,128)}), f32[16,2,8,128]{3,2,1,0:T(8,128)S(1)}, u32[]{:S(2)}, u32[]{:S(2)}) async-start(f32[16,2,8,128]{3,2,1,0:T(8,128)} %copy.21), calls=%async_computation.6 | async-start | bytes 262144 | tf_op jit(solution)/shard_map/all_to_all | solution.py:59
  132.9 15.8 %all-to-all-start.7 = ((f32[16,2,8,128]{3,2,1,0:T(8,128)}), f32[16,2,8,128]{3,2,1,0:T(8,128)S(1)}, u32[]{:S(2)}, u32[]{:S(2)}) async-start(f32[16,2,8,128]{3,2,1,0:T(8,128)} %broadcast_in_dim.162), calls=%async_computation.7 | async-start | bytes 262144 | tf_op jit(solution)/shard_map/all_to_all | solution.py:62
  148.7 21.2 %copy-start.5 = (bf16[512,512]{1,0:T(8,128)(2,1)S(1)}, bf16[512,512]{1,0:T(8,128)(2,1)}, u32[]{:S(2)}) copy-start(bf16[512,512]{1,0:T(8,128)(2,1)} %get-tuple-element.78) | copy-start | bytes 1572868
  148.7 21.5 %copy-start.6 = (bf16[512,512]{1,0:T(8,128)(2,1)S(1)}, bf16[512,512]{1,0:T(8,128)(2,1)}, u32[]{:S(2)}) copy-start(bf16[512,512]{1,0:T(8,128)(2,1)} %get-tuple-element.80) | copy-start | bytes 1572868
  148.7 21.8 %copy-start.7 = (bf16[512,512]{1,0:T(8,128)(2,1)S(1)}, bf16[512,512]{1,0:T(8,128)(2,1)}, u32[]{:S(2)}) copy-start(bf16[512,512]{1,0:T(8,128)(2,1)} %get-tuple-element.82) | copy-start | bytes 1572868
  160.8 8.0 %collective-permute-start.2 = (f32[2,128,128]{2,1,0:T(8,128)S(1)}, f32[2,128,128]{2,1,0:T(8,128)S(1)}, u32[]{:S(2)}, u32[]{:S(2)}) collective-permute-start(f32[2,128,128]{2,1,0:T(8,128)S(1)} %bitcast.158), channel_id=1, source_target_pairs={{0,16},{16,0},{1,17},{17,1},{2,18},{18,2},{3,19},{19,3},{4,20},{20... | collective-permute-start | bytes 393224 | tf_op jit(solution)/shard_map/ppermute | solution.py:78
  168.9 1.9 copy-start.8
  169.8 1.3 copy-start.9
  169.9 1.6 copy-start.4
  172.4 1.0 copy-start.3

commit v12 on v11

--- a/solution.py
+++ b/solution.py
@@ -69,7 +69,8 @@
         start = lax.axis_index("col") * piece
         summed = lax.dynamic_slice_in_dim(offset, start, piece, 1) - summed
     spread = jnp.broadcast_to(summed[None], (n_z,) + summed.shape)
-    gathered, out = beside(z_step, spread, works[1])
+    middle_work = works[1](outputs) if callable(works[1]) else works[1]
+    gathered, out = beside(z_step, spread, middle_work)
     outputs.append(out)
     last_work = works[2](outputs) if callable(works[2]) else works[2]
     moved, out = beside(col_step, gathered, last_work)
@@ -142,7 +143,7 @@
         return ((field_xy[:, rows], lid_pair[0][rows], lid_pair[1][rows]), tile_chunk)
 
     top_solved, tiles_a = col_sum_to_columns(
-        top_partial, works=(works[0], None, lambda done: chunk_work(1, done[0][1]))
+        top_partial, works=(works[0], lambda done: chunk_work(1, done[0][1]), None)
     )
     lid_pair = tiles_a[0][1]
     tiles_a = [tiles_a[0][0], tiles_a[1]]

time: 219 us -> 218 us (level)
    all_to_all x3, waiting for transfers between devices: 24.7 us -> 19.2 us  [z_step(): return lax.all_to_all(value, 'z', 0, 0, tiled=True)]
    all_to_all x5, waiting for transfers between devices: 10.7 us -> 16.1 us  [col_step(): return lax.all_to_all(value, 'col', 0, 0, tiled=True)]
where the time goes in v12:
time: 218 us; the launch traced here: 217 us
  starting transfers between devices  70.5 us (32%)
  blocking collectives  53.7 us (25%)
  other arithmetic  39.7 us (18%)
  waiting for transfers between devices  38 us (17%)
  local copies, waits for them, and re-layouts  7.67 us (4%)
  matrix products  5.32 us (2%)
    all_to_all x1, blocking collectives, per_device(): summed = lax.all_to_all(split, 'col', 0, 0, tiled=True).sum(0)  41.6 us
    convert_element_type x6, other arithmetic, green_tile(): (amplitude * jnp.sin(phase_angle)).astype(jnp.bfloat16)  33.3 us
    all_to_all x5, starting transfers between devices, col_step(): return lax.all_to_all(value, 'col', 0, 0, tiled=True)  26.8 us
    all_to_all x3, starting transfers between devices, z_step(): return lax.all_to_all(value, 'z', 0, 0, tiled=True)  23.1 us
    ppermute x3, starting transfers between devices, col_sum_to_columns(): other = lax.ppermute(block, 'core', [(0, 1), (1, 0)])  20.6 us
    all_to_all x3, waiting for transfers between devices, z_step(): return lax.all_to_all(value, 'z', 0, 0, tiled=True)  19.2 us
    all_to_all x5, waiting for transfers between devices, col_step(): return lax.all_to_all(value, 'col', 0, 0, tiled=True)  16.1 us
    all_to_all x1, blocking collectives, col_step(): return lax.all_to_all(value, 'col', 0, 0, tiled=True)  12.1 us
  transfers between devices with their start and end apart: 11, of which 10 were waited for; matrix products, arithmetic and copies ran while one was open for 17% of the time, Pallas kernels for 0%

profile of v12, /device:TPU:1, one launch (start us, length us, event | category | flops | bytes accessed | tf_op | source)
XLA Modules:
  0.0 216.9 jit_solution(5496053182541685737)
XLA Ops:
  0.6 0.0 copy-start
  0.7 1.0 fusion.18
  1.7 1.0 slice_bitcast_fusion.4
  2.7 0.0 copy-start.1
  2.8 0.6 convolution_bitcast_fusion.2
  3.4 0.7 copy.17
  4.1 7.6 %all-to-all-start = ((f32[16,2,8,128]{3,2,1,0:T(8,128)}), f32[16,2,8,128]{3,2,1,0:T(8,128)S(1)}, u32[]{:S(2)}, u32[]{:S(2)}) async-start(f32[16,2,8,128]{3,2,1,0:T(8,128)} %copy.17), calls=%async_computation | async-start | bytes 262144 | tf_op jit(solution)/shard_map/all_to_all | solution.py:59
  12.3 0.6 fusion.39
  13.1 1.3 broadcast_select_fusion.7
  14.3 1.2 broadcast_select_fusion.6
  15.5 5.5 %multiply_convert_fusion.10 = (bf16[512,512]{1,0:T(8,128)(2,1)S(1)}, bf16[512,512]{1,0:T(8,128)(2,1)}) fusion(f32[]{:T(128)} %bitcast.126, f32[512]{0:T(512)S(1)} %bitcast.177, f32[512]{0:T(512)S(1)} %bitcast.165, f32[512]{0:T(512)S(1)} %bitcast.184, f32[512]{0:T(512)S(1)} %bitcast.159, f32[512]{0:T(512)S(1)} %bitcast.183, f32[512]{0:T(512)S(1)} %bitcast.171, ...), kind=kLoop, calls=%fused_computation.40 | loop fusion | flops 3670016 | bytes 1065476 | tf_op jit(solution)/shard_map/convert_element_type | solution.py:37
  21.1 0.0 all-to-all-done
  21.1 0.7 broadcast_in_dim.152
  21.8 15.0 %all-to-all-start.1 = ((f32[16,2,8,128]{3,2,1,0:T(8,128)}), f32[16,2,8,128]{3,2,1,0:T(8,128)}, u32[]{:S(2)}, u32[]{:S(2)}) async-start(f32[16,2,8,128]{3,2,1,0:T(8,128)} %broadcast_in_dim.152), calls=%async_computation.1 | async-start | bytes 262144 | tf_op jit(solution)/shard_map/all_to_all | solution.py:62
  36.8 5.5 %multiply_convert_fusion.8 = (bf16[512,512]{1,0:T(8,128)(2,1)S(1)}, bf16[512,512]{1,0:T(8,128)(2,1)}) fusion(f32[512]{0:T(512)S(1)} %bitcast.192, f32[512]{0:T(512)S(1)} %bitcast.191, f32[]{:T(128)} %bitcast.127, f32[512]{0:T(512)S(1)} %bitcast.178, f32[512]{0:T(512)S(1)} %bitcast.166, f32[512]{0:T(512)S(1)} %bitcast.160, f32[512]{0:T(512)S(1)} %bitcast.172, ...), kind=kLoop, calls=%fused_computation.35 | loop fusion | flops 3670016 | bytes 1065476 | tf_op jit(solution)/shard_map/convert_element_type | solution.py:37
  42.3 6.5 %all-to-all-done.1 = f32[16,2,8,128]{3,2,1,0:T(8,128)} async-done(((f32[16,2,8,128]{3,2,1,0:T(8,128)}), f32[16,2,8,128]{3,2,1,0:T(8,128)}, u32[]{:S(2)}, u32[]{:S(2)}) %all-to-all-start.1) | async-done | bytes 131104 | tf_op jit(solution)/shard_map/all_to_all | solution.py:62
  48.8 6.7 %all-to-all-start.2 = ((f32[16,2,8,128]{3,2,1,0:T(8,128)}), f32[16,2,8,128]{3,2,1,0:T(8,128)S(1)}, u32[]{:S(2)}, u32[]{:S(2)}) async-start(f32[16,2,8,128]{3,2,1,0:T(8,128)} %all-to-all-done.1), calls=%async_computation.2 | async-start | bytes 262144 | tf_op jit(solution)/shard_map/all_to_all | solution.py:59
  55.5 6.8 %all-to-all-done.2 = f32[16,2,8,128]{3,2,1,0:T(8,128)S(1)} async-done(((f32[16,2,8,128]{3,2,1,0:T(8,128)}), f32[16,2,8,128]{3,2,1,0:T(8,128)S(1)}, u32[]{:S(2)}, u32[]{:S(2)}) %all-to-all-start.2) | async-done | bytes 131104 | tf_op jit(solution)/shard_map/all_to_all | solution.py:59
  62.3 7.1 %collective-permute-start = (f32[2,128,128]{2,1,0:T(8,128)S(1)}, f32[2,128,128]{2,1,0:T(8,128)S(1)}, u32[]{:S(2)}, u32[]{:S(2)}) collective-permute-start(f32[2,128,128]{2,1,0:T(8,128)S(1)} %bitcast.156), channel_id=1, source_target_pairs={{0,16},{16,0},{1,17},{17,1},{2,18},{18,2},{3,19},{19,3},{4,20},{20... | collective-permute-start | bytes 393224 | tf_op jit(solution)/shard_map/ppermute | solution.py:79
  69.5 0.9 collective-permute-done
  70.4 0.0 copy-start.2
  70.5 0.6 convolution_bitcast_fusion.1
  71.1 0.7 copy.19
  71.8 3.5 %all-to-all-start.3 = ((f32[16,2,8,128]{3,2,1,0:T(8,128)}), f32[16,2,8,128]{3,2,1,0:T(8,128)S(1)}, u32[]{:S(2)}, u32[]{:S(2)}) async-start(f32[16,2,8,128]{3,2,1,0:T(8,128)} %copy.19), calls=%async_computation.3 | async-start | bytes 262144 | tf_op jit(solution)/shard_map/all_to_all | solution.py:59
  75.3 5.5 %multiply_convert_fusion.6 = (bf16[512,512]{1,0:T(8,128)(2,1)S(1)}, bf16[512,512]{1,0:T(8,128)(2,1)}) fusion(f32[512]{0:T(512)S(1)} %bitcast.188, f32[512]{0:T(512)S(1)} %bitcast.187, f32[]{:T(128)} %bitcast.128, f32[512]{0:T(512)S(1)} %bitcast.179, f32[512]{0:T(512)S(1)} %bitcast.167, f32[512]{0:T(512)S(1)} %bitcast.161, f32[512]{0:T(512)S(1)} %bitcast.173, ...), kind=kLoop, calls=%fused_computation.30 | loop fusion | flops 3670016 | bytes 1065476 | tf_op jit(solution)/shard_map/convert_element_type | solution.py:37
  80.8 1.3 all-to-all-done.3
  82.1 0.7 dynamic-slice_subtract_fusion
  82.8 0.7 broadcast_in_dim.157
  83.5 4.2 %all-to-all-start.4 = ((f32[16,2,8,128]{3,2,1,0:T(8,128)}), f32[16,2,8,128]{3,2,1,0:T(8,128)}, u32[]{:S(2)}, u32[]{:S(2)}) async-start(f32[16,2,8,128]{3,2,1,0:T(8,128)} %broadcast_in_dim.157), calls=%async_computation.4 | async-start | bytes 262144 | tf_op jit(solution)/shard_map/all_to_all | solution.py:62
  87.7 5.5 %multiply_convert_fusion.4 = (bf16[512,512]{1,0:T(8,128)(2,1)S(1)}, bf16[512,512]{1,0:T(8,128)(2,1)}) fusion(f32[512]{0:T(512)S(1)} %bitcast.194, f32[512]{0:T(512)S(1)} %bitcast.193, f32[]{:T(128)} %bitcast.129, f32[512]{0:T(512)S(1)} %bitcast.180, f32[512]{0:T(512)S(1)} %bitcast.168, f32[512]{0:T(512)S(1)} %bitcast.162, f32[512]{0:T(512)S(1)} %bitcast.174, ...), kind=kLoop, calls=%fused_computation.25 | loop fusion | flops 3670016 | bytes 1065476 | tf_op jit(solution)/shard_map/convert_element_type | solution.py:37
  93.2 6.4 %all-to-all-done.4 = f32[16,2,8,128]{3,2,1,0:T(8,128)} async-done(((f32[16,2,8,128]{3,2,1,0:T(8,128)}), f32[16,2,8,128]{3,2,1,0:T(8,128)}, u32[]{:S(2)}, u32[]{:S(2)}) %all-to-all-start.4) | async-done | bytes 131104 | tf_op jit(solution)/shard_map/all_to_all | solution.py:62
  99.6 5.5 %all-to-all-start.5 = ((f32[16,2,8,128]{3,2,1,0:T(8,128)}), f32[16,2,8,128]{3,2,1,0:T(8,128)S(1)}, u32[]{:S(2)}, u32[]{:S(2)}) async-start(f32[16,2,8,128]{3,2,1,0:T(8,128)} %all-to-all-done.4), calls=%async_computation.5 | async-start | bytes 262144 | tf_op jit(solution)/shard_map/all_to_all | solution.py:59
  105.1 6.8 %all-to-all-done.5 = f32[16,2,8,128]{3,2,1,0:T(8,128)S(1)} async-done(((f32[16,2,8,128]{3,2,1,0:T(8,128)}), f32[16,2,8,128]{3,2,1,0:T(8,128)S(1)}, u32[]{:S(2)}, u32[]{:S(2)}) %all-to-all-start.5) | async-done | bytes 131104 | tf_op jit(solution)/shard_map/all_to_all | solution.py:59
  112.0 6.4 %collective-permute-start.1 = (f32[2,128,128]{2,1,0:T(8,128)S(1)}, f32[2,128,128]{2,1,0:T(8,128)S(1)}, u32[]{:S(2)}, u32[]{:S(2)}) collective-permute-start(f32[2,128,128]{2,1,0:T(8,128)S(1)} %bitcast.157), channel_id=1, source_target_pairs={{0,16},{16,0},{1,17},{17,1},{2,18},{18,2},{3,19},{19,3},{4,20},{20... | collective-permute-start | bytes 393224 | tf_op jit(solution)/shard_map/ppermute | solution.py:79
  118.5 0.9 collective-permute-done.1
  119.4 0.6 convolution_bitcast_fusion
  120.0 0.7 copy.21
  120.7 3.5 %all-to-all-start.6 = ((f32[16,2,8,128]{3,2,1,0:T(8,128)}), f32[16,2,8,128]{3,2,1,0:T(8,128)S(1)}, u32[]{:S(2)}, u32[]{:S(2)}) async-start(f32[16,2,8,128]{3,2,1,0:T(8,128)} %copy.21), calls=%async_computation.6 | async-start | bytes 262144 | tf_op jit(solution)/shard_map/all_to_all | solution.py:59
  124.2 5.5 %multiply_convert_fusion.2 = (bf16[512,512]{1,0:T(8,128)(2,1)S(1)}, bf16[512,512]{1,0:T(8,128)(2,1)}) fusion(f32[512]{0:T(512)S(1)} %bitcast.190, f32[512]{0:T(512)S(1)} %bitcast.189, f32[]{:T(128)} %bitcast.130, f32[512]{0:T(512)S(1)} %bitcast.181, f32[512]{0:T(512)S(1)} %bitcast.169, f32[512]{0:T(512)S(1)} %bitcast.163, f32[512]{0:T(512)S(1)} %bitcast.175, ...), kind=kLoop, calls=%fused_computation.20 | loop fusion | flops 3670016 | bytes 1065476 | tf_op jit(solution)/shard_map/convert_element_type | solution.py:37
  129.8 1.3 all-to-all-done.6
  131.0 0.7 broadcast_in_dim.162
  131.7 4.0 %all-to-all-start.7 = ((f32[16,2,8,128]{3,2,1,0:T(8,128)}), f32[16,2,8,128]{3,2,1,0:T(8,128)S(1)}, u32[]{:S(2)}, u32[]{:S(2)}) async-start(f32[16,2,8,128]{3,2,1,0:T(8,128)} %broadcast_in_dim.162), calls=%async_computation.7 | async-start | bytes 262144 | tf_op jit(solution)/shard_map/all_to_all | solution.py:62
  135.7 5.6 %multiply_convert_fusion = (bf16[512,512]{1,0:T(8,128)(2,1)}, bf16[512,512]{1,0:T(8,128)(2,1)}) fusion(f32[512]{0:T(512)S(1)} %bitcast.186, f32[512]{0:T(512)S(1)} %bitcast.185, f32[]{:T(128)} %bitcast.125, f32[512]{0:T(512)S(1)} %bitcast.182, f32[512]{0:T(512)S(1)} %bitcast.170, f32[512]{0:T(512)S(1)} %bitcast.164, f32[512]{0:T(512)S(1)} %bitcast.176, ...), kind=kLoop, calls=%fused_computation.15 | loop fusion | flops 3670016 | bytes 1065476 | tf_op jit(solution)/shard_map/convert_element_type | solution.py:37
  141.3 6.3 %all-to-all-done.7 = f32[16,2,8,128]{3,2,1,0:T(8,128)S(1)} async-done(((f32[16,2,8,128]{3,2,1,0:T(8,128)}), f32[16,2,8,128]{3,2,1,0:T(8,128)S(1)}, u32[]{:S(2)}, u32[]{:S(2)}) %all-to-all-start.7) | async-done | bytes 131104 | tf_op jit(solution)/shard_map/all_to_all | solution.py:62
  147.7 12.1 %all_to_all.50 = f32[16,2,8,128]{3,2,1,0:T(8,128)S(1)} all-to-all(f32[16,2,8,128]{3,2,1,0:T(8,128)S(1)} %all-to-all-done.7), channel_id=1, replica_groups=mesh['z'=16,'core'=2,'col'=16] {'col'}, dimensions={0} | all-to-all | bytes 262144 | tf_op jit(solution)/shard_map/all_to_all | solution.py:59
  159.8 7.1 %collective-permute-start.2 = (f32[2,128,128]{2,1,0:T(8,128)S(1)}, f32[2,128,128]{2,1,0:T(8,128)S(1)}, u32[]{:S(2)}, u32[]{:S(2)}) collective-permute-start(f32[2,128,128]{2,1,0:T(8,128)S(1)} %bitcast.158), channel_id=1, source_target_pairs={{0,16},{16,0},{1,17},{17,1},{2,18},{18,2},{3,19},{19,3},{4,20},{20... | collective-permute-start | bytes 393224 | tf_op jit(solution)/shard_map/ppermute | solution.py:79
  166.9 1.0 collective-permute-done.2
  167.9 0.9 fusion.28
  168.8 0.3 fusion.26
  169.1 0.3 fusion.25
  169.5 0.3 fusion.24
  169.8 0.3 fusion.23
  170.1 0.3 fusion.22
  170.4 0.3 fusion.27
  170.7 0.3 fusion.5
  171.0 0.3 fusion.4
  171.3 0.3 fusion.3
  171.6 0.3 fusion.2
  171.9 0.3 fusion.1
  172.2 0.1 copy-done.3
  172.4 0.3 fusion
  172.7 41.6 %all_to_all.51 = f32[16,192,256]{2,1,0:T(8,128)S(1)} all-to-all(f32[16,192,256]{2,1,0:T(8,128)S(1)} %bitcast.150), channel_id=1, replica_groups=mesh['z'=16,'core'=2,'col'=16] {'col'}, dimensions={0} | all-to-all | bytes 6291456 | tf_op jit(solution)/shard_map/all_to_all | solution.py:178
  214.3 0.9 reduce_sum.39
  215.2 1.7 reshape.92
  (67 shorter events, 0.6 us)
Async XLA Ops:
  0.6 2.2 copy-start
  0.6 12.4 %copy-start.10 = (f32[2,3072]{1,0:T(2,128)S(1)}, f32[2,3072]{1,0:T(2,128)}, u32[]{:S(2)}) copy-start(f32[2,3072]{1,0:T(2,128)} %param.20) | copy-start | bytes 73732
  0.7 12.4 %copy-start.11 = (s32[3072]{0:T(1024)S(1)}, s32[3072]{0:T(1024)}, u32[]{:S(2)}) copy-start(s32[3072]{0:T(1024)} %param.21) | copy-start | bytes 36868
  0.7 11.6 %copy-start.14 = (s32[2,256]{1,0:T(2,128)S(1)}, s32[2,256]{1,0:T(2,128)}, u32[]{:S(2)}) copy-start(s32[2,256]{1,0:T(2,128)} %param.19) | copy-start | bytes 6148
  0.7 11.6 %copy-start.13 = (f32[2,2]{1,0:T(2,128)S(1)}, f32[2,2]{1,0:T(2,128)}, u32[]{:S(2)}) copy-start(f32[2,2]{1,0:T(2,128)} %param.22) | copy-start | bytes 52
  0.7 12.3 %copy-start.12 = (f32[2,2,256]{2,1,0:T(2,128)S(1)}, f32[2,2,256]{2,1,0:T(2,128)}, u32[]{:S(2)}) copy-start(f32[2,2,256]{2,1,0:T(2,128)} %param.17) | copy-start | bytes 12292
  0.7 12.3 %copy-start.15 = (f32[2,256]{1,0:T(2,128)S(1)}, f32[2,256]{1,0:T(2,128)}, u32[]{:S(2)}) copy-start(f32[2,256]{1,0:T(2,128)} %param.18) | copy-start | bytes 6148
  2.7 52.8 %copy-start.1 = (f32[2,128,256]{2,1,0:T(8,128)S(1)}, f32[2,128,256]{2,1,0:T(8,128)}, u32[]{:S(2)}) copy-start(f32[2,128,256]{2,1,0:T(8,128)} %param.14) | copy-start | bytes 786436
  4.1 17.0 %all-to-all-start = ((f32[16,2,8,128]{3,2,1,0:T(8,128)}), f32[16,2,8,128]{3,2,1,0:T(8,128)S(1)}, u32[]{:S(2)}, u32[]{:S(2)}) async-start(f32[16,2,8,128]{3,2,1,0:T(8,128)} %copy.17), calls=%async_computation | async-start | bytes 262144 | tf_op jit(solution)/shard_map/all_to_all | solution.py:59
  21.8 27.0 %all-to-all-start.1 = ((f32[16,2,8,128]{3,2,1,0:T(8,128)}), f32[16,2,8,128]{3,2,1,0:T(8,128)}, u32[]{:S(2)}, u32[]{:S(2)}) async-start(f32[16,2,8,128]{3,2,1,0:T(8,128)} %broadcast_in_dim.152), calls=%async_computation.1 | async-start | bytes 262144 | tf_op jit(solution)/shard_map/all_to_all | solution.py:62
  48.8 13.5 %all-to-all-start.2 = ((f32[16,2,8,128]{3,2,1,0:T(8,128)}), f32[16,2,8,128]{3,2,1,0:T(8,128)S(1)}, u32[]{:S(2)}, u32[]{:S(2)}) async-start(f32[16,2,8,128]{3,2,1,0:T(8,128)} %all-to-all-done.1), calls=%async_computation.2 | async-start | bytes 262144 | tf_op jit(solution)/shard_map/all_to_all | solution.py:59
  62.3 8.1 %collective-permute-start = (f32[2,128,128]{2,1,0:T(8,128)S(1)}, f32[2,128,128]{2,1,0:T(8,128)S(1)}, u32[]{:S(2)}, u32[]{:S(2)}) collective-permute-start(f32[2,128,128]{2,1,0:T(8,128)S(1)} %bitcast.156), channel_id=1, source_target_pairs={{0,16},{16,0},{1,17},{17,1},{2,18},{18,2},{3,19},{19,3},{4,20},{20... | collective-permute-start | bytes 393224 | tf_op jit(solution)/shard_map/ppermute | solution.py:79
  70.4 34.7 %copy-start.2 = (f32[2,128,256]{2,1,0:T(8,128)S(1)}, f32[2,128,256]{2,1,0:T(8,128)}, u32[]{:S(2)}) copy-start(f32[2,128,256]{2,1,0:T(8,128)} %param.13) | copy-start | bytes 786436
  71.8 10.3 %all-to-all-start.3 = ((f32[16,2,8,128]{3,2,1,0:T(8,128)}), f32[16,2,8,128]{3,2,1,0:T(8,128)S(1)}, u32[]{:S(2)}, u32[]{:S(2)}) async-start(f32[16,2,8,128]{3,2,1,0:T(8,128)} %copy.19), calls=%async_computation.3 | async-start | bytes 262144 | tf_op jit(solution)/shard_map/all_to_all | solution.py:59
  83.5 16.1 %all-to-all-start.4 = ((f32[16,2,8,128]{3,2,1,0:T(8,128)}), f32[16,2,8,128]{3,2,1,0:T(8,128)}, u32[]{:S(2)}, u32[]{:S(2)}) async-start(f32[16,2,8,128]{3,2,1,0:T(8,128)} %broadcast_in_dim.157), calls=%async_computation.4 | async-start | bytes 262144 | tf_op jit(solution)/shard_map/all_to_all | solution.py:62
  99.6 12.3 %all-to-all-start.5 = ((f32[16,2,8,128]{3,2,1,0:T(8,128)}), f32[16,2,8,128]{3,2,1,0:T(8,128)S(1)}, u32[]{:S(2)}, u32[]{:S(2)}) async-start(f32[16,2,8,128]{3,2,1,0:T(8,128)} %all-to-all-done.4), calls=%async_computation.5 | async-start | bytes 262144 | tf_op jit(solution)/shard_map/all_to_all | solution.py:59
  112.0 7.4 %collective-permute-start.1 = (f32[2,128,128]{2,1,0:T(8,128)S(1)}, f32[2,128,128]{2,1,0:T(8,128)S(1)}, u32[]{:S(2)}, u32[]{:S(2)}) collective-permute-start(f32[2,128,128]{2,1,0:T(8,128)S(1)} %bitcast.157), channel_id=1, source_target_pairs={{0,16},{16,0},{1,17},{17,1},{2,18},{18,2},{3,19},{19,3},{4,20},{20... | collective-permute-start | bytes 393224 | tf_op jit(solution)/shard_map/ppermute | solution.py:79
  120.7 10.3 %all-to-all-start.6 = ((f32[16,2,8,128]{3,2,1,0:T(8,128)}), f32[16,2,8,128]{3,2,1,0:T(8,128)S(1)}, u32[]{:S(2)}, u32[]{:S(2)}) async-start(f32[16,2,8,128]{3,2,1,0:T(8,128)} %copy.21), calls=%async_computation.6 | async-start | bytes 262144 | tf_op jit(solution)/shard_map/all_to_all | solution.py:59
  131.7 16.0 %all-to-all-start.7 = ((f32[16,2,8,128]{3,2,1,0:T(8,128)}), f32[16,2,8,128]{3,2,1,0:T(8,128)S(1)}, u32[]{:S(2)}, u32[]{:S(2)}) async-start(f32[16,2,8,128]{3,2,1,0:T(8,128)} %broadcast_in_dim.162), calls=%async_computation.7 | async-start | bytes 262144 | tf_op jit(solution)/shard_map/all_to_all | solution.py:62
  147.6 21.2 %copy-start.5 = (bf16[512,512]{1,0:T(8,128)(2,1)S(1)}, bf16[512,512]{1,0:T(8,128)(2,1)}, u32[]{:S(2)}) copy-start(bf16[512,512]{1,0:T(8,128)(2,1)} %get-tuple-element.78) | copy-start | bytes 1572868
  147.7 21.5 %copy-start.6 = (bf16[512,512]{1,0:T(8,128)(2,1)S(1)}, bf16[512,512]{1,0:T(8,128)(2,1)}, u32[]{:S(2)}) copy-start(bf16[512,512]{1,0:T(8,128)(2,1)} %get-tuple-element.80) | copy-start | bytes 1572868
  147.7 21.8 %copy-start.7 = (bf16[512,512]{1,0:T(8,128)(2,1)S(1)}, bf16[512,512]{1,0:T(8,128)(2,1)}, u32[]{:S(2)}) copy-start(bf16[512,512]{1,0:T(8,128)(2,1)} %get-tuple-element.82) | copy-start | bytes 1572868
  159.8 8.0 %collective-permute-start.2 = (f32[2,128,128]{2,1,0:T(8,128)S(1)}, f32[2,128,128]{2,1,0:T(8,128)S(1)}, u32[]{:S(2)}, u32[]{:S(2)}) collective-permute-start(f32[2,128,128]{2,1,0:T(8,128)S(1)} %bitcast.158), channel_id=1, source_target_pairs={{0,16},{16,0},{1,17},{17,1},{2,18},{18,2},{3,19},{19,3},{4,20},{20... | collective-permute-start | bytes 393224 | tf_op jit(solution)/shard_map/ppermute | solution.py:79
  167.9 1.9 copy-start.8
  168.7 1.3 copy-start.9
  168.8 1.6 copy-start.4
  171.3 1.0 copy-start.3
